TPU v7x, 512 devices: a whole 4x8x8 slice. The times are simulated.
512 devices in a mesh: lane: 32 (over y_lo, z, core), rec: 16 (over y_hi, x).
Axes of the slice: x: 4, y: 8 (y_hi: 4, y_lo: 2; y = y_hi * 2 + y_lo), z: 8, core: 2. Of those that a mesh axis runs over, the one named last changes fastest.
Arguments:
- waveforms: bfloat16 [512, 65536], P('lane', 'rec'), may hold values from -6 to 6
- patterns: int32 [512, 65536], P('lane', 'rec'), may hold values from 0 to 3
- partners: int32 [512, 8], P('lane'), may hold values from 0 to 511, as said below
- counts: int32 [512], P('lane'), may hold values from 1 to 8, as said below
Outputs:
- responses: float32 [2, 256, 4096], P(None, 'rec', 'lane')
Inputs may be any that keep to these rules, and one draw needn't show every extreme that they name: partners[l, s] is never l; the 8 partners of a lane lie on 8 different indices of lane; of the 128 entries of the lanes of one index of lane, exactly 4 name lanes of each index of lane. `counts`: uneven over lanes and over indices of lane.
All inputs are finite; a program needn't handle non-finite values.
Results may differ from a plain program's by a relative error of at most 0.0003.
Values may be sent and summed in bfloat16 or wider, within the bound.
No kernel may reach another device: no remote copies, remote signals or barrier semaphores. Data moves between devices by JAX's collectives and lax.ppermute only.
A program may use at most 64 MiB of HBM per device.

v0:
```python
import jax
import jax.numpy as jnp
from jax import lax
from jax.experimental import pallas as pl
from jax.experimental.pallas import tpu as pltpu
from jax.sharding import PartitionSpec as P

LAGS = 256
PHASE = 16
WIDE = 384


def passed_along(block, axis, distance):
    devices = range(lax.axis_size(axis))
    route = [(i - distance, i) for i in devices if i - distance in devices]
    return lax.ppermute(block, axis, route)


def request_layout(targets, lane_dev, capacity):
    target_dev = targets // lane_dev
    serial = jnp.arange(targets.shape[0], dtype=jnp.int32)
    earlier = (target_dev[None, :] == target_dev[:, None]) & (serial[None, :] < serial[:, None])
    ranks = jnp.sum(earlier.astype(jnp.int32), axis=1)
    slot_of = target_dev * capacity + ranks
    order = jnp.sum(jnp.where(slot_of[None, :] == serial[:, None], serial[None, :], 0), axis=1)
    return (slot_of, order)


def deinterleave(rows):
    lead = rows.shape[:-1]
    n = rows.shape[-1]
    split = rows.reshape(lead + (n // PHASE, PHASE))
    return jnp.swapaxes(split, -1, -2)


def pick_rows(onehot, table):
    flat = table.reshape(table.shape[0], -1)
    out = jnp.dot(onehot, flat, preferred_element_type=jnp.float32).astype(table.dtype)
    return out.reshape((onehot.shape[0],) + table.shape[1:])


def lane_kernel(rows_ref, phased_ref, out_ref, win_ref, cross_ref):
    slots = rows_ref.shape[0]
    blocks = rows_ref.shape[3]
    for d in range(2):
        phased = phased_ref[0, d].astype(jnp.float32)
        for q in range(WIDE // PHASE):
            shifted = phased if q == 0 else pltpu.roll(phased, WIDE - q, 1)
            win_ref[q * PHASE : (q + 1) * PHASE, :] = shifted[:, :blocks].astype(jnp.bfloat16)
        lhs = rows_ref[:, d].reshape(slots * PHASE, blocks)
        cross = lax.dot_general(
            lhs, win_ref[...], (((1,), (1,)), ((), ())), preferred_element_type=jnp.float32
        )
        for c in range(WIDE // 128):
            cross_ref[c] = cross[:, c * 128 : (c + 1) * 128]
        total = None
        for i in range(PHASE):
            picked = jnp.concatenate(
                [cross_ref[c, pl.ds(i, slots, stride=PHASE), :] for c in range(WIDE // 128)], axis=1
            )
            shifted = picked if i == 0 else pltpu.roll(picked, WIDE - i, 1)
            total = shifted[:, :LAGS] if total is None else total + shifted[:, :LAGS]
        out_ref[0, d] = total


def correlate(rows, phased):
    lanes = phased.shape[0]
    slots = rows.shape[0] // lanes
    blocks = rows.shape[3]
    return pl.pallas_call(
        lane_kernel,
        grid=(lanes,),
        in_specs=[
            pl.BlockSpec((slots, 2, PHASE, blocks), lambda l: (l, 0, 0, 0)),
            pl.BlockSpec((1, 2, PHASE, WIDE), lambda l: (l, 0, 0, 0)),
        ],
        out_specs=pl.BlockSpec((1, 2, slots, LAGS), lambda l: (l, 0, 0, 0)),
        out_shape=jax.ShapeDtypeStruct((lanes, 2, slots, LAGS), jnp.float32),
        scratch_shapes=[
            pltpu.VMEM((WIDE, blocks), jnp.bfloat16),
            pltpu.VMEM((WIDE // 128, slots * PHASE, 128), jnp.float32),
        ],
    )(rows, phased)


def per_device(waveforms, patterns, partners, counts):
    lane_dev, time_dev = waveforms.shape
    slots = partners.shape[1]
    lane_count = lax.axis_size("lane")
    rec_count = lax.axis_size("rec")
    capacity = lane_dev * slots // lane_count
    total_time = time_dev * rec_count
    blocks = time_dev // PHASE
    levels = (2 * patterns - 3).astype(jnp.bfloat16)
    prev_rim = passed_along(levels[:, time_dev - LAGS :], "rec", 1)
    next_rim = passed_along(waveforms[:, :LAGS], "rec", -1)
    span = (blocks + WIDE // PHASE) * PHASE
    wav_ext = jnp.concatenate(
        [waveforms, next_rim, jnp.zeros((lane_dev, span - time_dev - LAGS), jnp.bfloat16)], axis=1
    )
    lev_ext = jnp.concatenate(
        [prev_rim[:, 1:], levels, jnp.zeros((lane_dev, span - time_dev - LAGS + 1), jnp.bfloat16)],
        axis=1,
    )
    phased = deinterleave(jnp.stack([wav_ext, lev_ext], axis=1))
    phased = jnp.pad(phased, ((0, 0), (0, 0), (0, 0), (0, WIDE - phased.shape[3])))

    targets = partners.reshape(-1)
    slot_of, order = request_layout(targets, lane_dev, capacity)
    local_index = targets % lane_dev
    send_index = local_index[order].reshape(lane_count, capacity)
    index_in = lax.all_to_all(send_index, "lane", split_axis=0, concat_axis=0, tiled=True)
    both = deinterleave(jnp.stack([waveforms, levels], axis=1))
    pick = (index_in.reshape(-1)[:, None] == jnp.arange(lane_dev)[None, :]).astype(jnp.bfloat16)
    reply = pick_rows(pick, both).reshape((lane_count, capacity) + both.shape[1:])
    got = lax.all_to_all(reply, "lane", split_axis=0, concat_axis=0, tiled=True)
    got = got.reshape((lane_count * capacity,) + both.shape[1:])
    place = (slot_of[:, None] == jnp.arange(lane_count * capacity)[None, :]).astype(jnp.bfloat16)
    mine = pick_rows(place, got)
    mine = jnp.flip(mine, axis=1)

    out = correlate(mine, phased)
    forward = out[:, 0].reshape(lane_dev * slots, LAGS)
    reverse = out[:, 1, :, ::-1].reshape(lane_dev * slots, LAGS)
    terms = jnp.stack([forward, reverse])
    lag_dev = LAGS // rec_count
    terms = terms.reshape(2, lane_dev * slots, rec_count, lag_dev).transpose(2, 0, 3, 1)
    parts = lax.all_to_all(terms, "rec", split_axis=0, concat_axis=0, tiled=True)
    summed = jnp.sum(parts.reshape(rec_count, 2, lag_dev, lane_dev * slots), axis=0)
    valid = (
        (jnp.arange(slots, dtype=jnp.int32)[None, :] < counts[:, None])
        .astype(jnp.float32)
        .reshape(-1)
    )
    scale = (5.0 * total_time) ** (-0.5)
    return summed * valid * scale


def solution(mesh):
    in_specs = (P("lane", "rec"), P("lane", "rec"), P("lane", None), P("lane"))
    out_specs = P(None, "rec", "lane")
    return jax.shard_map(
        per_device, mesh=mesh, in_specs=in_specs, out_specs=out_specs, check_vma=False
    )
```

profile of v0, /device:TPU:1, one launch (start us, length us, event | category | flops | bytes accessed | tf_op | source)
XLA Modules:
  0.0 130.0 jit_solution(146473403283027500)
XLA Ops:
  0.0 0.0 copy-start
  0.0 0.8 copy.30
  0.8 0.1 reshape.143
  0.9 0.2 convert_reduce_fusion
  1.1 0.1 select_reduce_fusion
  1.2 1.2 gather_fusion
  2.5 0.7 all_to_all.12
  3.2 13.0 %all-to-all-start = ((s32[32,1,4]{2,1,0:T(1,128)}), s32[32,1,4]{2,1,0:T(1,128)S(1)}, u32[]{:S(2)}, u32[]{:S(2)}) async-start(s32[32,1,4]{2,1,0:T(1,128)} %bitcast.2), calls=%async_computation | async-start | bytes 32768 | tf_op jit(solution)/shard_map/all_to_all | solution.py:112
  16.2 1.0 add_convert_fusion
  17.1 0.8 stack.26
  18.0 0.3 copy.33
  18.3 0.0 copy-done
  18.3 0.8 stack.25
  19.1 0.3 copy.32
  19.5 0.2 copy.40
  19.7 4.3 %all-to-all-done = s32[32,1,4]{2,1,0:T(1,128)S(1)} async-done(((s32[32,1,4]{2,1,0:T(1,128)}), s32[32,1,4]{2,1,0:T(1,128)S(1)}, u32[]{:S(2)}, u32[]{:S(2)}) %all-to-all-start) | async-done | bytes 544 | tf_op jit(solution)/shard_map/all_to_all | solution.py:112
  23.9 0.5 broadcast.159
  24.4 0.7 reduce.3
  25.1 0.1 eq.59
  25.2 0.8 convolution_convert_fusion
  26.0 2.0 %copy.41 = bf16[16,8,32,256]{3,2,1,0:T(8,128)(2,1)} copy(bf16[16,8,32,256]{3,1,2,0:T(8,128)(2,1)S(1)} %bitcast.27) | data formatting | bytes 4194304
  28.0 4.4 %all-to-all-start.1 = ((bf16[32,4,2,16,256]{4,3,2,1,0:T(8,128)(2,1)}), bf16[32,4,2,16,256]{4,3,2,1,0:T(8,128)(2,1)S(1)}, u32[]{:S(2)}, u32[]{:S(2)}) async-start(bf16[32,4,2,16,256]{4,3,2,1,0:T(8,128)(2,1)} %bitcast.28), calls=%async_computation.1 | async-start | bytes 4194304 | tf_op jit(solution)/shard_map/all_to_all | solution.py:116
  32.4 3.1 %collective-permute-start.1 = (bf16[16,256]{1,0:T(8,128)(2,1)S(1)}, bf16[16,256]{1,0:T(8,128)(2,1)S(1)}, u32[]{:S(2)}, u32[]{:S(2)}) collective-permute-start(bf16[16,256]{1,0:T(8,128)(2,1)S(1)} %slice.22), channel_id=1, source_target_pairs={{0,1},{1,2},{2,3},{3,4},{4,5},{5,6},{6,7},{7,8},{8,9},{9,10},{10,1... | collective-permute-start | bytes 24584 | tf_op jit(solution)/shard_map/ppermute | solution.py:16
  35.5 1.3 collective-permute-start
  36.8 0.0 collective-permute-done.1
  36.9 0.1 slice.23
  36.9 0.2 concatenate.10
  37.1 0.8 stack.29
  37.9 1.2 copy.35
  39.1 1.1 collective-permute-done
  40.2 0.9 maximum_maximum_fusion
  41.1 0.8 stack.28
  42.0 1.1 copy.34
  43.1 1.1 maximum_bitcast_fusion.1
  44.2 0.8 pad.4.phased_ref
  45.0 39.6 %all-to-all-done.1 = bf16[32,4,2,16,256]{4,3,2,1,0:T(8,128)(2,1)S(1)} async-done(((bf16[32,4,2,16,256]{4,3,2,1,0:T(8,128)(2,1)}), bf16[32,4,2,16,256]{4,3,2,1,0:T(8,128)(2,1)S(1)}, u32[]{:S(2)}, u32[]{:S(2)}) %all-to-all-start.1) | async-done | bytes 2097184 | tf_op jit(solution)/shard_map/all_to_all | solution.py:116
  84.6 2.4 %reshape_reshape.7 = bf16[128,8192]{1,0:T(8,128)(2,1)} reshape(bf16[32,4,2,16,256]{4,3,2,1,0:T(8,128)(2,1)S(1)} %all-to-all-done.1) | data formatting | bytes 4194304 | tf_op jit(solution)/shard_map/reshape;reshape | solution.py:37
  86.9 2.3 %convolution_convert_fusion.1 = bf16[128,8192]{1,0:T(8,128)(2,1)S(1)} fusion(bf16[128,8192]{1,0:T(8,128)(2,1)} %reshape_reshape.7, s32[128]{0:T(128)S(1)} %multiply_add_fusion), kind=kOutput, calls=%fused_computation.2 | convolution fusion | flops 269500416 | bytes 4194816 | tf_op jit(solution)/shard_map/dot_general | solution.py:38
  89.3 0.6 copy.42
  89.9 1.5 %rev.7.rows_ref = bf16[128,2,16,256]{3,2,1,0:T(8,128)(2,1)} reverse(bf16[128,2,16,256]{3,2,1,0:T(8,128)(2,1)S(1)} %bitcast.30), dimensions={1} | reverse | bytes 4194304 | tf_op jit(solution)/shard_map/jit(_flip)/rev | solution.py:120
  91.4 12.7 %shard_map.46 = f32[16,2,8,256]{3,2,1,0:T(8,128)} custom-call(bf16[128,2,16,256]{3,2,1,0:T(8,128)(2,1)} %rev.7.rows_ref, bf16[16,2,16,384]{3,2,1,0:T(8,128)(2,1)} %pad.4.phased_ref), custom_call_target="tpu_custom_call" | custom-call | tf_op jit(solution)/shard_map/pallas_call | solution.py:70
  104.1 1.0 fusion.5
  105.1 0.2 rev.8
  105.2 0.3 stack.32
  105.6 1.3 %stack.31 = f32[1,128,16,16]{3,2,1,0:T(8,128)} reshape(f32[16,1,8,256]{3,2,1,0:T(8,128)S(1)} %get-tuple-element.5) | data formatting | bytes 262144 | tf_op jit(solution)/shard_map/stack | solution.py:125
  106.9 1.4 %maximum_bitcast_fusion = f32[16,2,16,128]{2,0,3,1:T(8,128)S(1)} fusion(f32[1,128,16,16]{3,2,1,0:T(8,128)S(1)} %stack.32, f32[1,128,16,16]{3,2,1,0:T(8,128)} %stack.31), kind=kLoop, calls=%fused_computation.3 | loop fusion | flops 65536 | bytes 524288 | tf_op jit(solution)/shard_map/transpose | solution.py:127
  108.3 0.0 copy-start.1
  108.3 1.7 %copy.36 = f32[16,2,16,128]{3,2,1,0:T(8,128)} copy(f32[16,2,16,128]{2,0,3,1:T(8,128)S(1)} %maximum_bitcast_fusion) | data formatting | bytes 524288 | tf_op jit(solution)/shard_map/transpose | solution.py:127
  110.0 8.4 %all-to-all-start.2 = ((f32[16,2,16,128]{3,2,1,0:T(8,128)}), f32[16,2,16,128]{3,2,1,0:T(8,128)S(1)}, u32[]{:S(2)}, u32[]{:S(2)}) async-start(f32[16,2,16,128]{3,2,1,0:T(8,128)} %copy.36), calls=%async_computation.2 | async-start | bytes 524288 | tf_op jit(solution)/shard_map/all_to_all | solution.py:128
  118.4 0.0 copy-done.1
  118.4 0.1 fusion.3
  118.5 0.1 reshape.146
  118.6 10.8 %all-to-all-done.2 = f32[16,2,16,128]{3,2,1,0:T(8,128)S(1)} async-done(((f32[16,2,16,128]{3,2,1,0:T(8,128)}), f32[16,2,16,128]{3,2,1,0:T(8,128)S(1)}, u32[]{:S(2)}, u32[]{:S(2)}) %all-to-all-start.2) | async-done | bytes 262176 | tf_op jit(solution)/shard_map/all_to_all | solution.py:128
  129.4 0.6 multiply_multiply_fusion
  (11 shorter events, 0.1 us)
Async XLA Ops:
  0.0 18.3 %copy-start = (bf16[16,4096]{1,0:T(8,128)(2,1)S(1)}, bf16[16,4096]{1,0:T(8,128)(2,1)}, u32[]{:S(2)}) copy-start(bf16[16,4096]{1,0:T(8,128)(2,1)} %param.4) | copy-start | bytes 393220
  3.2 20.8 %all-to-all-start = ((s32[32,1,4]{2,1,0:T(1,128)}), s32[32,1,4]{2,1,0:T(1,128)S(1)}, u32[]{:S(2)}, u32[]{:S(2)}) async-start(s32[32,1,4]{2,1,0:T(1,128)} %bitcast.2), calls=%async_computation | async-start | bytes 32768 | tf_op jit(solution)/shard_map/all_to_all | solution.py:112
  28.0 56.6 %all-to-all-start.1 = ((bf16[32,4,2,16,256]{4,3,2,1,0:T(8,128)(2,1)}), bf16[32,4,2,16,256]{4,3,2,1,0:T(8,128)(2,1)S(1)}, u32[]{:S(2)}, u32[]{:S(2)}) async-start(bf16[32,4,2,16,256]{4,3,2,1,0:T(8,128)(2,1)} %bitcast.28), calls=%async_computation.1 | async-start | bytes 4194304 | tf_op jit(solution)/shard_map/all_to_all | solution.py:116
  32.4 4.5 %collective-permute-start.1 = (bf16[16,256]{1,0:T(8,128)(2,1)S(1)}, bf16[16,256]{1,0:T(8,128)(2,1)S(1)}, u32[]{:S(2)}, u32[]{:S(2)}) collective-permute-start(bf16[16,256]{1,0:T(8,128)(2,1)S(1)} %slice.22), channel_id=1, source_target_pairs={{0,1},{1,2},{2,3},{3,4},{4,5},{5,6},{6,7},{7,8},{8,9},{9,10},{10,1... | collective-permute-start | bytes 24584 | tf_op jit(solution)/shard_map/ppermute | solution.py:16
  35.5 4.7 %collective-permute-start = (bf16[16,256]{1,0:T(8,128)(2,1)S(1)}, bf16[16,256]{1,0:T(8,128)(2,1)S(1)}, u32[]{:S(2)}, u32[]{:S(2)}) collective-permute-start(bf16[16,256]{1,0:T(8,128)(2,1)S(1)} %slice.15), channel_id=1, source_target_pairs={{1,0},{2,1},{3,2},{4,3},{5,4},{6,5},{7,6},{8,7},{9,8},{10,9},{11,1... | collective-permute-start | bytes 24584 | tf_op jit(solution)/shard_map/ppermute | solution.py:16
  108.3 10.1 %copy-start.1 = (s32[16]{0:T(128)S(1)}, s32[16]{0:T(128)}, u32[]{:S(2)}) copy-start(s32[16]{0:T(128)} %param.7) | copy-start | bytes 196
  110.0 19.4 %all-to-all-start.2 = ((f32[16,2,16,128]{3,2,1,0:T(8,128)}), f32[16,2,16,128]{3,2,1,0:T(8,128)S(1)}, u32[]{:S(2)}, u32[]{:S(2)}) async-start(f32[16,2,16,128]{3,2,1,0:T(8,128)} %copy.36), calls=%async_computation.2 | async-start | bytes 524288 | tf_op jit(solution)/shard_map/all_to_all | solution.py:128
where the time goes:
time: 132 us; the launch traced here: 130 us
  waiting for transfers between devices  55.8 us (42%)
  starting transfers between devices  30.2 us (23%)
  local copies, waits for them, and re-layouts  21.9 us (17%)
  Pallas kernels  12.7 us (10%)
  other arithmetic  6.1 us (5%)
  matrix products  3.09 us (2%)
    all_to_all x1, waiting for transfers between devices, per_device(): got = lax.all_to_all(reply, 'lane', split_axis=0, concat_axis=0, tiled=True)  39.6 us
    all_to_all x1, starting transfers between devices, per_device(): lax.all_to_all(send_index, 'lane', split_axis=0, concat_axis=0, tiled=True)  13 us
    pallas_call x1, Pallas kernels, correlate(): pl.pallas_call(lane_kernel, grid=(lanes,), in_specs=[pl.BlockSpec((slots,...  12.7 us
    all_to_all x1, waiting for transfers between devices, per_device(): lax.all_to_all(terms, 'rec', split_axis=0, concat_axis=0, tiled=True)  10.8 us
    all_to_all x1, starting transfers between devices, per_device(): lax.all_to_all(terms, 'rec', split_axis=0, concat_axis=0, tiled=True)  8.4 us
    all_to_all x1, starting transfers between devices, per_device(): got = lax.all_to_all(reply, 'lane', split_axis=0, concat_axis=0, tiled=True)  4.41 us
    ppermute x2, starting transfers between devices, passed_along(): return lax.ppermute(block, axis, route)  4.4 us
    all_to_all x1, waiting for transfers between devices, per_device(): lax.all_to_all(send_index, 'lane', split_axis=0, concat_axis=0, tiled=True)  4.28 us
  transfers between devices with their start and end apart: 5, of which 4 were waited for; matrix products, arithmetic and copies ran while one was open for 8% of the time, Pallas kernels for 0%

commit v1 on v0

--- a/solution.py
+++ b/solution.py
@@ -39,15 +39,25 @@
     return out.reshape((onehot.shape[0],) + table.shape[1:])
 
 
-def lane_kernel(rows_ref, phased_ref, out_ref, win_ref, cross_ref):
-    slots = rows_ref.shape[0]
-    blocks = rows_ref.shape[3]
+def lane_kernel(slot_ref, *refs):
+    del slot_ref
+    acc_ref = refs[-1]
+    cross_ref = refs[-2]
+    win_ref = refs[-3]
+    out_ref = refs[-4]
+    phased_ref = refs[-5]
+    row_refs = refs[:-5]
+    slots = len(row_refs)
+    blocks = win_ref.shape[1]
+    top = WIDE // PHASE - 1
+    lane = pl.program_id(0)
     for d in range(2):
         phased = phased_ref[0, d].astype(jnp.float32)
         for q in range(WIDE // PHASE):
-            shifted = phased if q == 0 else pltpu.roll(phased, WIDE - q, 1)
+            step = q if d == 0 else top - q
+            shifted = phased if step == 0 else pltpu.roll(phased, WIDE - step, 1)
             win_ref[q * PHASE : (q + 1) * PHASE, :] = shifted[:, :blocks].astype(jnp.bfloat16)
-        lhs = rows_ref[:, d].reshape(slots * PHASE, blocks)
+        lhs = jnp.concatenate([ref[0, 1 - d] for ref in row_refs], axis=0)
         cross = lax.dot_general(
             lhs, win_ref[...], (((1,), (1,)), ((), ())), preferred_element_type=jnp.float32
         )
@@ -58,29 +68,45 @@
             picked = jnp.concatenate(
                 [cross_ref[c, pl.ds(i, slots, stride=PHASE), :] for c in range(WIDE // 128)], axis=1
             )
-            shifted = picked if i == 0 else pltpu.roll(picked, WIDE - i, 1)
+            step = i if d == 0 else (WIDE - LAGS) - i
+            shifted = picked if step == 0 else pltpu.roll(picked, WIDE - step, 1)
             total = shifted[:, :LAGS] if total is None else total + shifted[:, :LAGS]
-        out_ref[0, d] = total
+        acc_ref[d, pl.ds(pl.multiple_of(lane * slots, slots), slots), :] = total
+
+    @pl.when(lane == pl.num_programs(0) - 1)
+    def _():
+        for d in range(2):
+            flipped = acc_ref[d].T
+            out_ref[:, d] = flipped.reshape(out_ref.shape[0], out_ref.shape[2], out_ref.shape[3])
 
 
-def correlate(rows, phased):
+def correlate(got, slot_of, phased, rec_count):
     lanes = phased.shape[0]
-    slots = rows.shape[0] // lanes
-    blocks = rows.shape[3]
-    return pl.pallas_call(
-        lane_kernel,
+    pairs = slot_of.shape[0]
+    slots = pairs // lanes
+    blocks = got.shape[3]
+    lag_dev = LAGS // rec_count
+
+    def row_spec(s):
+        return pl.BlockSpec((1, 2, PHASE, blocks), lambda l, slot: (slot[l * slots + s], 0, 0, 0))
+
+    grid_spec = pltpu.PrefetchScalarGridSpec(
+        num_scalar_prefetch=1,
         grid=(lanes,),
-        in_specs=[
-            pl.BlockSpec((slots, 2, PHASE, blocks), lambda l: (l, 0, 0, 0)),
-            pl.BlockSpec((1, 2, PHASE, WIDE), lambda l: (l, 0, 0, 0)),
-        ],
-        out_specs=pl.BlockSpec((1, 2, slots, LAGS), lambda l: (l, 0, 0, 0)),
-        out_shape=jax.ShapeDtypeStruct((lanes, 2, slots, LAGS), jnp.float32),
+        in_specs=[row_spec(s) for s in range(slots)]
+        + [pl.BlockSpec((1, 2, PHASE, WIDE), lambda l, slot: (l, 0, 0, 0))],
+        out_specs=pl.BlockSpec((rec_count, 2, lag_dev, pairs), lambda l, slot: (0, 0, 0, 0)),
         scratch_shapes=[
             pltpu.VMEM((WIDE, blocks), jnp.bfloat16),
             pltpu.VMEM((WIDE // 128, slots * PHASE, 128), jnp.float32),
+            pltpu.VMEM((2, pairs, LAGS), jnp.float32),
         ],
-    )(rows, phased)
+    )
+    return pl.pallas_call(
+        lane_kernel,
+        grid_spec=grid_spec,
+        out_shape=jax.ShapeDtypeStruct((rec_count, 2, lag_dev, pairs), jnp.float32),
+    )(slot_of, *([got] * slots), phased)
 
 
 def per_device(waveforms, patterns, partners, counts):
@@ -103,6 +129,7 @@
         axis=1,
     )
     phased = deinterleave(jnp.stack([wav_ext, lev_ext], axis=1))
+    phased = jnp.concatenate([phased[:, :1], phased[:, 1:, ::-1]], axis=1)
     phased = jnp.pad(phased, ((0, 0), (0, 0), (0, 0), (0, WIDE - phased.shape[3])))
 
     targets = partners.reshape(-1)
@@ -115,16 +142,8 @@
     reply = pick_rows(pick, both).reshape((lane_count, capacity) + both.shape[1:])
     got = lax.all_to_all(reply, "lane", split_axis=0, concat_axis=0, tiled=True)
     got = got.reshape((lane_count * capacity,) + both.shape[1:])
-    place = (slot_of[:, None] == jnp.arange(lane_count * capacity)[None, :]).astype(jnp.bfloat16)
-    mine = pick_rows(place, got)
-    mine = jnp.flip(mine, axis=1)
-
-    out = correlate(mine, phased)
-    forward = out[:, 0].reshape(lane_dev * slots, LAGS)
-    reverse = out[:, 1, :, ::-1].reshape(lane_dev * slots, LAGS)
-    terms = jnp.stack([forward, reverse])
     lag_dev = LAGS // rec_count
-    terms = terms.reshape(2, lane_dev * slots, rec_count, lag_dev).transpose(2, 0, 3, 1)
+    terms = correlate(got, slot_of, phased, rec_count)
     parts = lax.all_to_all(terms, "rec", split_axis=0, concat_axis=0, tiled=True)
     summed = jnp.sum(parts.reshape(rec_count, 2, lag_dev, lane_dev * slots), axis=0)
     valid = (

time: 132 us -> 122 us (0.924)
  local copies, waits for them, and re-layouts: 21.9 us -> 13.6 us
  matrix products: 3.09 us -> 0.75 us
    another operation x3 -> x0, local copies, waits for them, and re-layouts: 4.01 us -> none  [the longest x1 2.36 us: pick_rows(): flat = table.reshape(table.shape[0], -1)]
    dot_general x2 -> x1, matrix products: 3.09 us -> 0.75 us  [pick_rows(): jnp.dot(onehot, flat, preferred_element_type=jnp.float32)]
    transpose x1 -> x0, local copies, waits for them, and re-layouts: 1.69 us -> none  [per_device(): terms.reshape(2, lane_dev * slots, rec_count, lag_dev).transpose(2, 0, 3, 1)]
    rev x2 -> x1, local copies, waits for them, and re-layouts: 1.71 us -> 0.19 us  [per_device(): phased = jnp.concatenate([phased[:, :1], phased[:, 1:, ::-1]], axis=1)]
    transpose x1 -> x0, other arithmetic: 1.36 us -> none  [per_device(): terms.reshape(2, lane_dev * slots, rec_count, lag_dev).transpose(2, 0, 3, 1)]
    unnamed x8 -> x11, local copies, waits for them, and re-layouts: 3.5 us -> 4.24 us
  transfers between devices with their start and end apart: 5 -> 5, of which waited for: 4 -> 4; matrix products, arithmetic and copies ran while one was open for 8% -> 9% of each run, Pallas kernels for 0% -> 0%
where the time goes in v1:
time: 122 us; the launch traced here: 120 us
  waiting for transfers between devices  55.5 us (45%)
  starting transfers between devices  30.2 us (25%)
  local copies, waits for them, and re-layouts  13.6 us (11%)
  Pallas kernels  13.6 us (11%)
  other arithmetic  5.54 us (5%)
    all_to_all x1, waiting for transfers between devices, per_device(): got = lax.all_to_all(reply, 'lane', split_axis=0, concat_axis=0, tiled=True)  39.3 us
    pallas_call x1, Pallas kernels, correlate(): pl.pallas_call(lane_kernel, grid_spec=grid_spec, out_shape=jax.ShapeDtype...  13.6 us
    all_to_all x1, starting transfers between devices, per_device(): lax.all_to_all(send_index, 'lane', split_axis=0, concat_axis=0, tiled=True)  13 us
    all_to_all x1, waiting for transfers between devices, per_device(): lax.all_to_all(terms, 'rec', split_axis=0, concat_axis=0, tiled=True)  10.8 us
    all_to_all x1, starting transfers between devices, per_device(): lax.all_to_all(terms, 'rec', split_axis=0, concat_axis=0, tiled=True)  8.4 us
    all_to_all x1, starting transfers between devices, per_device(): got = lax.all_to_all(reply, 'lane', split_axis=0, concat_axis=0, tiled=True)  4.41 us
    ppermute x2, starting transfers between devices, passed_along(): return lax.ppermute(block, axis, route)  4.41 us
    all_to_all x1, waiting for transfers between devices, per_device(): lax.all_to_all(send_index, 'lane', split_axis=0, concat_axis=0, tiled=True)  4.27 us
  transfers between devices with their start and end apart: 5, of which 4 were waited for; matrix products, arithmetic and copies ran while one was open for 9% of the time, Pallas kernels for 0%

profile of v1, /device:TPU:1, one launch (start us, length us, event | category | flops | bytes accessed | tf_op | source)
XLA Modules:
  0.0 119.5 jit_solution(3292999169014559072)
XLA Ops:
  0.0 0.0 copy-start.1
  0.0 0.8 copy.16
  0.8 0.1 reshape.125
  0.9 0.2 convert_reduce_fusion
  1.1 0.0 copy-start.2
  1.1 0.1 select_reduce_fusion
  1.2 1.2 %gather_fusion = s32[128]{0:T(128)S(1)} fusion(s32[128]{0:T(128)S(1)} %get-tuple-element.7, s32[1024]{0:T(1024)S(1)} %pad_clamp_fusion), kind=kCustom, calls=%fused_computation | custom fusion | bytes 1536 | tf_op jit(solution)/shard_map/gather | solution.py:138
  2.5 0.7 all_to_all.12
  3.2 13.0 %all-to-all-start = ((s32[32,1,4]{2,1,0:T(1,128)}), s32[32,1,4]{2,1,0:T(1,128)S(1)}, u32[]{:S(2)}, u32[]{:S(2)}) async-start(s32[32,1,4]{2,1,0:T(1,128)} %bitcast.2), calls=%async_computation | async-start | bytes 32768 | tf_op jit(solution)/shard_map/all_to_all | solution.py:139
  16.2 1.0 add_convert_fusion
  17.2 0.8 stack.19
  18.0 0.3 copy.19
  18.3 0.0 copy-done.1
  18.3 0.8 stack.18
  19.2 0.0 copy-done.2
  19.2 0.3 copy.18
  19.5 0.2 copy.22
  19.7 4.3 %all-to-all-done = s32[32,1,4]{2,1,0:T(1,128)S(1)} async-done(((s32[32,1,4]{2,1,0:T(1,128)}), s32[32,1,4]{2,1,0:T(1,128)S(1)}, u32[]{:S(2)}, u32[]{:S(2)}) %all-to-all-start) | async-done | bytes 544 | tf_op jit(solution)/shard_map/all_to_all | solution.py:139
  23.9 0.5 broadcast.142
  24.5 0.7 reduce.3
  25.1 0.1 eq.46
  25.2 0.7 convolution_convert_fusion
  26.0 1.9 %copy.23 = bf16[16,8,32,256]{3,2,1,0:T(8,128)(2,1)} copy(bf16[16,8,32,256]{3,1,2,0:T(8,128)(2,1)S(1)} %bitcast.24) | data formatting | bytes 4194304
  27.9 4.4 %all-to-all-start.1 = ((bf16[32,4,2,16,256]{4,3,2,1,0:T(8,128)(2,1)}), bf16[32,4,2,16,256]{4,3,2,1,0:T(8,128)(2,1)S(1)}, u32[]{:S(2)}, u32[]{:S(2)}) async-start(bf16[32,4,2,16,256]{4,3,2,1,0:T(8,128)(2,1)} %bitcast.25), calls=%async_computation.1 | async-start | bytes 4194304 | tf_op jit(solution)/shard_map/all_to_all | solution.py:143
  32.4 3.1 %collective-permute-start.1 = (bf16[16,256]{1,0:T(8,128)(2,1)S(1)}, bf16[16,256]{1,0:T(8,128)(2,1)S(1)}, u32[]{:S(2)}, u32[]{:S(2)}) collective-permute-start(bf16[16,256]{1,0:T(8,128)(2,1)S(1)} %slice.22), channel_id=1, source_target_pairs={{0,1},{1,2},{2,3},{3,4},{4,5},{5,6},{6,7},{7,8},{8,9},{9,10},{10,1... | collective-permute-start | bytes 24584 | tf_op jit(solution)/shard_map/ppermute | solution.py:16
  35.5 1.3 %collective-permute-start = (bf16[16,256]{1,0:T(8,128)(2,1)S(1)}, bf16[16,256]{1,0:T(8,128)(2,1)S(1)}, u32[]{:S(2)}, u32[]{:S(2)}) collective-permute-start(bf16[16,256]{1,0:T(8,128)(2,1)S(1)} %slice.15), channel_id=1, source_target_pairs={{1,0},{2,1},{3,2},{4,3},{5,4},{6,5},{7,6},{8,7},{9,8},{10,9},{11,1... | collective-permute-start | bytes 24584 | tf_op jit(solution)/shard_map/ppermute | solution.py:16
  36.8 0.0 collective-permute-done.1
  36.9 0.1 slice.23
  36.9 0.2 concatenate.12
  37.1 0.8 stack.22
  37.9 1.1 copy.21
  39.1 1.1 collective-permute-done
  40.2 0.9 maximum_maximum_fusion
  41.1 0.8 stack.21
  42.0 1.1 copy.20
  43.1 1.1 maximum_bitcast_fusion
  44.2 0.2 rev.3
  44.4 0.8 fusion.2.refs_8_
  45.2 39.3 %all-to-all-done.1 = bf16[32,4,2,16,256]{4,3,2,1,0:T(8,128)(2,1)S(1)} async-done(((bf16[32,4,2,16,256]{4,3,2,1,0:T(8,128)(2,1)}), bf16[32,4,2,16,256]{4,3,2,1,0:T(8,128)(2,1)S(1)}, u32[]{:S(2)}, u32[]{:S(2)}) %all-to-all-start.1) | async-done | bytes 2097184 | tf_op jit(solution)/shard_map/all_to_all | solution.py:143
  84.5 0.0 copy-start
  84.5 1.3 %copy-done = bf16[32,4,2,16,256]{4,3,2,1,0:T(8,128)(2,1)} copy-done((bf16[32,4,2,16,256]{4,3,2,1,0:T(8,128)(2,1)}, bf16[32,4,2,16,256]{4,3,2,1,0:T(8,128)(2,1)S(1)}, u32[]{:S(2)}) %copy-start) | copy-done | bytes 2097176
  85.9 0.0 copy-start.3
  85.9 13.6 %shard_map.46 = f32[16,2,16,128]{3,2,1,0:T(8,128)} custom-call(s32[128]{0:T(128)} %copy-done.2, bf16[128,2,16,256]{3,2,1,0:T(8,128)(2,1)} %bitcast.16, bf16[128,2,16,256]{3,2,1,0:T(8,128)(2,1)} %bitcast.17, bf16[128,2,16,256]{3,2,1,0:T(8,128)(2,1)} %bitcast.18, bf16[128,2,16,256]{3,2,1,0:T(8,128)(2,1)} %bitcast.19, bf16[128,2,16,256]{3,2,1,0:T(8,128)(2,1)} %bitcast.20, ...), custom_call_target="tpu_custom_call" | custom-call | tf_op jit(solution)/shard_map/pallas_call | solution.py:105
  99.5 8.4 %all-to-all-start.2 = ((f32[16,2,16,128]{3,2,1,0:T(8,128)}), f32[16,2,16,128]{3,2,1,0:T(8,128)S(1)}, u32[]{:S(2)}, u32[]{:S(2)}) async-start(f32[16,2,16,128]{3,2,1,0:T(8,128)} %shard_map.46), calls=%async_computation.2 | async-start | bytes 524288 | tf_op jit(solution)/shard_map/all_to_all | solution.py:147
  107.9 0.0 copy-done.3
  107.9 0.1 fusion.5
  108.0 0.1 reshape.128
  108.1 10.8 %all-to-all-done.2 = f32[16,2,16,128]{3,2,1,0:T(8,128)S(1)} async-done(((f32[16,2,16,128]{3,2,1,0:T(8,128)}), f32[16,2,16,128]{3,2,1,0:T(8,128)S(1)}, u32[]{:S(2)}, u32[]{:S(2)}) %all-to-all-start.2) | async-done | bytes 262176 | tf_op jit(solution)/shard_map/all_to_all | solution.py:147
  118.9 0.6 multiply_multiply_fusion
  (12 shorter events, 0.1 us)
Async XLA Ops:
  0.0 18.3 %copy-start.1 = (bf16[16,4096]{1,0:T(8,128)(2,1)S(1)}, bf16[16,4096]{1,0:T(8,128)(2,1)}, u32[]{:S(2)}) copy-start(bf16[16,4096]{1,0:T(8,128)(2,1)} %param.4) | copy-start | bytes 393220
  1.1 18.1 %copy-start.2 = (s32[128]{0:T(128)}, s32[128]{0:T(128)S(1)}, u32[]{:S(2)}) copy-start(s32[128]{0:T(128)S(1)} %multiply_add_fusion.slot_ref) | copy-start | bytes 1540
  3.2 20.8 %all-to-all-start = ((s32[32,1,4]{2,1,0:T(1,128)}), s32[32,1,4]{2,1,0:T(1,128)S(1)}, u32[]{:S(2)}, u32[]{:S(2)}) async-start(s32[32,1,4]{2,1,0:T(1,128)} %bitcast.2), calls=%async_computation | async-start | bytes 32768 | tf_op jit(solution)/shard_map/all_to_all | solution.py:139
  27.9 56.6 %all-to-all-start.1 = ((bf16[32,4,2,16,256]{4,3,2,1,0:T(8,128)(2,1)}), bf16[32,4,2,16,256]{4,3,2,1,0:T(8,128)(2,1)S(1)}, u32[]{:S(2)}, u32[]{:S(2)}) async-start(bf16[32,4,2,16,256]{4,3,2,1,0:T(8,128)(2,1)} %bitcast.25), calls=%async_computation.1 | async-start | bytes 4194304 | tf_op jit(solution)/shard_map/all_to_all | solution.py:143
  32.4 4.5 %collective-permute-start.1 = (bf16[16,256]{1,0:T(8,128)(2,1)S(1)}, bf16[16,256]{1,0:T(8,128)(2,1)S(1)}, u32[]{:S(2)}, u32[]{:S(2)}) collective-permute-start(bf16[16,256]{1,0:T(8,128)(2,1)S(1)} %slice.22), channel_id=1, source_target_pairs={{0,1},{1,2},{2,3},{3,4},{4,5},{5,6},{6,7},{7,8},{8,9},{9,10},{10,1... | collective-permute-start | bytes 24584 | tf_op jit(solution)/shard_map/ppermute | solution.py:16
  35.5 4.7 %collective-permute-start = (bf16[16,256]{1,0:T(8,128)(2,1)S(1)}, bf16[16,256]{1,0:T(8,128)(2,1)S(1)}, u32[]{:S(2)}, u32[]{:S(2)}) collective-permute-start(bf16[16,256]{1,0:T(8,128)(2,1)S(1)} %slice.15), channel_id=1, source_target_pairs={{1,0},{2,1},{3,2},{4,3},{5,4},{6,5},{7,6},{8,7},{9,8},{10,9},{11,1... | collective-permute-start | bytes 24584 | tf_op jit(solution)/shard_map/ppermute | solution.py:16
  84.5 1.3 %copy-start = (bf16[32,4,2,16,256]{4,3,2,1,0:T(8,128)(2,1)}, bf16[32,4,2,16,256]{4,3,2,1,0:T(8,128)(2,1)S(1)}, u32[]{:S(2)}) copy-start(bf16[32,4,2,16,256]{4,3,2,1,0:T(8,128)(2,1)S(1)} %all-to-all-done.1) | copy-start | bytes 6291460
  85.9 22.0 %copy-start.3 = (s32[16]{0:T(128)S(1)}, s32[16]{0:T(128)}, u32[]{:S(2)}) copy-start(s32[16]{0:T(128)} %param.7) | copy-start | bytes 196
  99.5 19.4 %all-to-all-start.2 = ((f32[16,2,16,128]{3,2,1,0:T(8,128)}), f32[16,2,16,128]{3,2,1,0:T(8,128)S(1)}, u32[]{:S(2)}, u32[]{:S(2)}) async-start(f32[16,2,16,128]{3,2,1,0:T(8,128)} %shard_map.46), calls=%async_computation.2 | async-start | bytes 524288 | tf_op jit(solution)/shard_map/all_to_all | solution.py:147

commit v2 on v1

--- a/solution.py
+++ b/solution.py
@@ -39,27 +39,41 @@
     return out.reshape((onehot.shape[0],) + table.shape[1:])
 
 
-def lane_kernel(slot_ref, *refs):
-    del slot_ref
-    acc_ref = refs[-1]
-    cross_ref = refs[-2]
-    win_ref = refs[-3]
-    out_ref = refs[-4]
-    phased_ref = refs[-5]
-    row_refs = refs[:-5]
-    slots = len(row_refs)
-    blocks = win_ref.shape[1]
+def window_kernel(phased_ref, win_ref):
+    blocks = win_ref.shape[3]
     top = WIDE // PHASE - 1
-    lane = pl.program_id(0)
     for d in range(2):
         phased = phased_ref[0, d].astype(jnp.float32)
         for q in range(WIDE // PHASE):
             step = q if d == 0 else top - q
             shifted = phased if step == 0 else pltpu.roll(phased, WIDE - step, 1)
-            win_ref[q * PHASE : (q + 1) * PHASE, :] = shifted[:, :blocks].astype(jnp.bfloat16)
+            win_ref[0, d, q * PHASE : (q + 1) * PHASE, :] = shifted[:, :blocks].astype(jnp.bfloat16)
+
+
+def windows(phased, blocks):
+    lanes = phased.shape[0]
+    return pl.pallas_call(
+        window_kernel,
+        grid=(lanes,),
+        in_specs=[pl.BlockSpec((1, 2, PHASE, WIDE), lambda l: (l, 0, 0, 0))],
+        out_specs=pl.BlockSpec((1, 2, WIDE, blocks), lambda l: (l, 0, 0, 0)),
+        out_shape=jax.ShapeDtypeStruct((lanes, 2, WIDE, blocks), jnp.bfloat16),
+    )(phased)
+
+
+def lane_kernel(slot_ref, *refs):
+    del slot_ref
+    acc_ref = refs[-1]
+    cross_ref = refs[-2]
+    out_ref = refs[-3]
+    win_ref = refs[-4]
+    row_refs = refs[:-4]
+    slots = len(row_refs)
+    lane = pl.program_id(0)
+    for d in range(2):
         lhs = jnp.concatenate([ref[0, 1 - d] for ref in row_refs], axis=0)
         cross = lax.dot_general(
-            lhs, win_ref[...], (((1,), (1,)), ((), ())), preferred_element_type=jnp.float32
+            lhs, win_ref[0, d], (((1,), (1,)), ((), ())), preferred_element_type=jnp.float32
         )
         for c in range(WIDE // 128):
             cross_ref[c] = cross[:, c * 128 : (c + 1) * 128]
@@ -80,8 +94,8 @@
             out_ref[:, d] = flipped.reshape(out_ref.shape[0], out_ref.shape[2], out_ref.shape[3])
 
 
-def correlate(got, slot_of, phased, rec_count):
-    lanes = phased.shape[0]
+def correlate(got, slot_of, wins, rec_count):
+    lanes = wins.shape[0]
     pairs = slot_of.shape[0]
     slots = pairs // lanes
     blocks = got.shape[3]
@@ -94,10 +108,9 @@
         num_scalar_prefetch=1,
         grid=(lanes,),
         in_specs=[row_spec(s) for s in range(slots)]
-        + [pl.BlockSpec((1, 2, PHASE, WIDE), lambda l, slot: (l, 0, 0, 0))],
+        + [pl.BlockSpec((1, 2, WIDE, blocks), lambda l, slot: (l, 0, 0, 0))],
         out_specs=pl.BlockSpec((rec_count, 2, lag_dev, pairs), lambda l, slot: (0, 0, 0, 0)),
         scratch_shapes=[
-            pltpu.VMEM((WIDE, blocks), jnp.bfloat16),
             pltpu.VMEM((WIDE // 128, slots * PHASE, 128), jnp.float32),
             pltpu.VMEM((2, pairs, LAGS), jnp.float32),
         ],
@@ -106,7 +119,7 @@
         lane_kernel,
         grid_spec=grid_spec,
         out_shape=jax.ShapeDtypeStruct((rec_count, 2, lag_dev, pairs), jnp.float32),
-    )(slot_of, *([got] * slots), phased)
+    )(slot_of, *([got] * slots), wins)
 
 
 def per_device(waveforms, patterns, partners, counts):
@@ -143,7 +156,7 @@
     got = lax.all_to_all(reply, "lane", split_axis=0, concat_axis=0, tiled=True)
     got = got.reshape((lane_count * capacity,) + both.shape[1:])
     lag_dev = LAGS // rec_count
-    terms = correlate(got, slot_of, phased, rec_count)
+    terms = correlate(got, slot_of, windows(phased, blocks), rec_count)
     parts = lax.all_to_all(terms, "rec", split_axis=0, concat_axis=0, tiled=True)
     summed = jnp.sum(parts.reshape(rec_count, 2, lag_dev, lane_dev * slots), axis=0)
     valid = (

time: 122 us -> 123 us (level)
  Pallas kernels: 13.6 us -> 25 us
  waiting for transfers between devices: 55.5 us -> 46 us
    all_to_all x1, waiting for transfers between devices: 39.3 us -> 29 us  [per_device(): got = lax.all_to_all(reply, 'lane', split_axis=0, concat_axis=0, tiled=True)]
    pallas_call x0 -> x1, Pallas kernels: none -> 10.2 us  [windows(): pl.pallas_call(window_kernel, grid=(lanes,), in_specs=[pl.BlockSpec((1, 2...]
  transfers between devices with their start and end apart: 5 -> 5, of which waited for: 4 -> 4; matrix products, arithmetic and copies ran while one was open for 9% -> 9% of each run, Pallas kernels for 0% -> 8%
where the time goes in v2:
time: 123 us; the launch traced here: 121 us
  waiting for transfers between devices  46 us (37%)
  starting transfers between devices  30.2 us (25%)
  Pallas kernels  25 us (20%)
  local copies, waits for them, and re-layouts  13.7 us (11%)
  other arithmetic  5.61 us (5%)
    all_to_all x1, waiting for transfers between devices, per_device(): got = lax.all_to_all(reply, 'lane', split_axis=0, concat_axis=0, tiled=True)  29 us
    pallas_call x1, Pallas kernels, correlate(): pl.pallas_call(lane_kernel, grid_spec=grid_spec, out_shape=jax.ShapeDtype...  14.7 us
    all_to_all x1, starting transfers between devices, per_device(): lax.all_to_all(send_index, 'lane', split_axis=0, concat_axis=0, tiled=True)  13 us
    all_to_all x1, waiting for transfers between devices, per_device(): lax.all_to_all(terms, 'rec', split_axis=0, concat_axis=0, tiled=True)  11.6 us
    pallas_call x1, Pallas kernels, windows(): pl.pallas_call(window_kernel, grid=(lanes,), in_specs=[pl.BlockSpec((1, 2...  10.2 us
    all_to_all x1, starting transfers between devices, per_device(): lax.all_to_all(terms, 'rec', split_axis=0, concat_axis=0, tiled=True)  8.4 us
    all_to_all x1, starting transfers between devices, per_device(): got = lax.all_to_all(reply, 'lane', split_axis=0, concat_axis=0, tiled=True)  4.41 us
    ppermute x2, starting transfers between devices, passed_along(): return lax.ppermute(block, axis, route)  4.41 us
  transfers between devices with their start and end apart: 5, of which 4 were waited for; matrix products, arithmetic and copies ran while one was open for 9% of the time, Pallas kernels for 8%

profile of v2, /device:TPU:1, one launch (start us, length us, event | category | flops | bytes accessed | tf_op | source)
XLA Modules:
  0.0 121.5 jit_solution(18034550839357202728)
XLA Ops:
  0.0 0.0 copy-start.1
  0.0 0.8 copy.16
  0.8 0.1 reshape.125
  0.9 0.2 convert_reduce_fusion
  1.1 0.0 copy-start.2
  1.1 0.1 select_reduce_fusion
  1.2 1.2 %gather_fusion = s32[128]{0:T(128)S(1)} fusion(s32[128]{0:T(128)S(1)} %get-tuple-element.7, s32[1024]{0:T(1024)S(1)} %pad_clamp_fusion), kind=kCustom, calls=%fused_computation | custom fusion | bytes 1536 | tf_op jit(solution)/shard_map/gather | solution.py:151
  2.5 0.7 all_to_all.12
  3.2 13.0 %all-to-all-start = ((s32[32,1,4]{2,1,0:T(1,128)}), s32[32,1,4]{2,1,0:T(1,128)S(1)}, u32[]{:S(2)}, u32[]{:S(2)}) async-start(s32[32,1,4]{2,1,0:T(1,128)} %bitcast.2), calls=%async_computation | async-start | bytes 32768 | tf_op jit(solution)/shard_map/all_to_all | solution.py:152
  16.2 1.0 add_convert_fusion
  17.2 0.8 stack.19
  18.0 0.3 copy.19
  18.3 0.0 copy-done.1
  18.3 0.8 stack.18
  19.2 0.0 copy-done.2
  19.2 0.3 copy.18
  19.5 0.2 copy.22
  19.7 4.3 %all-to-all-done = s32[32,1,4]{2,1,0:T(1,128)S(1)} async-done(((s32[32,1,4]{2,1,0:T(1,128)}), s32[32,1,4]{2,1,0:T(1,128)S(1)}, u32[]{:S(2)}, u32[]{:S(2)}) %all-to-all-start) | async-done | bytes 544 | tf_op jit(solution)/shard_map/all_to_all | solution.py:152
  23.9 0.5 broadcast.142
  24.5 0.7 reduce.3
  25.1 0.1 eq.46
  25.2 0.7 convolution_convert_fusion
  26.0 2.0 %copy.23 = bf16[16,8,32,256]{3,2,1,0:T(8,128)(2,1)} copy(bf16[16,8,32,256]{3,1,2,0:T(8,128)(2,1)S(1)} %bitcast.24) | data formatting | bytes 4194304
  28.0 4.4 %all-to-all-start.1 = ((bf16[32,4,2,16,256]{4,3,2,1,0:T(8,128)(2,1)}), bf16[32,4,2,16,256]{4,3,2,1,0:T(8,128)(2,1)S(1)}, u32[]{:S(2)}, u32[]{:S(2)}) async-start(bf16[32,4,2,16,256]{4,3,2,1,0:T(8,128)(2,1)} %bitcast.25), calls=%async_computation.1 | async-start | bytes 4194304 | tf_op jit(solution)/shard_map/all_to_all | solution.py:156
  32.4 3.1 %collective-permute-start.1 = (bf16[16,256]{1,0:T(8,128)(2,1)S(1)}, bf16[16,256]{1,0:T(8,128)(2,1)S(1)}, u32[]{:S(2)}, u32[]{:S(2)}) collective-permute-start(bf16[16,256]{1,0:T(8,128)(2,1)S(1)} %slice.22), channel_id=1, source_target_pairs={{0,1},{1,2},{2,3},{3,4},{4,5},{5,6},{6,7},{7,8},{8,9},{9,10},{10,1... | collective-permute-start | bytes 24584 | tf_op jit(solution)/shard_map/ppermute | solution.py:16
  35.5 1.3 %collective-permute-start = (bf16[16,256]{1,0:T(8,128)(2,1)S(1)}, bf16[16,256]{1,0:T(8,128)(2,1)S(1)}, u32[]{:S(2)}, u32[]{:S(2)}) collective-permute-start(bf16[16,256]{1,0:T(8,128)(2,1)S(1)} %slice.15), channel_id=1, source_target_pairs={{1,0},{2,1},{3,2},{4,3},{5,4},{6,5},{7,6},{8,7},{9,8},{10,9},{11,1... | collective-permute-start | bytes 24584 | tf_op jit(solution)/shard_map/ppermute | solution.py:16
  36.9 0.0 collective-permute-done.1
  36.9 0.1 slice.23
  36.9 0.2 concatenate.12
  37.1 0.8 stack.22
  37.9 1.1 copy.21
  39.1 1.2 collective-permute-done
  40.2 0.9 maximum_maximum_fusion
  41.2 0.8 stack.21
  42.0 1.1 copy.20
  43.1 1.1 maximum_bitcast_fusion
  44.3 0.2 rev.3
  44.5 0.9 fusion.2.phased_ref
  45.3 10.2 %shard_map.46.refs_8_ = bf16[16,2,384,256]{3,2,1,0:T(8,128)(2,1)} custom-call(bf16[16,2,16,384]{3,2,1,0:T(8,128)(2,1)} %fusion.2.phased_ref), custom_call_target="tpu_custom_call" | custom-call | tf_op jit(solution)/shard_map/pallas_call | solution.py:55
  55.6 29.0 %all-to-all-done.1 = bf16[32,4,2,16,256]{4,3,2,1,0:T(8,128)(2,1)S(1)} async-done(((bf16[32,4,2,16,256]{4,3,2,1,0:T(8,128)(2,1)}), bf16[32,4,2,16,256]{4,3,2,1,0:T(8,128)(2,1)S(1)}, u32[]{:S(2)}, u32[]{:S(2)}) %all-to-all-start.1) | async-done | bytes 2097184 | tf_op jit(solution)/shard_map/all_to_all | solution.py:156
  84.6 0.0 copy-start
  84.6 1.3 %copy-done = bf16[32,4,2,16,256]{4,3,2,1,0:T(8,128)(2,1)} copy-done((bf16[32,4,2,16,256]{4,3,2,1,0:T(8,128)(2,1)}, bf16[32,4,2,16,256]{4,3,2,1,0:T(8,128)(2,1)S(1)}, u32[]{:S(2)}) %copy-start) | copy-done | bytes 2097176
  85.9 0.0 copy-start.3
  85.9 14.7 %shard_map.47 = f32[16,2,16,128]{3,2,1,0:T(8,128)} custom-call(s32[128]{0:T(128)} %copy-done.2, bf16[128,2,16,256]{3,2,1,0:T(8,128)(2,1)} %bitcast.16, bf16[128,2,16,256]{3,2,1,0:T(8,128)(2,1)} %bitcast.17, bf16[128,2,16,256]{3,2,1,0:T(8,128)(2,1)} %bitcast.18, bf16[128,2,16,256]{3,2,1,0:T(8,128)(2,1)} %bitcast.19, bf16[128,2,16,256]{3,2,1,0:T(8,128)(2,1)} %bitcast.20, ...), custom_call_target="tpu_custom_call" | custom-call | tf_op jit(solution)/shard_map/pallas_call | solution.py:118
  100.6 8.4 %all-to-all-start.2 = ((f32[16,2,16,128]{3,2,1,0:T(8,128)}), f32[16,2,16,128]{3,2,1,0:T(8,128)S(1)}, u32[]{:S(2)}, u32[]{:S(2)}) async-start(f32[16,2,16,128]{3,2,1,0:T(8,128)} %shard_map.47), calls=%async_computation.2 | async-start | bytes 524288 | tf_op jit(solution)/shard_map/all_to_all | solution.py:160
  109.1 0.0 copy-done.3
  109.1 0.1 fusion.5
  109.1 0.1 reshape.128
  109.2 11.6 %all-to-all-done.2 = f32[16,2,16,128]{3,2,1,0:T(8,128)S(1)} async-done(((f32[16,2,16,128]{3,2,1,0:T(8,128)}), f32[16,2,16,128]{3,2,1,0:T(8,128)S(1)}, u32[]{:S(2)}, u32[]{:S(2)}) %all-to-all-start.2) | async-done | bytes 262176 | tf_op jit(solution)/shard_map/all_to_all | solution.py:160
  120.8 0.6 multiply_multiply_fusion
  (12 shorter events, 0.1 us)
Async XLA Ops:
  0.0 18.3 %copy-start.1 = (bf16[16,4096]{1,0:T(8,128)(2,1)S(1)}, bf16[16,4096]{1,0:T(8,128)(2,1)}, u32[]{:S(2)}) copy-start(bf16[16,4096]{1,0:T(8,128)(2,1)} %param.4) | copy-start | bytes 393220
  1.1 18.1 %copy-start.2 = (s32[128]{0:T(128)}, s32[128]{0:T(128)S(1)}, u32[]{:S(2)}) copy-start(s32[128]{0:T(128)S(1)} %multiply_add_fusion.slot_ref) | copy-start | bytes 1540
  3.2 20.8 %all-to-all-start = ((s32[32,1,4]{2,1,0:T(1,128)}), s32[32,1,4]{2,1,0:T(1,128)S(1)}, u32[]{:S(2)}, u32[]{:S(2)}) async-start(s32[32,1,4]{2,1,0:T(1,128)} %bitcast.2), calls=%async_computation | async-start | bytes 32768 | tf_op jit(solution)/shard_map/all_to_all | solution.py:152
  28.0 56.6 %all-to-all-start.1 = ((bf16[32,4,2,16,256]{4,3,2,1,0:T(8,128)(2,1)}), bf16[32,4,2,16,256]{4,3,2,1,0:T(8,128)(2,1)S(1)}, u32[]{:S(2)}, u32[]{:S(2)}) async-start(bf16[32,4,2,16,256]{4,3,2,1,0:T(8,128)(2,1)} %bitcast.25), calls=%async_computation.1 | async-start | bytes 4194304 | tf_op jit(solution)/shard_map/all_to_all | solution.py:156
  32.4 4.5 %collective-permute-start.1 = (bf16[16,256]{1,0:T(8,128)(2,1)S(1)}, bf16[16,256]{1,0:T(8,128)(2,1)S(1)}, u32[]{:S(2)}, u32[]{:S(2)}) collective-permute-start(bf16[16,256]{1,0:T(8,128)(2,1)S(1)} %slice.22), channel_id=1, source_target_pairs={{0,1},{1,2},{2,3},{3,4},{4,5},{5,6},{6,7},{7,8},{8,9},{9,10},{10,1... | collective-permute-start | bytes 24584 | tf_op jit(solution)/shard_map/ppermute | solution.py:16
  35.5 4.7 %collective-permute-start = (bf16[16,256]{1,0:T(8,128)(2,1)S(1)}, bf16[16,256]{1,0:T(8,128)(2,1)S(1)}, u32[]{:S(2)}, u32[]{:S(2)}) collective-permute-start(bf16[16,256]{1,0:T(8,128)(2,1)S(1)} %slice.15), channel_id=1, source_target_pairs={{1,0},{2,1},{3,2},{4,3},{5,4},{6,5},{7,6},{8,7},{9,8},{10,9},{11,1... | collective-permute-start | bytes 24584 | tf_op jit(solution)/shard_map/ppermute | solution.py:16
  84.6 1.3 %copy-start = (bf16[32,4,2,16,256]{4,3,2,1,0:T(8,128)(2,1)}, bf16[32,4,2,16,256]{4,3,2,1,0:T(8,128)(2,1)S(1)}, u32[]{:S(2)}) copy-start(bf16[32,4,2,16,256]{4,3,2,1,0:T(8,128)(2,1)S(1)} %all-to-all-done.1) | copy-start | bytes 6291460
  85.9 23.2 %copy-start.3 = (s32[16]{0:T(128)S(1)}, s32[16]{0:T(128)}, u32[]{:S(2)}) copy-start(s32[16]{0:T(128)} %param.7) | copy-start | bytes 196
  100.6 20.2 %all-to-all-start.2 = ((f32[16,2,16,128]{3,2,1,0:T(8,128)}), f32[16,2,16,128]{3,2,1,0:T(8,128)S(1)}, u32[]{:S(2)}, u32[]{:S(2)}) async-start(f32[16,2,16,128]{3,2,1,0:T(8,128)} %shard_map.47), calls=%async_computation.2 | async-start | bytes 524288 | tf_op jit(solution)/shard_map/all_to_all | solution.py:160

commit v3 on v2

--- a/solution.py
+++ b/solution.py
@@ -40,14 +40,16 @@
 
 
 def window_kernel(phased_ref, win_ref):
-    blocks = win_ref.shape[3]
+    blocks = win_ref.shape[2]
     top = WIDE // PHASE - 1
     for d in range(2):
         phased = phased_ref[0, d].astype(jnp.float32)
+        parts = []
         for q in range(WIDE // PHASE):
             step = q if d == 0 else top - q
             shifted = phased if step == 0 else pltpu.roll(phased, WIDE - step, 1)
-            win_ref[0, d, q * PHASE : (q + 1) * PHASE, :] = shifted[:, :blocks].astype(jnp.bfloat16)
+            parts.append(shifted[:, :blocks])
+        win_ref[0, d] = jnp.concatenate(parts, axis=0).T.astype(jnp.bfloat16)
 
 
 def windows(phased, blocks):
@@ -56,8 +58,8 @@
         window_kernel,
         grid=(lanes,),
         in_specs=[pl.BlockSpec((1, 2, PHASE, WIDE), lambda l: (l, 0, 0, 0))],
-        out_specs=pl.BlockSpec((1, 2, WIDE, blocks), lambda l: (l, 0, 0, 0)),
-        out_shape=jax.ShapeDtypeStruct((lanes, 2, WIDE, blocks), jnp.bfloat16),
+        out_specs=pl.BlockSpec((1, 2, blocks, WIDE), lambda l: (l, 0, 0, 0)),
+        out_shape=jax.ShapeDtypeStruct((lanes, 2, blocks, WIDE), jnp.bfloat16),
     )(phased)
 
 
@@ -73,7 +75,7 @@
     for d in range(2):
         lhs = jnp.concatenate([ref[0, 1 - d] for ref in row_refs], axis=0)
         cross = lax.dot_general(
-            lhs, win_ref[0, d], (((1,), (1,)), ((), ())), preferred_element_type=jnp.float32
+            lhs, win_ref[0, d], (((1,), (0,)), ((), ())), preferred_element_type=jnp.float32
         )
         for c in range(WIDE // 128):
             cross_ref[c] = cross[:, c * 128 : (c + 1) * 128]
@@ -108,7 +110,7 @@
         num_scalar_prefetch=1,
         grid=(lanes,),
         in_specs=[row_spec(s) for s in range(slots)]
-        + [pl.BlockSpec((1, 2, WIDE, blocks), lambda l, slot: (l, 0, 0, 0))],
+        + [pl.BlockSpec((1, 2, blocks, WIDE), lambda l, slot: (l, 0, 0, 0))],
         out_specs=pl.BlockSpec((rec_count, 2, lag_dev, pairs), lambda l, slot: (0, 0, 0, 0)),
         scratch_shapes=[
             pltpu.VMEM((WIDE // 128, slots * PHASE, 128), jnp.float32),

time: 123 us -> 123 us (level)
  transfers between devices with their start and end apart: 5 -> 5, of which waited for: 4 -> 4; matrix products, arithmetic and copies ran while one was open for 9% -> 9% of each run, Pallas kernels for 8% -> 9%
where the time goes in v3:
time: 123 us; the launch traced here: 121 us
  waiting for transfers between devices  45.4 us (37%)
  starting transfers between devices  30.2 us (25%)
  Pallas kernels  25.6 us (21%)
  local copies, waits for them, and re-layouts  13.7 us (11%)
  other arithmetic  5.61 us (5%)
    all_to_all x1, waiting for transfers between devices, per_device(): got = lax.all_to_all(reply, 'lane', split_axis=0, concat_axis=0, tiled=True)  28.2 us
    pallas_call x1, Pallas kernels, correlate(): pl.pallas_call(lane_kernel, grid_spec=grid_spec, out_shape=jax.ShapeDtype...  14.6 us
    all_to_all x1, starting transfers between devices, per_device(): lax.all_to_all(send_index, 'lane', split_axis=0, concat_axis=0, tiled=True)  13 us
    all_to_all x1, waiting for transfers between devices, per_device(): lax.all_to_all(terms, 'rec', split_axis=0, concat_axis=0, tiled=True)  11.8 us
    pallas_call x1, Pallas kernels, windows(): pl.pallas_call(window_kernel, grid=(lanes,), in_specs=[pl.BlockSpec((1, 2...  11 us
    all_to_all x1, starting transfers between devices, per_device(): lax.all_to_all(terms, 'rec', split_axis=0, concat_axis=0, tiled=True)  8.4 us
    all_to_all x1, starting transfers between devices, per_device(): got = lax.all_to_all(reply, 'lane', split_axis=0, concat_axis=0, tiled=True)  4.41 us
    ppermute x2, starting transfers between devices, passed_along(): return lax.ppermute(block, axis, route)  4.41 us
  transfers between devices with their start and end apart: 5, of which 4 were waited for; matrix products, arithmetic and copies ran while one was open for 9% of the time, Pallas kernels for 9%

profile of v3, /device:TPU:1, one launch (start us, length us, event | category | flops | bytes accessed | tf_op | source)
XLA Modules:
  0.0 121.5 jit_solution(1922662117858578196)
XLA Ops:
  0.0 0.0 copy-start.1
  0.0 0.8 copy.16
  0.8 0.1 reshape.125
  0.9 0.2 convert_reduce_fusion
  1.1 0.0 copy-start.2
  1.1 0.1 select_reduce_fusion
  1.2 1.2 %gather_fusion = s32[128]{0:T(128)S(1)} fusion(s32[128]{0:T(128)S(1)} %get-tuple-element.7, s32[1024]{0:T(1024)S(1)} %pad_clamp_fusion), kind=kCustom, calls=%fused_computation | custom fusion | bytes 1536 | tf_op jit(solution)/shard_map/gather | solution.py:153
  2.5 0.7 all_to_all.12
  3.2 13.0 %all-to-all-start = ((s32[32,1,4]{2,1,0:T(1,128)}), s32[32,1,4]{2,1,0:T(1,128)S(1)}, u32[]{:S(2)}, u32[]{:S(2)}) async-start(s32[32,1,4]{2,1,0:T(1,128)} %bitcast.2), calls=%async_computation | async-start | bytes 32768 | tf_op jit(solution)/shard_map/all_to_all | solution.py:154
  16.2 1.0 add_convert_fusion
  17.2 0.8 stack.19
  18.0 0.3 copy.19
  18.3 0.0 copy-done.1
  18.3 0.8 stack.18
  19.2 0.0 copy-done.2
  19.2 0.3 copy.18
  19.5 0.2 copy.22
  19.7 4.3 %all-to-all-done = s32[32,1,4]{2,1,0:T(1,128)S(1)} async-done(((s32[32,1,4]{2,1,0:T(1,128)}), s32[32,1,4]{2,1,0:T(1,128)S(1)}, u32[]{:S(2)}, u32[]{:S(2)}) %all-to-all-start) | async-done | bytes 544 | tf_op jit(solution)/shard_map/all_to_all | solution.py:154
  23.9 0.5 broadcast.142
  24.5 0.7 reduce.3
  25.1 0.1 eq.46
  25.2 0.7 convolution_convert_fusion
  26.0 2.0 %copy.23 = bf16[16,8,32,256]{3,2,1,0:T(8,128)(2,1)} copy(bf16[16,8,32,256]{3,1,2,0:T(8,128)(2,1)S(1)} %bitcast.24) | data formatting | bytes 4194304
  28.0 4.4 %all-to-all-start.1 = ((bf16[32,4,2,16,256]{4,3,2,1,0:T(8,128)(2,1)}), bf16[32,4,2,16,256]{4,3,2,1,0:T(8,128)(2,1)S(1)}, u32[]{:S(2)}, u32[]{:S(2)}) async-start(bf16[32,4,2,16,256]{4,3,2,1,0:T(8,128)(2,1)} %bitcast.25), calls=%async_computation.1 | async-start | bytes 4194304 | tf_op jit(solution)/shard_map/all_to_all | solution.py:158
  32.4 3.1 %collective-permute-start.1 = (bf16[16,256]{1,0:T(8,128)(2,1)S(1)}, bf16[16,256]{1,0:T(8,128)(2,1)S(1)}, u32[]{:S(2)}, u32[]{:S(2)}) collective-permute-start(bf16[16,256]{1,0:T(8,128)(2,1)S(1)} %slice.22), channel_id=1, source_target_pairs={{0,1},{1,2},{2,3},{3,4},{4,5},{5,6},{6,7},{7,8},{8,9},{9,10},{10,1... | collective-permute-start | bytes 24584 | tf_op jit(solution)/shard_map/ppermute | solution.py:16
  35.5 1.3 %collective-permute-start = (bf16[16,256]{1,0:T(8,128)(2,1)S(1)}, bf16[16,256]{1,0:T(8,128)(2,1)S(1)}, u32[]{:S(2)}, u32[]{:S(2)}) collective-permute-start(bf16[16,256]{1,0:T(8,128)(2,1)S(1)} %slice.15), channel_id=1, source_target_pairs={{1,0},{2,1},{3,2},{4,3},{5,4},{6,5},{7,6},{8,7},{9,8},{10,9},{11,1... | collective-permute-start | bytes 24584 | tf_op jit(solution)/shard_map/ppermute | solution.py:16
  36.9 0.0 collective-permute-done.1
  36.9 0.1 slice.23
  36.9 0.2 concatenate.12
  37.1 0.8 stack.22
  37.9 1.1 copy.21
  39.1 1.2 collective-permute-done
  40.2 0.9 maximum_maximum_fusion
  41.2 0.8 stack.21
  42.0 1.1 copy.20
  43.1 1.1 maximum_bitcast_fusion
  44.3 0.2 rev.3
  44.5 0.9 fusion.2.phased_ref
  45.3 11.0 %shard_map.46.refs_8_ = bf16[16,2,256,384]{3,2,1,0:T(8,128)(2,1)} custom-call(bf16[16,2,16,384]{3,2,1,0:T(8,128)(2,1)} %fusion.2.phased_ref), custom_call_target="tpu_custom_call" | custom-call | tf_op jit(solution)/shard_map/pallas_call | solution.py:57
  56.3 28.2 %all-to-all-done.1 = bf16[32,4,2,16,256]{4,3,2,1,0:T(8,128)(2,1)S(1)} async-done(((bf16[32,4,2,16,256]{4,3,2,1,0:T(8,128)(2,1)}), bf16[32,4,2,16,256]{4,3,2,1,0:T(8,128)(2,1)S(1)}, u32[]{:S(2)}, u32[]{:S(2)}) %all-to-all-start.1) | async-done | bytes 2097184 | tf_op jit(solution)/shard_map/all_to_all | solution.py:158
  84.6 0.0 copy-start
  84.6 1.3 %copy-done = bf16[32,4,2,16,256]{4,3,2,1,0:T(8,128)(2,1)} copy-done((bf16[32,4,2,16,256]{4,3,2,1,0:T(8,128)(2,1)}, bf16[32,4,2,16,256]{4,3,2,1,0:T(8,128)(2,1)S(1)}, u32[]{:S(2)}) %copy-start) | copy-done | bytes 2097176
  85.9 0.0 copy-start.3
  85.9 14.6 %shard_map.47 = f32[16,2,16,128]{3,2,1,0:T(8,128)} custom-call(s32[128]{0:T(128)} %copy-done.2, bf16[128,2,16,256]{3,2,1,0:T(8,128)(2,1)} %bitcast.16, bf16[128,2,16,256]{3,2,1,0:T(8,128)(2,1)} %bitcast.17, bf16[128,2,16,256]{3,2,1,0:T(8,128)(2,1)} %bitcast.18, bf16[128,2,16,256]{3,2,1,0:T(8,128)(2,1)} %bitcast.19, bf16[128,2,16,256]{3,2,1,0:T(8,128)(2,1)} %bitcast.20, ...), custom_call_target="tpu_custom_call" | custom-call | tf_op jit(solution)/shard_map/pallas_call | solution.py:120
  100.5 8.4 %all-to-all-start.2 = ((f32[16,2,16,128]{3,2,1,0:T(8,128)}), f32[16,2,16,128]{3,2,1,0:T(8,128)S(1)}, u32[]{:S(2)}, u32[]{:S(2)}) async-start(f32[16,2,16,128]{3,2,1,0:T(8,128)} %shard_map.47), calls=%async_computation.2 | async-start | bytes 524288 | tf_op jit(solution)/shard_map/all_to_all | solution.py:162
  108.9 0.0 copy-done.3
  108.9 0.1 fusion.5
  109.0 0.1 reshape.128
  109.0 11.8 %all-to-all-done.2 = f32[16,2,16,128]{3,2,1,0:T(8,128)S(1)} async-done(((f32[16,2,16,128]{3,2,1,0:T(8,128)}), f32[16,2,16,128]{3,2,1,0:T(8,128)S(1)}, u32[]{:S(2)}, u32[]{:S(2)}) %all-to-all-start.2) | async-done | bytes 262176 | tf_op jit(solution)/shard_map/all_to_all | solution.py:162
  120.9 0.6 multiply_multiply_fusion
  (12 shorter events, 0.1 us)
Async XLA Ops:
  0.0 18.3 %copy-start.1 = (bf16[16,4096]{1,0:T(8,128)(2,1)S(1)}, bf16[16,4096]{1,0:T(8,128)(2,1)}, u32[]{:S(2)}) copy-start(bf16[16,4096]{1,0:T(8,128)(2,1)} %param.4) | copy-start | bytes 393220
  1.1 18.1 %copy-start.2 = (s32[128]{0:T(128)}, s32[128]{0:T(128)S(1)}, u32[]{:S(2)}) copy-start(s32[128]{0:T(128)S(1)} %multiply_add_fusion.slot_ref) | copy-start | bytes 1540
  3.2 20.8 %all-to-all-start = ((s32[32,1,4]{2,1,0:T(1,128)}), s32[32,1,4]{2,1,0:T(1,128)S(1)}, u32[]{:S(2)}, u32[]{:S(2)}) async-start(s32[32,1,4]{2,1,0:T(1,128)} %bitcast.2), calls=%async_computation | async-start | bytes 32768 | tf_op jit(solution)/shard_map/all_to_all | solution.py:154
  28.0 56.6 %all-to-all-start.1 = ((bf16[32,4,2,16,256]{4,3,2,1,0:T(8,128)(2,1)}), bf16[32,4,2,16,256]{4,3,2,1,0:T(8,128)(2,1)S(1)}, u32[]{:S(2)}, u32[]{:S(2)}) async-start(bf16[32,4,2,16,256]{4,3,2,1,0:T(8,128)(2,1)} %bitcast.25), calls=%async_computation.1 | async-start | bytes 4194304 | tf_op jit(solution)/shard_map/all_to_all | solution.py:158
  32.4 4.5 %collective-permute-start.1 = (bf16[16,256]{1,0:T(8,128)(2,1)S(1)}, bf16[16,256]{1,0:T(8,128)(2,1)S(1)}, u32[]{:S(2)}, u32[]{:S(2)}) collective-permute-start(bf16[16,256]{1,0:T(8,128)(2,1)S(1)} %slice.22), channel_id=1, source_target_pairs={{0,1},{1,2},{2,3},{3,4},{4,5},{5,6},{6,7},{7,8},{8,9},{9,10},{10,1... | collective-permute-start | bytes 24584 | tf_op jit(solution)/shard_map/ppermute | solution.py:16
  35.5 4.7 %collective-permute-start = (bf16[16,256]{1,0:T(8,128)(2,1)S(1)}, bf16[16,256]{1,0:T(8,128)(2,1)S(1)}, u32[]{:S(2)}, u32[]{:S(2)}) collective-permute-start(bf16[16,256]{1,0:T(8,128)(2,1)S(1)} %slice.15), channel_id=1, source_target_pairs={{1,0},{2,1},{3,2},{4,3},{5,4},{6,5},{7,6},{8,7},{9,8},{10,9},{11,1... | collective-permute-start | bytes 24584 | tf_op jit(solution)/shard_map/ppermute | solution.py:16
  84.6 1.3 %copy-start = (bf16[32,4,2,16,256]{4,3,2,1,0:T(8,128)(2,1)}, bf16[32,4,2,16,256]{4,3,2,1,0:T(8,128)(2,1)S(1)}, u32[]{:S(2)}) copy-start(bf16[32,4,2,16,256]{4,3,2,1,0:T(8,128)(2,1)S(1)} %all-to-all-done.1) | copy-start | bytes 6291460
  85.9 23.0 %copy-start.3 = (s32[16]{0:T(128)S(1)}, s32[16]{0:T(128)}, u32[]{:S(2)}) copy-start(s32[16]{0:T(128)} %param.7) | copy-start | bytes 196
  100.5 20.4 %all-to-all-start.2 = ((f32[16,2,16,128]{3,2,1,0:T(8,128)}), f32[16,2,16,128]{3,2,1,0:T(8,128)S(1)}, u32[]{:S(2)}, u32[]{:S(2)}) async-start(f32[16,2,16,128]{3,2,1,0:T(8,128)} %shard_map.47), calls=%async_computation.2 | async-start | bytes 524288 | tf_op jit(solution)/shard_map/all_to_all | solution.py:162

commit v4 on v3

--- a/solution.py
+++ b/solution.py
@@ -66,10 +66,9 @@
 def lane_kernel(slot_ref, *refs):
     del slot_ref
     acc_ref = refs[-1]
-    cross_ref = refs[-2]
-    out_ref = refs[-3]
-    win_ref = refs[-4]
-    row_refs = refs[:-4]
+    out_ref = refs[-2]
+    win_ref = refs[-3]
+    row_refs = refs[:-3]
     slots = len(row_refs)
     lane = pl.program_id(0)
     for d in range(2):
@@ -77,16 +76,13 @@
         cross = lax.dot_general(
             lhs, win_ref[0, d], (((1,), (0,)), ((), ())), preferred_element_type=jnp.float32
         )
-        for c in range(WIDE // 128):
-            cross_ref[c] = cross[:, c * 128 : (c + 1) * 128]
-        total = None
-        for i in range(PHASE):
-            picked = jnp.concatenate(
-                [cross_ref[c, pl.ds(i, slots, stride=PHASE), :] for c in range(WIDE // 128)], axis=1
-            )
-            step = i if d == 0 else (WIDE - LAGS) - i
-            shifted = picked if step == 0 else pltpu.roll(picked, WIDE - step, 1)
-            total = shifted[:, :LAGS] if total is None else total + shifted[:, :LAGS]
+        base = WIDE - (PHASE - 1) if d == 0 else LAGS
+        sums = []
+        for s in range(slots):
+            block = cross[s * PHASE : (s + 1) * PHASE, :]
+            lined = pltpu.roll(block, base, 1, stride=1, stride_axis=0)
+            sums.append(jnp.sum(lined, axis=0, keepdims=True))
+        total = jnp.concatenate(sums, axis=0)[:, :LAGS]
         acc_ref[d, pl.ds(pl.multiple_of(lane * slots, slots), slots), :] = total
 
     @pl.when(lane == pl.num_programs(0) - 1)
@@ -113,7 +109,6 @@
         + [pl.BlockSpec((1, 2, blocks, WIDE), lambda l, slot: (l, 0, 0, 0))],
         out_specs=pl.BlockSpec((rec_count, 2, lag_dev, pairs), lambda l, slot: (0, 0, 0, 0)),
         scratch_shapes=[
-            pltpu.VMEM((WIDE // 128, slots * PHASE, 128), jnp.float32),
             pltpu.VMEM((2, pairs, LAGS), jnp.float32),
         ],
     )
@@ -153,6 +148,7 @@
     send_index = local_index[order].reshape(lane_count, capacity)
     index_in = lax.all_to_all(send_index, "lane", split_axis=0, concat_axis=0, tiled=True)
     both = deinterleave(jnp.stack([waveforms, levels], axis=1))
+    both = jnp.concatenate([both[:, :1], both[:, 1:, ::-1]], axis=1)
     pick = (index_in.reshape(-1)[:, None] == jnp.arange(lane_dev)[None, :]).astype(jnp.bfloat16)
     reply = pick_rows(pick, both).reshape((lane_count, capacity) + both.shape[1:])
     got = lax.all_to_all(reply, "lane", split_axis=0, concat_axis=0, tiled=True)

time: 123 us -> 123 us (level)
  no operation moved by 1% of the time
where the time goes in v4:
time: 123 us; the launch traced here: 121 us
  waiting for transfers between devices  45.3 us (37%)
  starting transfers between devices  30.2 us (25%)
  Pallas kernels  25.4 us (21%)
  local copies, waits for them, and re-layouts  13.8 us (11%)
  other arithmetic  5.62 us (5%)
    all_to_all x1, waiting for transfers between devices, per_device(): got = lax.all_to_all(reply, 'lane', split_axis=0, concat_axis=0, tiled=True)  28.2 us
    pallas_call x1, Pallas kernels, correlate(): pl.pallas_call(lane_kernel, grid_spec=grid_spec, out_shape=jax.ShapeDtype...  14.3 us
    all_to_all x1, starting transfers between devices, per_device(): lax.all_to_all(send_index, 'lane', split_axis=0, concat_axis=0, tiled=True)  13 us
    all_to_all x1, waiting for transfers between devices, per_device(): lax.all_to_all(terms, 'rec', split_axis=0, concat_axis=0, tiled=True)  11.9 us
    pallas_call x1, Pallas kernels, windows(): pl.pallas_call(window_kernel, grid=(lanes,), in_specs=[pl.BlockSpec((1, 2...  11 us
    all_to_all x1, starting transfers between devices, per_device(): lax.all_to_all(terms, 'rec', split_axis=0, concat_axis=0, tiled=True)  8.4 us
    all_to_all x1, starting transfers between devices, per_device(): got = lax.all_to_all(reply, 'lane', split_axis=0, concat_axis=0, tiled=True)  4.41 us
    ppermute x2, starting transfers between devices, passed_along(): return lax.ppermute(block, axis, route)  4.41 us
  transfers between devices with their start and end apart: 5, of which 4 were waited for; matrix products, arithmetic and copies ran while one was open for 9% of the time, Pallas kernels for 9%

profile of v4, /device:TPU:1, one launch (start us, length us, event | category | flops | bytes accessed | tf_op | source)
XLA Modules:
  0.0 121.3 jit_solution(14584205865628620720)
XLA Ops:
  0.0 0.0 copy-start.1
  0.0 0.8 copy.16
  0.8 0.1 reshape.125
  0.9 0.2 convert_reduce_fusion
  1.1 0.0 copy-start.2
  1.1 0.1 select_reduce_fusion
  1.2 1.2 %gather_fusion = s32[128]{0:T(128)S(1)} fusion(s32[128]{0:T(128)S(1)} %get-tuple-element.9, s32[1024]{0:T(1024)S(1)} %pad_clamp_fusion), kind=kCustom, calls=%fused_computation | custom fusion | bytes 1536 | tf_op jit(solution)/shard_map/gather | solution.py:148
  2.5 0.7 all_to_all.12
  3.2 13.0 %all-to-all-start = ((s32[32,1,4]{2,1,0:T(1,128)}), s32[32,1,4]{2,1,0:T(1,128)S(1)}, u32[]{:S(2)}, u32[]{:S(2)}) async-start(s32[32,1,4]{2,1,0:T(1,128)} %bitcast.2), calls=%async_computation | async-start | bytes 32768 | tf_op jit(solution)/shard_map/all_to_all | solution.py:149
  16.2 1.0 add_convert_fusion
  17.2 0.8 stack.19
  18.0 0.3 copy.19
  18.3 0.0 copy-done.1
  18.3 0.8 stack.18
  19.2 0.0 copy-done.2
  19.2 0.3 copy.18
  19.5 0.1 rev.6
  19.7 0.2 copy.22
  19.9 4.1 %all-to-all-done = s32[32,1,4]{2,1,0:T(1,128)S(1)} async-done(((s32[32,1,4]{2,1,0:T(1,128)}), s32[32,1,4]{2,1,0:T(1,128)S(1)}, u32[]{:S(2)}, u32[]{:S(2)}) %all-to-all-start) | async-done | bytes 544 | tf_op jit(solution)/shard_map/all_to_all | solution.py:149
  23.9 0.5 broadcast.142
  24.5 0.7 reduce.3
  25.1 0.1 eq.46
  25.2 0.7 convolution_convert_fusion
  26.0 2.0 %copy.23 = bf16[16,8,32,256]{3,2,1,0:T(8,128)(2,1)} copy(bf16[16,8,32,256]{3,1,2,0:T(8,128)(2,1)S(1)} %bitcast.25) | data formatting | bytes 4194304
  28.0 4.4 %all-to-all-start.1 = ((bf16[32,4,2,16,256]{4,3,2,1,0:T(8,128)(2,1)}), bf16[32,4,2,16,256]{4,3,2,1,0:T(8,128)(2,1)S(1)}, u32[]{:S(2)}, u32[]{:S(2)}) async-start(bf16[32,4,2,16,256]{4,3,2,1,0:T(8,128)(2,1)} %bitcast.26), calls=%async_computation.1 | async-start | bytes 4194304 | tf_op jit(solution)/shard_map/all_to_all | solution.py:154
  32.4 3.1 %collective-permute-start.1 = (bf16[16,256]{1,0:T(8,128)(2,1)S(1)}, bf16[16,256]{1,0:T(8,128)(2,1)S(1)}, u32[]{:S(2)}, u32[]{:S(2)}) collective-permute-start(bf16[16,256]{1,0:T(8,128)(2,1)S(1)} %slice.32), channel_id=1, source_target_pairs={{0,1},{1,2},{2,3},{3,4},{4,5},{5,6},{6,7},{7,8},{8,9},{9,10},{10,1... | collective-permute-start | bytes 24584 | tf_op jit(solution)/shard_map/ppermute | solution.py:16
  35.5 1.3 %collective-permute-start = (bf16[16,256]{1,0:T(8,128)(2,1)S(1)}, bf16[16,256]{1,0:T(8,128)(2,1)S(1)}, u32[]{:S(2)}, u32[]{:S(2)}) collective-permute-start(bf16[16,256]{1,0:T(8,128)(2,1)S(1)} %slice.23), channel_id=1, source_target_pairs={{1,0},{2,1},{3,2},{4,3},{5,4},{6,5},{7,6},{8,7},{9,8},{10,9},{11,1... | collective-permute-start | bytes 24584 | tf_op jit(solution)/shard_map/ppermute | solution.py:16
  36.8 0.0 collective-permute-done.1
  36.9 0.1 slice.33
  36.9 0.2 concatenate.16
  37.1 0.8 stack.22
  37.9 1.1 copy.21
  39.1 1.2 collective-permute-done
  40.2 0.9 maximum_maximum_fusion
  41.1 0.8 stack.21
  42.0 1.1 copy.20
  43.1 1.1 maximum_bitcast_fusion
  44.2 0.2 rev.7
  44.4 0.9 fusion.2.phased_ref
  45.3 11.0 %shard_map.46.refs_8_ = bf16[16,2,256,384]{3,2,1,0:T(8,128)(2,1)} custom-call(bf16[16,2,16,384]{3,2,1,0:T(8,128)(2,1)} %fusion.2.phased_ref), custom_call_target="tpu_custom_call" | custom-call | tf_op jit(solution)/shard_map/pallas_call | solution.py:57
  56.3 28.2 %all-to-all-done.1 = bf16[32,4,2,16,256]{4,3,2,1,0:T(8,128)(2,1)S(1)} async-done(((bf16[32,4,2,16,256]{4,3,2,1,0:T(8,128)(2,1)}), bf16[32,4,2,16,256]{4,3,2,1,0:T(8,128)(2,1)S(1)}, u32[]{:S(2)}, u32[]{:S(2)}) %all-to-all-start.1) | async-done | bytes 2097184 | tf_op jit(solution)/shard_map/all_to_all | solution.py:154
  84.5 0.0 copy-start
  84.5 1.3 %copy-done = bf16[32,4,2,16,256]{4,3,2,1,0:T(8,128)(2,1)} copy-done((bf16[32,4,2,16,256]{4,3,2,1,0:T(8,128)(2,1)}, bf16[32,4,2,16,256]{4,3,2,1,0:T(8,128)(2,1)S(1)}, u32[]{:S(2)}) %copy-start) | copy-done | bytes 2097176
  85.9 0.0 copy-start.3
  85.9 14.3 %shard_map.47 = f32[16,2,16,128]{3,2,1,0:T(8,128)} custom-call(s32[128]{0:T(128)} %copy-done.2, bf16[128,2,16,256]{3,2,1,0:T(8,128)(2,1)} %bitcast.17, bf16[128,2,16,256]{3,2,1,0:T(8,128)(2,1)} %bitcast.18, bf16[128,2,16,256]{3,2,1,0:T(8,128)(2,1)} %bitcast.19, bf16[128,2,16,256]{3,2,1,0:T(8,128)(2,1)} %bitcast.20, bf16[128,2,16,256]{3,2,1,0:T(8,128)(2,1)} %bitcast.21, ...), custom_call_target="tpu_custom_call" | custom-call | tf_op jit(solution)/shard_map/pallas_call | solution.py:115
  100.2 8.4 %all-to-all-start.2 = ((f32[16,2,16,128]{3,2,1,0:T(8,128)}), f32[16,2,16,128]{3,2,1,0:T(8,128)S(1)}, u32[]{:S(2)}, u32[]{:S(2)}) async-start(f32[16,2,16,128]{3,2,1,0:T(8,128)} %shard_map.47), calls=%async_computation.2 | async-start | bytes 524288 | tf_op jit(solution)/shard_map/all_to_all | solution.py:158
  108.6 0.0 copy-done.3
  108.6 0.1 fusion.5
  108.7 0.1 reshape.128
  108.8 11.9 %all-to-all-done.2 = f32[16,2,16,128]{3,2,1,0:T(8,128)S(1)} async-done(((f32[16,2,16,128]{3,2,1,0:T(8,128)}), f32[16,2,16,128]{3,2,1,0:T(8,128)S(1)}, u32[]{:S(2)}, u32[]{:S(2)}) %all-to-all-start.2) | async-done | bytes 262176 | tf_op jit(solution)/shard_map/all_to_all | solution.py:158
  120.7 0.6 multiply_multiply_fusion
  (14 shorter events, 0.2 us)
Async XLA Ops:
  0.0 18.3 %copy-start.1 = (bf16[16,4096]{1,0:T(8,128)(2,1)S(1)}, bf16[16,4096]{1,0:T(8,128)(2,1)}, u32[]{:S(2)}) copy-start(bf16[16,4096]{1,0:T(8,128)(2,1)} %param.4) | copy-start | bytes 393220
  1.1 18.1 %copy-start.2 = (s32[128]{0:T(128)}, s32[128]{0:T(128)S(1)}, u32[]{:S(2)}) copy-start(s32[128]{0:T(128)S(1)} %multiply_add_fusion.slot_ref) | copy-start | bytes 1540
  3.2 20.8 %all-to-all-start = ((s32[32,1,4]{2,1,0:T(1,128)}), s32[32,1,4]{2,1,0:T(1,128)S(1)}, u32[]{:S(2)}, u32[]{:S(2)}) async-start(s32[32,1,4]{2,1,0:T(1,128)} %bitcast.2), calls=%async_computation | async-start | bytes 32768 | tf_op jit(solution)/shard_map/all_to_all | solution.py:149
  28.0 56.6 %all-to-all-start.1 = ((bf16[32,4,2,16,256]{4,3,2,1,0:T(8,128)(2,1)}), bf16[32,4,2,16,256]{4,3,2,1,0:T(8,128)(2,1)S(1)}, u32[]{:S(2)}, u32[]{:S(2)}) async-start(bf16[32,4,2,16,256]{4,3,2,1,0:T(8,128)(2,1)} %bitcast.26), calls=%async_computation.1 | async-start | bytes 4194304 | tf_op jit(solution)/shard_map/all_to_all | solution.py:154
  32.4 4.5 %collective-permute-start.1 = (bf16[16,256]{1,0:T(8,128)(2,1)S(1)}, bf16[16,256]{1,0:T(8,128)(2,1)S(1)}, u32[]{:S(2)}, u32[]{:S(2)}) collective-permute-start(bf16[16,256]{1,0:T(8,128)(2,1)S(1)} %slice.32), channel_id=1, source_target_pairs={{0,1},{1,2},{2,3},{3,4},{4,5},{5,6},{6,7},{7,8},{8,9},{9,10},{10,1... | collective-permute-start | bytes 24584 | tf_op jit(solution)/shard_map/ppermute | solution.py:16
  35.5 4.7 %collective-permute-start = (bf16[16,256]{1,0:T(8,128)(2,1)S(1)}, bf16[16,256]{1,0:T(8,128)(2,1)S(1)}, u32[]{:S(2)}, u32[]{:S(2)}) collective-permute-start(bf16[16,256]{1,0:T(8,128)(2,1)S(1)} %slice.23), channel_id=1, source_target_pairs={{1,0},{2,1},{3,2},{4,3},{5,4},{6,5},{7,6},{8,7},{9,8},{10,9},{11,1... | collective-permute-start | bytes 24584 | tf_op jit(solution)/shard_map/ppermute | solution.py:16
  84.5 1.3 %copy-start = (bf16[32,4,2,16,256]{4,3,2,1,0:T(8,128)(2,1)}, bf16[32,4,2,16,256]{4,3,2,1,0:T(8,128)(2,1)S(1)}, u32[]{:S(2)}) copy-start(bf16[32,4,2,16,256]{4,3,2,1,0:T(8,128)(2,1)S(1)} %all-to-all-done.1) | copy-start | bytes 6291460
  85.9 22.7 %copy-start.3 = (s32[16]{0:T(128)S(1)}, s32[16]{0:T(128)}, u32[]{:S(2)}) copy-start(s32[16]{0:T(128)} %param.7) | copy-start | bytes 196
  100.2 20.4 %all-to-all-start.2 = ((f32[16,2,16,128]{3,2,1,0:T(8,128)}), f32[16,2,16,128]{3,2,1,0:T(8,128)S(1)}, u32[]{:S(2)}, u32[]{:S(2)}) async-start(f32[16,2,16,128]{3,2,1,0:T(8,128)} %shard_map.47), calls=%async_computation.2 | async-start | bytes 524288 | tf_op jit(solution)/shard_map/all_to_all | solution.py:158

commit v5 on v4

--- a/solution.py
+++ b/solution.py
@@ -1,3 +1,5 @@
+import functools
+
 import jax
 import jax.numpy as jnp
 from jax import lax
@@ -63,16 +65,12 @@
     )(phased)
 
 
-def lane_kernel(slot_ref, *refs):
-    del slot_ref
-    acc_ref = refs[-1]
-    out_ref = refs[-2]
-    win_ref = refs[-3]
-    row_refs = refs[:-3]
-    slots = len(row_refs)
+def lane_kernel(slots, slot_ref, got_ref, win_ref, out_ref, acc_ref):
     lane = pl.program_id(0)
     for d in range(2):
-        lhs = jnp.concatenate([ref[0, 1 - d] for ref in row_refs], axis=0)
+        lhs = jnp.concatenate(
+            [got_ref[slot_ref[lane * slots + s], 1 - d] for s in range(slots)], axis=0
+        )
         cross = lax.dot_general(
             lhs, win_ref[0, d], (((1,), (0,)), ((), ())), preferred_element_type=jnp.float32
         )
@@ -99,24 +97,23 @@
     blocks = got.shape[3]
     lag_dev = LAGS // rec_count
 
-    def row_spec(s):
-        return pl.BlockSpec((1, 2, PHASE, blocks), lambda l, slot: (slot[l * slots + s], 0, 0, 0))
-
     grid_spec = pltpu.PrefetchScalarGridSpec(
         num_scalar_prefetch=1,
         grid=(lanes,),
-        in_specs=[row_spec(s) for s in range(slots)]
-        + [pl.BlockSpec((1, 2, blocks, WIDE), lambda l, slot: (l, 0, 0, 0))],
+        in_specs=[
+            pl.BlockSpec(got.shape, lambda l, slot: (0, 0, 0, 0)),
+            pl.BlockSpec((1, 2, blocks, WIDE), lambda l, slot: (l, 0, 0, 0)),
+        ],
         out_specs=pl.BlockSpec((rec_count, 2, lag_dev, pairs), lambda l, slot: (0, 0, 0, 0)),
         scratch_shapes=[
             pltpu.VMEM((2, pairs, LAGS), jnp.float32),
         ],
     )
     return pl.pallas_call(
-        lane_kernel,
+        functools.partial(lane_kernel, slots),
         grid_spec=grid_spec,
         out_shape=jax.ShapeDtypeStruct((rec_count, 2, lag_dev, pairs), jnp.float32),
-    )(slot_of, *([got] * slots), wins)
+    )(slot_of, got, wins)
 
 
 def per_device(waveforms, patterns, partners, counts):

time: 123 us -> 122 us (level)
  no operation moved by 1% of the time
where the time goes in v5:
time: 122 us; the launch traced here: 121 us
  waiting for transfers between devices  45.3 us (37%)
  starting transfers between devices  30.2 us (25%)
  Pallas kernels  24.6 us (20%)
  local copies, waits for them, and re-layouts  13.8 us (11%)
  other arithmetic  5.62 us (5%)
    all_to_all x1, waiting for transfers between devices, per_device(): got = lax.all_to_all(reply, 'lane', split_axis=0, concat_axis=0, tiled=True)  28.2 us
    pallas_call x1, Pallas kernels, correlate(): pl.pallas_call(functools.partial(lane_kernel, slots), grid_spec=grid_spec...  13.6 us
    all_to_all x1, starting transfers between devices, per_device(): lax.all_to_all(send_index, 'lane', split_axis=0, concat_axis=0, tiled=True)  13 us
    all_to_all x1, waiting for transfers between devices, per_device(): lax.all_to_all(terms, 'rec', split_axis=0, concat_axis=0, tiled=True)  11.9 us
    pallas_call x1, Pallas kernels, windows(): pl.pallas_call(window_kernel, grid=(lanes,), in_specs=[pl.BlockSpec((1, 2...  11 us
    all_to_all x1, starting transfers between devices, per_device(): lax.all_to_all(terms, 'rec', split_axis=0, concat_axis=0, tiled=True)  8.4 us
    all_to_all x1, starting transfers between devices, per_device(): got = lax.all_to_all(reply, 'lane', split_axis=0, concat_axis=0, tiled=True)  4.41 us
    ppermute x2, starting transfers between devices, passed_along(): return lax.ppermute(block, axis, route)  4.41 us
  transfers between devices with their start and end apart: 5, of which 4 were waited for; matrix products, arithmetic and copies ran while one was open for 9% of the time, Pallas kernels for 9%

profile of v5, /device:TPU:1, one launch (start us, length us, event | category | flops | bytes accessed | tf_op | source)
XLA Modules:
  0.0 120.6 jit_solution(12626869586100579950)
XLA Ops:
  0.0 0.0 copy-start.1
  0.0 0.8 copy.16
  0.8 0.1 reshape.125
  0.9 0.2 convert_reduce_fusion
  1.1 0.0 copy-start.2
  1.1 0.1 select_reduce_fusion
  1.2 1.2 %gather_fusion = s32[128]{0:T(128)S(1)} fusion(s32[128]{0:T(128)S(1)} %get-tuple-element.9, s32[1024]{0:T(1024)S(1)} %pad_clamp_fusion), kind=kCustom, calls=%fused_computation | custom fusion | bytes 1536 | tf_op jit(solution)/shard_map/gather | solution.py:145
  2.5 0.7 all_to_all.12
  3.2 13.0 %all-to-all-start = ((s32[32,1,4]{2,1,0:T(1,128)}), s32[32,1,4]{2,1,0:T(1,128)S(1)}, u32[]{:S(2)}, u32[]{:S(2)}) async-start(s32[32,1,4]{2,1,0:T(1,128)} %bitcast.2), calls=%async_computation | async-start | bytes 32768 | tf_op jit(solution)/shard_map/all_to_all | solution.py:146
  16.2 1.0 add_convert_fusion
  17.2 0.8 stack.19
  18.0 0.3 copy.19
  18.3 0.0 copy-done.1
  18.3 0.8 stack.18
  19.2 0.0 copy-done.2
  19.2 0.3 copy.18
  19.5 0.1 rev.6
  19.7 0.2 copy.22
  19.9 4.1 %all-to-all-done = s32[32,1,4]{2,1,0:T(1,128)S(1)} async-done(((s32[32,1,4]{2,1,0:T(1,128)}), s32[32,1,4]{2,1,0:T(1,128)S(1)}, u32[]{:S(2)}, u32[]{:S(2)}) %all-to-all-start) | async-done | bytes 544 | tf_op jit(solution)/shard_map/all_to_all | solution.py:146
  23.9 0.5 broadcast.142
  24.5 0.7 reduce.3
  25.1 0.1 eq.46
  25.2 0.7 convolution_convert_fusion
  26.0 2.0 %copy.23 = bf16[16,8,32,256]{3,2,1,0:T(8,128)(2,1)} copy(bf16[16,8,32,256]{3,1,2,0:T(8,128)(2,1)S(1)} %bitcast.18) | data formatting | bytes 4194304
  28.0 4.4 %all-to-all-start.1 = ((bf16[32,4,2,16,256]{4,3,2,1,0:T(8,128)(2,1)}), bf16[32,4,2,16,256]{4,3,2,1,0:T(8,128)(2,1)S(1)}, u32[]{:S(2)}, u32[]{:S(2)}) async-start(bf16[32,4,2,16,256]{4,3,2,1,0:T(8,128)(2,1)} %bitcast.19), calls=%async_computation.1 | async-start | bytes 4194304 | tf_op jit(solution)/shard_map/all_to_all | solution.py:151
  32.4 3.1 %collective-permute-start.1 = (bf16[16,256]{1,0:T(8,128)(2,1)S(1)}, bf16[16,256]{1,0:T(8,128)(2,1)S(1)}, u32[]{:S(2)}, u32[]{:S(2)}) collective-permute-start(bf16[16,256]{1,0:T(8,128)(2,1)S(1)} %slice.32), channel_id=1, source_target_pairs={{0,1},{1,2},{2,3},{3,4},{4,5},{5,6},{6,7},{7,8},{8,9},{9,10},{10,1... | collective-permute-start | bytes 24584 | tf_op jit(solution)/shard_map/ppermute | solution.py:18
  35.5 1.3 %collective-permute-start = (bf16[16,256]{1,0:T(8,128)(2,1)S(1)}, bf16[16,256]{1,0:T(8,128)(2,1)S(1)}, u32[]{:S(2)}, u32[]{:S(2)}) collective-permute-start(bf16[16,256]{1,0:T(8,128)(2,1)S(1)} %slice.23), channel_id=1, source_target_pairs={{1,0},{2,1},{3,2},{4,3},{5,4},{6,5},{7,6},{8,7},{9,8},{10,9},{11,1... | collective-permute-start | bytes 24584 | tf_op jit(solution)/shard_map/ppermute | solution.py:18
  36.8 0.0 collective-permute-done.1
  36.9 0.1 slice.33
  36.9 0.2 concatenate.16
  37.1 0.8 stack.22
  37.9 1.1 copy.21
  39.1 1.2 collective-permute-done
  40.2 0.9 maximum_maximum_fusion
  41.1 0.8 stack.21
  42.0 1.1 copy.20
  43.1 1.1 maximum_bitcast_fusion
  44.2 0.2 rev.7
  44.4 0.9 fusion.2.phased_ref
  45.3 11.0 %shard_map.46.win_ref = bf16[16,2,256,384]{3,2,1,0:T(8,128)(2,1)} custom-call(bf16[16,2,16,384]{3,2,1,0:T(8,128)(2,1)} %fusion.2.phased_ref), custom_call_target="tpu_custom_call" | custom-call | tf_op jit(solution)/shard_map/pallas_call | solution.py:59
  56.3 28.2 %all-to-all-done.1 = bf16[32,4,2,16,256]{4,3,2,1,0:T(8,128)(2,1)S(1)} async-done(((bf16[32,4,2,16,256]{4,3,2,1,0:T(8,128)(2,1)}), bf16[32,4,2,16,256]{4,3,2,1,0:T(8,128)(2,1)S(1)}, u32[]{:S(2)}, u32[]{:S(2)}) %all-to-all-start.1) | async-done | bytes 2097184 | tf_op jit(solution)/shard_map/all_to_all | solution.py:151
  84.5 0.0 copy-start
  84.5 1.3 %copy-done = bf16[32,4,2,16,256]{4,3,2,1,0:T(8,128)(2,1)} copy-done((bf16[32,4,2,16,256]{4,3,2,1,0:T(8,128)(2,1)}, bf16[32,4,2,16,256]{4,3,2,1,0:T(8,128)(2,1)S(1)}, u32[]{:S(2)}) %copy-start) | copy-done | bytes 2097176
  85.9 0.0 copy-start.3
  85.9 13.6 %shard_map.47 = f32[16,2,16,128]{3,2,1,0:T(8,128)} custom-call(s32[128]{0:T(128)} %copy-done.2, bf16[128,2,16,256]{3,2,1,0:T(8,128)(2,1)} %bitcast.17, bf16[16,2,256,384]{3,2,1,0:T(8,128)(2,1)} %shard_map.46.win_ref), custom_call_target="tpu_custom_call" | custom-call | tf_op jit(solution)/shard_map/pallas_call | solution.py:112
  99.5 8.4 %all-to-all-start.2 = ((f32[16,2,16,128]{3,2,1,0:T(8,128)}), f32[16,2,16,128]{3,2,1,0:T(8,128)S(1)}, u32[]{:S(2)}, u32[]{:S(2)}) async-start(f32[16,2,16,128]{3,2,1,0:T(8,128)} %shard_map.47), calls=%async_computation.2 | async-start | bytes 524288 | tf_op jit(solution)/shard_map/all_to_all | solution.py:155
  107.9 0.0 copy-done.3
  107.9 0.1 fusion.5
  108.0 0.1 reshape.128
  108.1 11.9 %all-to-all-done.2 = f32[16,2,16,128]{3,2,1,0:T(8,128)S(1)} async-done(((f32[16,2,16,128]{3,2,1,0:T(8,128)}), f32[16,2,16,128]{3,2,1,0:T(8,128)S(1)}, u32[]{:S(2)}, u32[]{:S(2)}) %all-to-all-start.2) | async-done | bytes 262176 | tf_op jit(solution)/shard_map/all_to_all | solution.py:155
  120.0 0.6 multiply_multiply_fusion
  (14 shorter events, 0.2 us)
Async XLA Ops:
  0.0 18.3 %copy-start.1 = (bf16[16,4096]{1,0:T(8,128)(2,1)S(1)}, bf16[16,4096]{1,0:T(8,128)(2,1)}, u32[]{:S(2)}) copy-start(bf16[16,4096]{1,0:T(8,128)(2,1)} %param.4) | copy-start | bytes 393220
  1.1 18.1 %copy-start.2 = (s32[128]{0:T(128)}, s32[128]{0:T(128)S(1)}, u32[]{:S(2)}) copy-start(s32[128]{0:T(128)S(1)} %multiply_add_fusion.slot_ref) | copy-start | bytes 1540
  3.2 20.8 %all-to-all-start = ((s32[32,1,4]{2,1,0:T(1,128)}), s32[32,1,4]{2,1,0:T(1,128)S(1)}, u32[]{:S(2)}, u32[]{:S(2)}) async-start(s32[32,1,4]{2,1,0:T(1,128)} %bitcast.2), calls=%async_computation | async-start | bytes 32768 | tf_op jit(solution)/shard_map/all_to_all | solution.py:146
  28.0 56.6 %all-to-all-start.1 = ((bf16[32,4,2,16,256]{4,3,2,1,0:T(8,128)(2,1)}), bf16[32,4,2,16,256]{4,3,2,1,0:T(8,128)(2,1)S(1)}, u32[]{:S(2)}, u32[]{:S(2)}) async-start(bf16[32,4,2,16,256]{4,3,2,1,0:T(8,128)(2,1)} %bitcast.19), calls=%async_computation.1 | async-start | bytes 4194304 | tf_op jit(solution)/shard_map/all_to_all | solution.py:151
  32.4 4.5 %collective-permute-start.1 = (bf16[16,256]{1,0:T(8,128)(2,1)S(1)}, bf16[16,256]{1,0:T(8,128)(2,1)S(1)}, u32[]{:S(2)}, u32[]{:S(2)}) collective-permute-start(bf16[16,256]{1,0:T(8,128)(2,1)S(1)} %slice.32), channel_id=1, source_target_pairs={{0,1},{1,2},{2,3},{3,4},{4,5},{5,6},{6,7},{7,8},{8,9},{9,10},{10,1... | collective-permute-start | bytes 24584 | tf_op jit(solution)/shard_map/ppermute | solution.py:18
  35.5 4.7 %collective-permute-start = (bf16[16,256]{1,0:T(8,128)(2,1)S(1)}, bf16[16,256]{1,0:T(8,128)(2,1)S(1)}, u32[]{:S(2)}, u32[]{:S(2)}) collective-permute-start(bf16[16,256]{1,0:T(8,128)(2,1)S(1)} %slice.23), channel_id=1, source_target_pairs={{1,0},{2,1},{3,2},{4,3},{5,4},{6,5},{7,6},{8,7},{9,8},{10,9},{11,1... | collective-permute-start | bytes 24584 | tf_op jit(solution)/shard_map/ppermute | solution.py:18
  84.5 1.3 %copy-start = (bf16[32,4,2,16,256]{4,3,2,1,0:T(8,128)(2,1)}, bf16[32,4,2,16,256]{4,3,2,1,0:T(8,128)(2,1)S(1)}, u32[]{:S(2)}) copy-start(bf16[32,4,2,16,256]{4,3,2,1,0:T(8,128)(2,1)S(1)} %all-to-all-done.1) | copy-start | bytes 6291460
  85.9 22.0 %copy-start.3 = (s32[16]{0:T(128)S(1)}, s32[16]{0:T(128)}, u32[]{:S(2)}) copy-start(s32[16]{0:T(128)} %param.7) | copy-start | bytes 196
  99.5 20.4 %all-to-all-start.2 = ((f32[16,2,16,128]{3,2,1,0:T(8,128)}), f32[16,2,16,128]{3,2,1,0:T(8,128)S(1)}, u32[]{:S(2)}, u32[]{:S(2)}) async-start(f32[16,2,16,128]{3,2,1,0:T(8,128)} %shard_map.47), calls=%async_computation.2 | async-start | bytes 524288 | tf_op jit(solution)/shard_map/all_to_all | solution.py:155

commit v6 on v5

--- a/solution.py
+++ b/solution.py
@@ -1,3 +1,4 @@
+import math
 import functools
 
 import jax
@@ -65,25 +66,27 @@
     )(phased)
 
 
-def lane_kernel(slots, slot_ref, got_ref, win_ref, out_ref, acc_ref):
-    lane = pl.program_id(0)
-    for d in range(2):
-        lhs = jnp.concatenate(
-            [got_ref[slot_ref[lane * slots + s], 1 - d] for s in range(slots)], axis=0
-        )
-        cross = lax.dot_general(
-            lhs, win_ref[0, d], (((1,), (0,)), ((), ())), preferred_element_type=jnp.float32
-        )
-        base = WIDE - (PHASE - 1) if d == 0 else LAGS
-        sums = []
-        for s in range(slots):
-            block = cross[s * PHASE : (s + 1) * PHASE, :]
-            lined = pltpu.roll(block, base, 1, stride=1, stride_axis=0)
-            sums.append(jnp.sum(lined, axis=0, keepdims=True))
-        total = jnp.concatenate(sums, axis=0)[:, :LAGS]
-        acc_ref[d, pl.ds(pl.multiple_of(lane * slots, slots), slots), :] = total
+def lane_kernel(slots, group, slot_ref, got_ref, win_ref, out_ref, acc_ref):
+    step_id = pl.program_id(0)
+    for g in range(group):
+        lane = step_id * group + g
+        for d in range(2):
+            lhs = jnp.concatenate(
+                [got_ref[slot_ref[lane * slots + s], 1 - d] for s in range(slots)], axis=0
+            )
+            cross = lax.dot_general(
+                lhs, win_ref[g, d], (((1,), (0,)), ((), ())), preferred_element_type=jnp.float32
+            )
+            base = WIDE - (PHASE - 1) if d == 0 else LAGS
+            sums = []
+            for s in range(slots):
+                block = cross[s * PHASE : (s + 1) * PHASE, :]
+                lined = pltpu.roll(block, base, 1, stride=1, stride_axis=0)
+                sums.append(jnp.sum(lined, axis=0, keepdims=True))
+            total = jnp.concatenate(sums, axis=0)[:, :LAGS]
+            acc_ref[d, pl.ds(pl.multiple_of(lane * slots, slots), slots), :] = total
 
-    @pl.when(lane == pl.num_programs(0) - 1)
+    @pl.when(step_id == pl.num_programs(0) - 1)
     def _():
         for d in range(2):
             flipped = acc_ref[d].T
@@ -96,13 +99,14 @@
     slots = pairs // lanes
     blocks = got.shape[3]
     lag_dev = LAGS // rec_count
+    group = math.gcd(lanes, 4)
 
     grid_spec = pltpu.PrefetchScalarGridSpec(
         num_scalar_prefetch=1,
-        grid=(lanes,),
+        grid=(lanes // group,),
         in_specs=[
             pl.BlockSpec(got.shape, lambda l, slot: (0, 0, 0, 0)),
-            pl.BlockSpec((1, 2, blocks, WIDE), lambda l, slot: (l, 0, 0, 0)),
+            pl.BlockSpec((group, 2, blocks, WIDE), lambda l, slot: (l, 0, 0, 0)),
         ],
         out_specs=pl.BlockSpec((rec_count, 2, lag_dev, pairs), lambda l, slot: (0, 0, 0, 0)),
         scratch_shapes=[
@@ -110,7 +114,7 @@
         ],
     )
     return pl.pallas_call(
-        functools.partial(lane_kernel, slots),
+        functools.partial(lane_kernel, slots, group),
         grid_spec=grid_spec,
         out_shape=jax.ShapeDtypeStruct((rec_count, 2, lag_dev, pairs), jnp.float32),
     )(slot_of, got, wins)

time: 122 us -> 116 us (0.951)
  Pallas kernels: 24.6 us -> 18.2 us
    pallas_call x1, Pallas kernels: 13.6 us -> 7.23 us  [correlate(): pl.pallas_call(functools.partial(lane_kernel, slots, group), grid_spec=gr...]
  transfers between devices with their start and end apart: 5 -> 5, of which waited for: 4 -> 4; matrix products, arithmetic and copies ran while one was open for 9% -> 10% of each run, Pallas kernels for 9% -> 10%
where the time goes in v6:
time: 116 us; the launch traced here: 114 us
  waiting for transfers between devices  45.3 us (39%)
  starting transfers between devices  30.2 us (26%)
  Pallas kernels  18.2 us (16%)
  local copies, waits for them, and re-layouts  13.8 us (12%)
  other arithmetic  5.62 us (5%)
    all_to_all x1, waiting for transfers between devices, per_device(): got = lax.all_to_all(reply, 'lane', split_axis=0, concat_axis=0, tiled=True)  28.2 us
    all_to_all x1, starting transfers between devices, per_device(): lax.all_to_all(send_index, 'lane', split_axis=0, concat_axis=0, tiled=True)  13 us
    all_to_all x1, waiting for transfers between devices, per_device(): lax.all_to_all(terms, 'rec', split_axis=0, concat_axis=0, tiled=True)  11.9 us
    pallas_call x1, Pallas kernels, windows(): pl.pallas_call(window_kernel, grid=(lanes,), in_specs=[pl.BlockSpec((1, 2...  11 us
    all_to_all x1, starting transfers between devices, per_device(): lax.all_to_all(terms, 'rec', split_axis=0, concat_axis=0, tiled=True)  8.41 us
    pallas_call x1, Pallas kernels, correlate(): pl.pallas_call(functools.partial(lane_kernel, slots, group), grid_spec=gr...  7.23 us
    all_to_all x1, starting transfers between devices, per_device(): got = lax.all_to_all(reply, 'lane', split_axis=0, concat_axis=0, tiled=True)  4.41 us
    ppermute x2, starting transfers between devices, passed_along(): return lax.ppermute(block, axis, route)  4.41 us
  transfers between devices with their start and end apart: 5, of which 4 were waited for; matrix products, arithmetic and copies ran while one was open for 10% of the time, Pallas kernels for 10%

profile of v6, /device:TPU:1, one launch (start us, length us, event | category | flops | bytes accessed | tf_op | source)
XLA Modules:
  0.0 114.2 jit_solution(8616539979857697777)
XLA Ops:
  0.0 0.0 copy-start.1
  0.0 0.8 copy.16
  0.8 0.1 reshape.125
  0.9 0.2 convert_reduce_fusion
  1.1 0.0 copy-start.2
  1.1 0.1 select_reduce_fusion
  1.2 1.2 %gather_fusion = s32[128]{0:T(128)S(1)} fusion(s32[128]{0:T(128)S(1)} %get-tuple-element.9, s32[1024]{0:T(1024)S(1)} %pad_clamp_fusion), kind=kCustom, calls=%fused_computation | custom fusion | bytes 1536 | tf_op jit(solution)/shard_map/gather | solution.py:149
  2.5 0.7 all_to_all.12
  3.2 13.0 %all-to-all-start = ((s32[32,1,4]{2,1,0:T(1,128)}), s32[32,1,4]{2,1,0:T(1,128)S(1)}, u32[]{:S(2)}, u32[]{:S(2)}) async-start(s32[32,1,4]{2,1,0:T(1,128)} %bitcast.2), calls=%async_computation | async-start | bytes 32768 | tf_op jit(solution)/shard_map/all_to_all | solution.py:150
  16.2 1.0 add_convert_fusion
  17.2 0.8 stack.19
  18.0 0.3 copy.19
  18.3 0.0 copy-done.1
  18.3 0.8 stack.18
  19.2 0.0 copy-done.2
  19.2 0.3 copy.18
  19.5 0.1 rev.6
  19.7 0.2 copy.22
  19.9 4.1 %all-to-all-done = s32[32,1,4]{2,1,0:T(1,128)S(1)} async-done(((s32[32,1,4]{2,1,0:T(1,128)}), s32[32,1,4]{2,1,0:T(1,128)S(1)}, u32[]{:S(2)}, u32[]{:S(2)}) %all-to-all-start) | async-done | bytes 544 | tf_op jit(solution)/shard_map/all_to_all | solution.py:150
  23.9 0.5 broadcast.142
  24.5 0.7 reduce.3
  25.1 0.1 eq.46
  25.2 0.7 convolution_convert_fusion
  26.0 2.0 %copy.23 = bf16[16,8,32,256]{3,2,1,0:T(8,128)(2,1)} copy(bf16[16,8,32,256]{3,1,2,0:T(8,128)(2,1)S(1)} %bitcast.18) | data formatting | bytes 4194304
  28.0 4.4 %all-to-all-start.1 = ((bf16[32,4,2,16,256]{4,3,2,1,0:T(8,128)(2,1)}), bf16[32,4,2,16,256]{4,3,2,1,0:T(8,128)(2,1)S(1)}, u32[]{:S(2)}, u32[]{:S(2)}) async-start(bf16[32,4,2,16,256]{4,3,2,1,0:T(8,128)(2,1)} %bitcast.19), calls=%async_computation.1 | async-start | bytes 4194304 | tf_op jit(solution)/shard_map/all_to_all | solution.py:155
  32.4 3.1 %collective-permute-start.1 = (bf16[16,256]{1,0:T(8,128)(2,1)S(1)}, bf16[16,256]{1,0:T(8,128)(2,1)S(1)}, u32[]{:S(2)}, u32[]{:S(2)}) collective-permute-start(bf16[16,256]{1,0:T(8,128)(2,1)S(1)} %slice.32), channel_id=1, source_target_pairs={{0,1},{1,2},{2,3},{3,4},{4,5},{5,6},{6,7},{7,8},{8,9},{9,10},{10,1... | collective-permute-start | bytes 24584 | tf_op jit(solution)/shard_map/ppermute | solution.py:19
  35.5 1.3 %collective-permute-start = (bf16[16,256]{1,0:T(8,128)(2,1)S(1)}, bf16[16,256]{1,0:T(8,128)(2,1)S(1)}, u32[]{:S(2)}, u32[]{:S(2)}) collective-permute-start(bf16[16,256]{1,0:T(8,128)(2,1)S(1)} %slice.23), channel_id=1, source_target_pairs={{1,0},{2,1},{3,2},{4,3},{5,4},{6,5},{7,6},{8,7},{9,8},{10,9},{11,1... | collective-permute-start | bytes 24584 | tf_op jit(solution)/shard_map/ppermute | solution.py:19
  36.8 0.0 collective-permute-done.1
  36.9 0.1 slice.33
  36.9 0.2 concatenate.16
  37.1 0.8 stack.22
  37.9 1.1 copy.21
  39.1 1.2 %collective-permute-done = bf16[16,256]{1,0:T(8,128)(2,1)S(1)} collective-permute-done((bf16[16,256]{1,0:T(8,128)(2,1)S(1)}, bf16[16,256]{1,0:T(8,128)(2,1)S(1)}, u32[]{:S(2)}, u32[]{:S(2)}) %collective-permute-start) | collective-permute-done | bytes 8224 | tf_op jit(solution)/shard_map/ppermute | solution.py:19
  40.2 0.9 maximum_maximum_fusion
  41.1 0.8 stack.21
  42.0 1.1 copy.20
  43.1 1.1 maximum_bitcast_fusion
  44.2 0.2 rev.7
  44.4 0.9 fusion.2.phased_ref
  45.3 11.0 %shard_map.46.win_ref = bf16[16,2,256,384]{3,2,1,0:T(8,128)(2,1)} custom-call(bf16[16,2,16,384]{3,2,1,0:T(8,128)(2,1)} %fusion.2.phased_ref), custom_call_target="tpu_custom_call" | custom-call | tf_op jit(solution)/shard_map/pallas_call | solution.py:60
  56.3 28.2 %all-to-all-done.1 = bf16[32,4,2,16,256]{4,3,2,1,0:T(8,128)(2,1)S(1)} async-done(((bf16[32,4,2,16,256]{4,3,2,1,0:T(8,128)(2,1)}), bf16[32,4,2,16,256]{4,3,2,1,0:T(8,128)(2,1)S(1)}, u32[]{:S(2)}, u32[]{:S(2)}) %all-to-all-start.1) | async-done | bytes 2097184 | tf_op jit(solution)/shard_map/all_to_all | solution.py:155
  84.5 0.0 copy-start
  84.5 1.3 %copy-done = bf16[32,4,2,16,256]{4,3,2,1,0:T(8,128)(2,1)} copy-done((bf16[32,4,2,16,256]{4,3,2,1,0:T(8,128)(2,1)}, bf16[32,4,2,16,256]{4,3,2,1,0:T(8,128)(2,1)S(1)}, u32[]{:S(2)}) %copy-start) | copy-done | bytes 2097176
  85.9 0.0 copy-start.3
  85.9 7.2 %shard_map.47 = f32[16,2,16,128]{3,2,1,0:T(8,128)} custom-call(s32[128]{0:T(128)} %copy-done.2, bf16[128,2,16,256]{3,2,1,0:T(8,128)(2,1)} %bitcast.17, bf16[16,2,256,384]{3,2,1,0:T(8,128)(2,1)} %shard_map.46.win_ref), custom_call_target="tpu_custom_call" | custom-call | tf_op jit(solution)/shard_map/pallas_call | solution.py:116
  93.1 8.4 %all-to-all-start.2 = ((f32[16,2,16,128]{3,2,1,0:T(8,128)}), f32[16,2,16,128]{3,2,1,0:T(8,128)S(1)}, u32[]{:S(2)}, u32[]{:S(2)}) async-start(f32[16,2,16,128]{3,2,1,0:T(8,128)} %shard_map.47), calls=%async_computation.2 | async-start | bytes 524288 | tf_op jit(solution)/shard_map/all_to_all | solution.py:159
  101.5 0.0 copy-done.3
  101.6 0.1 fusion.5
  101.6 0.1 reshape.128
  101.7 11.9 %all-to-all-done.2 = f32[16,2,16,128]{3,2,1,0:T(8,128)S(1)} async-done(((f32[16,2,16,128]{3,2,1,0:T(8,128)}), f32[16,2,16,128]{3,2,1,0:T(8,128)S(1)}, u32[]{:S(2)}, u32[]{:S(2)}) %all-to-all-start.2) | async-done | bytes 262176 | tf_op jit(solution)/shard_map/all_to_all | solution.py:159
  113.6 0.6 multiply_multiply_fusion
  (14 shorter events, 0.2 us)
Async XLA Ops:
  0.0 18.3 %copy-start.1 = (bf16[16,4096]{1,0:T(8,128)(2,1)S(1)}, bf16[16,4096]{1,0:T(8,128)(2,1)}, u32[]{:S(2)}) copy-start(bf16[16,4096]{1,0:T(8,128)(2,1)} %param.4) | copy-start | bytes 393220
  1.1 18.1 %copy-start.2 = (s32[128]{0:T(128)}, s32[128]{0:T(128)S(1)}, u32[]{:S(2)}) copy-start(s32[128]{0:T(128)S(1)} %multiply_add_fusion.slot_ref) | copy-start | bytes 1540
  3.2 20.8 %all-to-all-start = ((s32[32,1,4]{2,1,0:T(1,128)}), s32[32,1,4]{2,1,0:T(1,128)S(1)}, u32[]{:S(2)}, u32[]{:S(2)}) async-start(s32[32,1,4]{2,1,0:T(1,128)} %bitcast.2), calls=%async_computation | async-start | bytes 32768 | tf_op jit(solution)/shard_map/all_to_all | solution.py:150
  28.0 56.6 %all-to-all-start.1 = ((bf16[32,4,2,16,256]{4,3,2,1,0:T(8,128)(2,1)}), bf16[32,4,2,16,256]{4,3,2,1,0:T(8,128)(2,1)S(1)}, u32[]{:S(2)}, u32[]{:S(2)}) async-start(bf16[32,4,2,16,256]{4,3,2,1,0:T(8,128)(2,1)} %bitcast.19), calls=%async_computation.1 | async-start | bytes 4194304 | tf_op jit(solution)/shard_map/all_to_all | solution.py:155
  32.4 4.5 %collective-permute-start.1 = (bf16[16,256]{1,0:T(8,128)(2,1)S(1)}, bf16[16,256]{1,0:T(8,128)(2,1)S(1)}, u32[]{:S(2)}, u32[]{:S(2)}) collective-permute-start(bf16[16,256]{1,0:T(8,128)(2,1)S(1)} %slice.32), channel_id=1, source_target_pairs={{0,1},{1,2},{2,3},{3,4},{4,5},{5,6},{6,7},{7,8},{8,9},{9,10},{10,1... | collective-permute-start | bytes 24584 | tf_op jit(solution)/shard_map/ppermute | solution.py:19
  35.5 4.7 %collective-permute-start = (bf16[16,256]{1,0:T(8,128)(2,1)S(1)}, bf16[16,256]{1,0:T(8,128)(2,1)S(1)}, u32[]{:S(2)}, u32[]{:S(2)}) collective-permute-start(bf16[16,256]{1,0:T(8,128)(2,1)S(1)} %slice.23), channel_id=1, source_target_pairs={{1,0},{2,1},{3,2},{4,3},{5,4},{6,5},{7,6},{8,7},{9,8},{10,9},{11,1... | collective-permute-start | bytes 24584 | tf_op jit(solution)/shard_map/ppermute | solution.py:19
  84.5 1.3 %copy-start = (bf16[32,4,2,16,256]{4,3,2,1,0:T(8,128)(2,1)}, bf16[32,4,2,16,256]{4,3,2,1,0:T(8,128)(2,1)S(1)}, u32[]{:S(2)}) copy-start(bf16[32,4,2,16,256]{4,3,2,1,0:T(8,128)(2,1)S(1)} %all-to-all-done.1) | copy-start | bytes 6291460
  85.9 15.7 %copy-start.3 = (s32[16]{0:T(128)S(1)}, s32[16]{0:T(128)}, u32[]{:S(2)}) copy-start(s32[16]{0:T(128)} %param.7) | copy-start | bytes 196
  93.1 20.5 %all-to-all-start.2 = ((f32[16,2,16,128]{3,2,1,0:T(8,128)}), f32[16,2,16,128]{3,2,1,0:T(8,128)S(1)}, u32[]{:S(2)}, u32[]{:S(2)}) async-start(f32[16,2,16,128]{3,2,1,0:T(8,128)} %shard_map.47), calls=%async_computation.2 | async-start | bytes 524288 | tf_op jit(solution)/shard_map/all_to_all | solution.py:159

commit v7 on v6

--- a/solution.py
+++ b/solution.py
@@ -36,10 +36,28 @@
     return jnp.swapaxes(split, -1, -2)
 
 
-def pick_rows(onehot, table):
-    flat = table.reshape(table.shape[0], -1)
-    out = jnp.dot(onehot, flat, preferred_element_type=jnp.float32).astype(table.dtype)
-    return out.reshape((onehot.shape[0],) + table.shape[1:])
+def pick_kernel(index_ref, table_ref, out_ref):
+    def body(r, carry):
+        out_ref[r] = table_ref[index_ref[r]]
+        return carry
+
+    lax.fori_loop(0, out_ref.shape[0], body, 0)
+
+
+def pick_rows(index, table):
+    rest = table.shape[1:]
+    zeros = (0,) * len(table.shape)
+    grid_spec = pltpu.PrefetchScalarGridSpec(
+        num_scalar_prefetch=1,
+        grid=(1,),
+        in_specs=[pl.BlockSpec(table.shape, lambda g, idx: zeros)],
+        out_specs=pl.BlockSpec((index.shape[0],) + rest, lambda g, idx: zeros),
+    )
+    return pl.pallas_call(
+        pick_kernel,
+        grid_spec=grid_spec,
+        out_shape=jax.ShapeDtypeStruct((index.shape[0],) + rest, table.dtype),
+    )(index, table)
 
 
 def window_kernel(phased_ref, win_ref):
@@ -150,8 +168,7 @@
     index_in = lax.all_to_all(send_index, "lane", split_axis=0, concat_axis=0, tiled=True)
     both = deinterleave(jnp.stack([waveforms, levels], axis=1))
     both = jnp.concatenate([both[:, :1], both[:, 1:, ::-1]], axis=1)
-    pick = (index_in.reshape(-1)[:, None] == jnp.arange(lane_dev)[None, :]).astype(jnp.bfloat16)
-    reply = pick_rows(pick, both).reshape((lane_count, capacity) + both.shape[1:])
+    reply = pick_rows(index_in.reshape(-1), both).reshape((lane_count, capacity) + both.shape[1:])
     got = lax.all_to_all(reply, "lane", split_axis=0, concat_axis=0, tiled=True)
     got = got.reshape((lane_count * capacity,) + both.shape[1:])
     lag_dev = LAGS // rec_count

time: 116 us -> 117 us (level)
  Pallas kernels: 18.2 us -> 22 us
  local copies, waits for them, and re-layouts: 13.8 us -> 12.2 us
    pallas_call x0 -> x1, Pallas kernels: none -> 3.73 us  [pick_rows(): pl.pallas_call(pick_kernel, grid_spec=grid_spec, out_shape=jax.ShapeDtype...]
    unnamed x11 -> x9, local copies, waits for them, and re-layouts: 4.25 us -> 2.15 us
where the time goes in v7:
time: 117 us; the launch traced here: 116 us
  waiting for transfers between devices  44.6 us (38%)
  starting transfers between devices  30.4 us (26%)
  Pallas kernels  22 us (19%)
  local copies, waits for them, and re-layouts  12.2 us (10%)
  other arithmetic  6.31 us (5%)
    all_to_all x1, waiting for transfers between devices, per_device(): got = lax.all_to_all(reply, 'lane', split_axis=0, concat_axis=0, tiled=True)  28.1 us
    all_to_all x1, starting transfers between devices, per_device(): lax.all_to_all(send_index, 'lane', split_axis=0, concat_axis=0, tiled=True)  13 us
    all_to_all x1, waiting for transfers between devices, per_device(): lax.all_to_all(terms, 'rec', split_axis=0, concat_axis=0, tiled=True)  11.8 us
    pallas_call x1, Pallas kernels, windows(): pl.pallas_call(window_kernel, grid=(lanes,), in_specs=[pl.BlockSpec((1, 2...  11 us
    all_to_all x1, starting transfers between devices, per_device(): lax.all_to_all(terms, 'rec', split_axis=0, concat_axis=0, tiled=True)  8.21 us
    pallas_call x1, Pallas kernels, correlate(): pl.pallas_call(functools.partial(lane_kernel, slots, group), grid_spec=gr...  7.23 us
    all_to_all x1, starting transfers between devices, per_device(): got = lax.all_to_all(reply, 'lane', split_axis=0, concat_axis=0, tiled=True)  4.77 us
    ppermute x2, starting transfers between devices, passed_along(): return lax.ppermute(block, axis, route)  4.41 us
  transfers between devices with their start and end apart: 5, of which 4 were waited for; matrix products, arithmetic and copies ran while one was open for 10% of the time, Pallas kernels for 10%

profile of v7, /device:TPU:1, one launch (start us, length us, event | category | flops | bytes accessed | tf_op | source)
XLA Modules:
  0.0 115.8 jit_solution(11914528157138156589)
XLA Ops:
  0.0 0.0 copy-start.1
  0.0 0.8 copy.17
  0.8 0.1 reshape.127
  0.9 0.2 convert_reduce_fusion
  1.1 0.0 copy-start.2
  1.1 0.1 select_reduce_fusion
  1.2 1.2 %gather_fusion = s32[128]{0:T(128)S(1)} fusion(s32[128]{0:T(128)S(1)} %get-tuple-element.9, s32[1024]{0:T(1024)S(1)} %pad_clamp_fusion), kind=kCustom, calls=%fused_computation | custom fusion | bytes 1536 | tf_op jit(solution)/shard_map/gather | solution.py:167
  2.5 0.7 all_to_all.12
  3.2 13.0 %all-to-all-start = ((s32[32,1,4]{2,1,0:T(1,128)}), s32[32,1,4]{2,1,0:T(1,128)S(1)}, u32[]{:S(2)}, u32[]{:S(2)}) async-start(s32[32,1,4]{2,1,0:T(1,128)} %bitcast.2), calls=%async_computation | async-start | bytes 32768 | tf_op jit(solution)/shard_map/all_to_all | solution.py:168
  16.2 1.0 add_convert_fusion
  17.2 0.8 stack.19
  18.0 0.3 copy.20
  18.3 0.0 copy-done.1
  18.3 0.8 stack.18
  19.2 0.0 copy-done.2
  19.2 0.3 copy.19
  19.5 0.1 rev.6
  19.7 0.7 pad_maximum_fusion.table_ref
  20.4 3.5 %all-to-all-done = s32[32,1,4]{2,1,0:T(1,128)S(1)} async-done(((s32[32,1,4]{2,1,0:T(1,128)}), s32[32,1,4]{2,1,0:T(1,128)S(1)}, u32[]{:S(2)}, u32[]{:S(2)}) %all-to-all-start) | async-done | bytes 544 | tf_op jit(solution)/shard_map/all_to_all | solution.py:168
  23.9 0.5 broadcast.142
  24.5 0.7 reduce.3
  25.1 0.6 reshape.128.index_ref
  25.8 3.7 %shard_map.46 = bf16[128,2,16,256]{3,2,1,0:T(8,128)(2,1)} custom-call(s32[128]{0:T(128)} %reshape.128.index_ref, bf16[16,2,16,256]{3,2,1,0:T(8,128)(2,1)} %pad_maximum_fusion.table_ref), custom_call_target="tpu_custom_call" | custom-call | tf_op jit(solution)/shard_map/pallas_call | solution.py:56
  29.5 4.8 %all-to-all-start.1 = ((bf16[32,4,2,16,256]{4,3,2,1,0:T(8,128)(2,1)}), bf16[32,4,2,16,256]{4,3,2,1,0:T(8,128)(2,1)S(1)}, u32[]{:S(2)}, u32[]{:S(2)}) async-start(bf16[32,4,2,16,256]{4,3,2,1,0:T(8,128)(2,1)} %bitcast.12), calls=%async_computation.1 | async-start | bytes 4194304 | tf_op jit(solution)/shard_map/all_to_all | solution.py:172
  34.3 3.1 %collective-permute-start.1 = (bf16[16,256]{1,0:T(8,128)(2,1)S(1)}, bf16[16,256]{1,0:T(8,128)(2,1)S(1)}, u32[]{:S(2)}, u32[]{:S(2)}) collective-permute-start(bf16[16,256]{1,0:T(8,128)(2,1)S(1)} %slice.32), channel_id=1, source_target_pairs={{0,1},{1,2},{2,3},{3,4},{4,5},{5,6},{6,7},{7,8},{8,9},{9,10},{10,1... | collective-permute-start | bytes 24584 | tf_op jit(solution)/shard_map/ppermute | solution.py:19
  37.4 1.3 %collective-permute-start = (bf16[16,256]{1,0:T(8,128)(2,1)S(1)}, bf16[16,256]{1,0:T(8,128)(2,1)S(1)}, u32[]{:S(2)}, u32[]{:S(2)}) collective-permute-start(bf16[16,256]{1,0:T(8,128)(2,1)S(1)} %slice.23), channel_id=1, source_target_pairs={{1,0},{2,1},{3,2},{4,3},{5,4},{6,5},{7,6},{8,7},{9,8},{10,9},{11,1... | collective-permute-start | bytes 24584 | tf_op jit(solution)/shard_map/ppermute | solution.py:19
  38.7 0.0 collective-permute-done.1
  38.8 0.1 slice.33
  38.8 0.2 concatenate.16
  39.0 0.8 stack.22
  39.8 1.1 copy.22
  41.0 1.2 collective-permute-done
  42.1 0.9 maximum_maximum_fusion
  43.0 0.8 stack.21
  43.9 1.1 copy.21
  45.0 1.1 maximum_bitcast_fusion
  46.1 0.2 rev.7
  46.3 0.9 fusion.2.phased_ref
  47.2 11.0 %shard_map.47.win_ref = bf16[16,2,256,384]{3,2,1,0:T(8,128)(2,1)} custom-call(bf16[16,2,16,384]{3,2,1,0:T(8,128)(2,1)} %fusion.2.phased_ref), custom_call_target="tpu_custom_call" | custom-call | tf_op jit(solution)/shard_map/pallas_call | solution.py:78
  58.2 28.1 %all-to-all-done.1 = bf16[32,4,2,16,256]{4,3,2,1,0:T(8,128)(2,1)S(1)} async-done(((bf16[32,4,2,16,256]{4,3,2,1,0:T(8,128)(2,1)}), bf16[32,4,2,16,256]{4,3,2,1,0:T(8,128)(2,1)S(1)}, u32[]{:S(2)}, u32[]{:S(2)}) %all-to-all-start.1) | async-done | bytes 2097184 | tf_op jit(solution)/shard_map/all_to_all | solution.py:172
  86.3 0.0 copy-start
  86.3 1.3 %copy-done = bf16[32,4,2,16,256]{4,3,2,1,0:T(8,128)(2,1)} copy-done((bf16[32,4,2,16,256]{4,3,2,1,0:T(8,128)(2,1)}, bf16[32,4,2,16,256]{4,3,2,1,0:T(8,128)(2,1)S(1)}, u32[]{:S(2)}) %copy-start) | copy-done | bytes 2097176
  87.7 0.0 copy-start.3
  87.7 7.2 %shard_map.48 = f32[16,2,16,128]{3,2,1,0:T(8,128)} custom-call(s32[128]{0:T(128)} %copy-done.2, bf16[128,2,16,256]{3,2,1,0:T(8,128)(2,1)} %bitcast.11, bf16[16,2,256,384]{3,2,1,0:T(8,128)(2,1)} %shard_map.47.win_ref), custom_call_target="tpu_custom_call" | custom-call | tf_op jit(solution)/shard_map/pallas_call | solution.py:134
  94.9 8.2 %all-to-all-start.2 = ((f32[16,2,16,128]{3,2,1,0:T(8,128)}), f32[16,2,16,128]{3,2,1,0:T(8,128)S(1)}, u32[]{:S(2)}, u32[]{:S(2)}) async-start(f32[16,2,16,128]{3,2,1,0:T(8,128)} %shard_map.48), calls=%async_computation.2 | async-start | bytes 524288 | tf_op jit(solution)/shard_map/all_to_all | solution.py:176
  103.1 0.0 copy-done.3
  103.1 0.1 fusion.4
  103.2 0.1 reshape.131
  103.3 11.8 %all-to-all-done.2 = f32[16,2,16,128]{3,2,1,0:T(8,128)S(1)} async-done(((f32[16,2,16,128]{3,2,1,0:T(8,128)}), f32[16,2,16,128]{3,2,1,0:T(8,128)S(1)}, u32[]{:S(2)}, u32[]{:S(2)}) %all-to-all-start.2) | async-done | bytes 262176 | tf_op jit(solution)/shard_map/all_to_all | solution.py:176
  115.2 0.6 multiply_multiply_fusion
  (13 shorter events, 0.2 us)
Async XLA Ops:
  0.0 18.3 %copy-start.1 = (bf16[16,4096]{1,0:T(8,128)(2,1)S(1)}, bf16[16,4096]{1,0:T(8,128)(2,1)}, u32[]{:S(2)}) copy-start(bf16[16,4096]{1,0:T(8,128)(2,1)} %param.4) | copy-start | bytes 393220
  1.1 18.1 %copy-start.2 = (s32[128]{0:T(128)}, s32[128]{0:T(128)S(1)}, u32[]{:S(2)}) copy-start(s32[128]{0:T(128)S(1)} %multiply_add_fusion.slot_ref) | copy-start | bytes 1540
  3.2 20.8 %all-to-all-start = ((s32[32,1,4]{2,1,0:T(1,128)}), s32[32,1,4]{2,1,0:T(1,128)S(1)}, u32[]{:S(2)}, u32[]{:S(2)}) async-start(s32[32,1,4]{2,1,0:T(1,128)} %bitcast.2), calls=%async_computation | async-start | bytes 32768 | tf_op jit(solution)/shard_map/all_to_all | solution.py:168
  29.5 56.8 %all-to-all-start.1 = ((bf16[32,4,2,16,256]{4,3,2,1,0:T(8,128)(2,1)}), bf16[32,4,2,16,256]{4,3,2,1,0:T(8,128)(2,1)S(1)}, u32[]{:S(2)}, u32[]{:S(2)}) async-start(bf16[32,4,2,16,256]{4,3,2,1,0:T(8,128)(2,1)} %bitcast.12), calls=%async_computation.1 | async-start | bytes 4194304 | tf_op jit(solution)/shard_map/all_to_all | solution.py:172
  34.3 4.5 %collective-permute-start.1 = (bf16[16,256]{1,0:T(8,128)(2,1)S(1)}, bf16[16,256]{1,0:T(8,128)(2,1)S(1)}, u32[]{:S(2)}, u32[]{:S(2)}) collective-permute-start(bf16[16,256]{1,0:T(8,128)(2,1)S(1)} %slice.32), channel_id=1, source_target_pairs={{0,1},{1,2},{2,3},{3,4},{4,5},{5,6},{6,7},{7,8},{8,9},{9,10},{10,1... | collective-permute-start | bytes 24584 | tf_op jit(solution)/shard_map/ppermute | solution.py:19
  37.4 4.7 %collective-permute-start = (bf16[16,256]{1,0:T(8,128)(2,1)S(1)}, bf16[16,256]{1,0:T(8,128)(2,1)S(1)}, u32[]{:S(2)}, u32[]{:S(2)}) collective-permute-start(bf16[16,256]{1,0:T(8,128)(2,1)S(1)} %slice.23), channel_id=1, source_target_pairs={{1,0},{2,1},{3,2},{4,3},{5,4},{6,5},{7,6},{8,7},{9,8},{10,9},{11,1... | collective-permute-start | bytes 24584 | tf_op jit(solution)/shard_map/ppermute | solution.py:19
  86.3 1.3 %copy-start = (bf16[32,4,2,16,256]{4,3,2,1,0:T(8,128)(2,1)}, bf16[32,4,2,16,256]{4,3,2,1,0:T(8,128)(2,1)S(1)}, u32[]{:S(2)}) copy-start(bf16[32,4,2,16,256]{4,3,2,1,0:T(8,128)(2,1)S(1)} %all-to-all-done.1) | copy-start | bytes 6291460
  87.7 15.4 %copy-start.3 = (s32[16]{0:T(128)S(1)}, s32[16]{0:T(128)}, u32[]{:S(2)}) copy-start(s32[16]{0:T(128)} %param.7) | copy-start | bytes 196
  94.9 20.2 %all-to-all-start.2 = ((f32[16,2,16,128]{3,2,1,0:T(8,128)}), f32[16,2,16,128]{3,2,1,0:T(8,128)S(1)}, u32[]{:S(2)}, u32[]{:S(2)}) async-start(f32[16,2,16,128]{3,2,1,0:T(8,128)} %shard_map.48), calls=%async_computation.2 | async-start | bytes 524288 | tf_op jit(solution)/shard_map/all_to_all | solution.py:176

commit v8 on v6

--- a/solution.py
+++ b/solution.py
@@ -99,7 +99,7 @@
     slots = pairs // lanes
     blocks = got.shape[3]
     lag_dev = LAGS // rec_count
-    group = math.gcd(lanes, 4)
+    group = math.gcd(lanes, 8)
 
     grid_spec = pltpu.PrefetchScalarGridSpec(
         num_scalar_prefetch=1,

time: 116 us -> 115 us (level)
  no operation moved by 1% of the time
where the time goes in v8:
time: 115 us; the launch traced here: 113 us
  waiting for transfers between devices  45.3 us (39%)
  starting transfers between devices  30.2 us (26%)
  Pallas kernels  17.4 us (15%)
  local copies, waits for them, and re-layouts  13.8 us (12%)
  other arithmetic  5.62 us (5%)
    all_to_all x1, waiting for transfers between devices, per_device(): got = lax.all_to_all(reply, 'lane', split_axis=0, concat_axis=0, tiled=True)  28.2 us
    all_to_all x1, starting transfers between devices, per_device(): lax.all_to_all(send_index, 'lane', split_axis=0, concat_axis=0, tiled=True)  13 us
    all_to_all x1, waiting for transfers between devices, per_device(): lax.all_to_all(terms, 'rec', split_axis=0, concat_axis=0, tiled=True)  11.9 us
    pallas_call x1, Pallas kernels, windows(): pl.pallas_call(window_kernel, grid=(lanes,), in_specs=[pl.BlockSpec((1, 2...  11 us
    all_to_all x1, starting transfers between devices, per_device(): lax.all_to_all(terms, 'rec', split_axis=0, concat_axis=0, tiled=True)  8.4 us
    pallas_call x1, Pallas kernels, correlate(): pl.pallas_call(functools.partial(lane_kernel, slots, group), grid_spec=gr...  6.38 us
    all_to_all x1, starting transfers between devices, per_device(): got = lax.all_to_all(reply, 'lane', split_axis=0, concat_axis=0, tiled=True)  4.41 us
    ppermute x2, starting transfers between devices, passed_along(): return lax.ppermute(block, axis, route)  4.41 us
  transfers between devices with their start and end apart: 5, of which 4 were waited for; matrix products, arithmetic and copies ran while one was open for 10% of the time, Pallas kernels for 10%

profile of v8, /device:TPU:1, one launch (start us, length us, event | category | flops | bytes accessed | tf_op | source)
XLA Modules:
  0.0 113.4 jit_solution(18429941637874662570)
XLA Ops:
  0.0 0.0 copy-start.1
  0.0 0.8 copy.16
  0.8 0.1 reshape.125
  0.9 0.2 convert_reduce_fusion
  1.1 0.0 copy-start.2
  1.1 0.1 select_reduce_fusion
  1.2 1.2 %gather_fusion = s32[128]{0:T(128)S(1)} fusion(s32[128]{0:T(128)S(1)} %get-tuple-element.9, s32[1024]{0:T(1024)S(1)} %pad_clamp_fusion), kind=kCustom, calls=%fused_computation | custom fusion | bytes 1536 | tf_op jit(solution)/shard_map/gather | solution.py:149
  2.5 0.7 all_to_all.12
  3.2 13.0 %all-to-all-start = ((s32[32,1,4]{2,1,0:T(1,128)}), s32[32,1,4]{2,1,0:T(1,128)S(1)}, u32[]{:S(2)}, u32[]{:S(2)}) async-start(s32[32,1,4]{2,1,0:T(1,128)} %bitcast.2), calls=%async_computation | async-start | bytes 32768 | tf_op jit(solution)/shard_map/all_to_all | solution.py:150
  16.2 1.0 add_convert_fusion
  17.2 0.8 stack.19
  18.0 0.3 copy.19
  18.3 0.0 copy-done.1
  18.3 0.8 stack.18
  19.2 0.0 copy-done.2
  19.2 0.3 copy.18
  19.5 0.1 rev.6
  19.7 0.2 copy.22
  19.9 4.1 %all-to-all-done = s32[32,1,4]{2,1,0:T(1,128)S(1)} async-done(((s32[32,1,4]{2,1,0:T(1,128)}), s32[32,1,4]{2,1,0:T(1,128)S(1)}, u32[]{:S(2)}, u32[]{:S(2)}) %all-to-all-start) | async-done | bytes 544 | tf_op jit(solution)/shard_map/all_to_all | solution.py:150
  23.9 0.5 broadcast.142
  24.5 0.7 reduce.3
  25.1 0.1 eq.46
  25.2 0.7 convolution_convert_fusion
  26.0 2.0 %copy.23 = bf16[16,8,32,256]{3,2,1,0:T(8,128)(2,1)} copy(bf16[16,8,32,256]{3,1,2,0:T(8,128)(2,1)S(1)} %bitcast.18) | data formatting | bytes 4194304
  28.0 4.4 %all-to-all-start.1 = ((bf16[32,4,2,16,256]{4,3,2,1,0:T(8,128)(2,1)}), bf16[32,4,2,16,256]{4,3,2,1,0:T(8,128)(2,1)S(1)}, u32[]{:S(2)}, u32[]{:S(2)}) async-start(bf16[32,4,2,16,256]{4,3,2,1,0:T(8,128)(2,1)} %bitcast.19), calls=%async_computation.1 | async-start | bytes 4194304 | tf_op jit(solution)/shard_map/all_to_all | solution.py:155
  32.4 3.1 %collective-permute-start.1 = (bf16[16,256]{1,0:T(8,128)(2,1)S(1)}, bf16[16,256]{1,0:T(8,128)(2,1)S(1)}, u32[]{:S(2)}, u32[]{:S(2)}) collective-permute-start(bf16[16,256]{1,0:T(8,128)(2,1)S(1)} %slice.32), channel_id=1, source_target_pairs={{0,1},{1,2},{2,3},{3,4},{4,5},{5,6},{6,7},{7,8},{8,9},{9,10},{10,1... | collective-permute-start | bytes 24584 | tf_op jit(solution)/shard_map/ppermute | solution.py:19
  35.5 1.3 %collective-permute-start = (bf16[16,256]{1,0:T(8,128)(2,1)S(1)}, bf16[16,256]{1,0:T(8,128)(2,1)S(1)}, u32[]{:S(2)}, u32[]{:S(2)}) collective-permute-start(bf16[16,256]{1,0:T(8,128)(2,1)S(1)} %slice.23), channel_id=1, source_target_pairs={{1,0},{2,1},{3,2},{4,3},{5,4},{6,5},{7,6},{8,7},{9,8},{10,9},{11,1... | collective-permute-start | bytes 24584 | tf_op jit(solution)/shard_map/ppermute | solution.py:19
  36.8 0.0 collective-permute-done.1
  36.9 0.1 slice.33
  36.9 0.2 concatenate.16
  37.1 0.8 stack.22
  37.9 1.1 copy.21
  39.1 1.2 %collective-permute-done = bf16[16,256]{1,0:T(8,128)(2,1)S(1)} collective-permute-done((bf16[16,256]{1,0:T(8,128)(2,1)S(1)}, bf16[16,256]{1,0:T(8,128)(2,1)S(1)}, u32[]{:S(2)}, u32[]{:S(2)}) %collective-permute-start) | collective-permute-done | bytes 8224 | tf_op jit(solution)/shard_map/ppermute | solution.py:19
  40.2 0.9 maximum_maximum_fusion
  41.1 0.8 stack.21
  42.0 1.1 %copy.20 = bf16[16,1,280,16]{2,3,1,0:T(8,128)(2,1)} copy(bf16[16,1,280,16]{3,2,0,1:T(8,128)(2,1)S(1)} %stack.21) | data formatting | bytes 286720 | tf_op jit(solution)/shard_map/stack | solution.py:142
  43.1 1.1 maximum_bitcast_fusion
  44.2 0.2 rev.7
  44.4 0.9 fusion.2.phased_ref
  45.3 11.0 %shard_map.46.win_ref = bf16[16,2,256,384]{3,2,1,0:T(8,128)(2,1)} custom-call(bf16[16,2,16,384]{3,2,1,0:T(8,128)(2,1)} %fusion.2.phased_ref), custom_call_target="tpu_custom_call" | custom-call | tf_op jit(solution)/shard_map/pallas_call | solution.py:60
  56.3 28.2 %all-to-all-done.1 = bf16[32,4,2,16,256]{4,3,2,1,0:T(8,128)(2,1)S(1)} async-done(((bf16[32,4,2,16,256]{4,3,2,1,0:T(8,128)(2,1)}), bf16[32,4,2,16,256]{4,3,2,1,0:T(8,128)(2,1)S(1)}, u32[]{:S(2)}, u32[]{:S(2)}) %all-to-all-start.1) | async-done | bytes 2097184 | tf_op jit(solution)/shard_map/all_to_all | solution.py:155
  84.5 0.0 copy-start
  84.5 1.3 %copy-done = bf16[32,4,2,16,256]{4,3,2,1,0:T(8,128)(2,1)} copy-done((bf16[32,4,2,16,256]{4,3,2,1,0:T(8,128)(2,1)}, bf16[32,4,2,16,256]{4,3,2,1,0:T(8,128)(2,1)S(1)}, u32[]{:S(2)}) %copy-start) | copy-done | bytes 2097176
  85.9 0.0 copy-start.3
  85.9 6.4 %shard_map.47 = f32[16,2,16,128]{3,2,1,0:T(8,128)} custom-call(s32[128]{0:T(128)} %copy-done.2, bf16[128,2,16,256]{3,2,1,0:T(8,128)(2,1)} %bitcast.17, bf16[16,2,256,384]{3,2,1,0:T(8,128)(2,1)} %shard_map.46.win_ref), custom_call_target="tpu_custom_call" | custom-call | tf_op jit(solution)/shard_map/pallas_call | solution.py:116
  92.3 8.4 %all-to-all-start.2 = ((f32[16,2,16,128]{3,2,1,0:T(8,128)}), f32[16,2,16,128]{3,2,1,0:T(8,128)S(1)}, u32[]{:S(2)}, u32[]{:S(2)}) async-start(f32[16,2,16,128]{3,2,1,0:T(8,128)} %shard_map.47), calls=%async_computation.2 | async-start | bytes 524288 | tf_op jit(solution)/shard_map/all_to_all | solution.py:159
  100.7 0.0 copy-done.3
  100.7 0.1 fusion.5
  100.8 0.1 reshape.128
  100.9 11.9 %all-to-all-done.2 = f32[16,2,16,128]{3,2,1,0:T(8,128)S(1)} async-done(((f32[16,2,16,128]{3,2,1,0:T(8,128)}), f32[16,2,16,128]{3,2,1,0:T(8,128)S(1)}, u32[]{:S(2)}, u32[]{:S(2)}) %all-to-all-start.2) | async-done | bytes 262176 | tf_op jit(solution)/shard_map/all_to_all | solution.py:159
  112.8 0.6 multiply_multiply_fusion
  (14 shorter events, 0.2 us)
Async XLA Ops:
  0.0 18.3 %copy-start.1 = (bf16[16,4096]{1,0:T(8,128)(2,1)S(1)}, bf16[16,4096]{1,0:T(8,128)(2,1)}, u32[]{:S(2)}) copy-start(bf16[16,4096]{1,0:T(8,128)(2,1)} %param.4) | copy-start | bytes 393220
  1.1 18.1 %copy-start.2 = (s32[128]{0:T(128)}, s32[128]{0:T(128)S(1)}, u32[]{:S(2)}) copy-start(s32[128]{0:T(128)S(1)} %multiply_add_fusion.slot_ref) | copy-start | bytes 1540
  3.2 20.8 %all-to-all-start = ((s32[32,1,4]{2,1,0:T(1,128)}), s32[32,1,4]{2,1,0:T(1,128)S(1)}, u32[]{:S(2)}, u32[]{:S(2)}) async-start(s32[32,1,4]{2,1,0:T(1,128)} %bitcast.2), calls=%async_computation | async-start | bytes 32768 | tf_op jit(solution)/shard_map/all_to_all | solution.py:150
  28.0 56.6 %all-to-all-start.1 = ((bf16[32,4,2,16,256]{4,3,2,1,0:T(8,128)(2,1)}), bf16[32,4,2,16,256]{4,3,2,1,0:T(8,128)(2,1)S(1)}, u32[]{:S(2)}, u32[]{:S(2)}) async-start(bf16[32,4,2,16,256]{4,3,2,1,0:T(8,128)(2,1)} %bitcast.19), calls=%async_computation.1 | async-start | bytes 4194304 | tf_op jit(solution)/shard_map/all_to_all | solution.py:155
  32.4 4.5 %collective-permute-start.1 = (bf16[16,256]{1,0:T(8,128)(2,1)S(1)}, bf16[16,256]{1,0:T(8,128)(2,1)S(1)}, u32[]{:S(2)}, u32[]{:S(2)}) collective-permute-start(bf16[16,256]{1,0:T(8,128)(2,1)S(1)} %slice.32), channel_id=1, source_target_pairs={{0,1},{1,2},{2,3},{3,4},{4,5},{5,6},{6,7},{7,8},{8,9},{9,10},{10,1... | collective-permute-start | bytes 24584 | tf_op jit(solution)/shard_map/ppermute | solution.py:19
  35.5 4.7 %collective-permute-start = (bf16[16,256]{1,0:T(8,128)(2,1)S(1)}, bf16[16,256]{1,0:T(8,128)(2,1)S(1)}, u32[]{:S(2)}, u32[]{:S(2)}) collective-permute-start(bf16[16,256]{1,0:T(8,128)(2,1)S(1)} %slice.23), channel_id=1, source_target_pairs={{1,0},{2,1},{3,2},{4,3},{5,4},{6,5},{7,6},{8,7},{9,8},{10,9},{11,1... | collective-permute-start | bytes 24584 | tf_op jit(solution)/shard_map/ppermute | solution.py:19
  84.5 1.3 %copy-start = (bf16[32,4,2,16,256]{4,3,2,1,0:T(8,128)(2,1)}, bf16[32,4,2,16,256]{4,3,2,1,0:T(8,128)(2,1)S(1)}, u32[]{:S(2)}) copy-start(bf16[32,4,2,16,256]{4,3,2,1,0:T(8,128)(2,1)S(1)} %all-to-all-done.1) | copy-start | bytes 6291460
  85.9 14.8 %copy-start.3 = (s32[16]{0:T(128)S(1)}, s32[16]{0:T(128)}, u32[]{:S(2)}) copy-start(s32[16]{0:T(128)} %param.7) | copy-start | bytes 196
  92.3 20.5 %all-to-all-start.2 = ((f32[16,2,16,128]{3,2,1,0:T(8,128)}), f32[16,2,16,128]{3,2,1,0:T(8,128)S(1)}, u32[]{:S(2)}, u32[]{:S(2)}) async-start(f32[16,2,16,128]{3,2,1,0:T(8,128)} %shard_map.47), calls=%async_computation.2 | async-start | bytes 524288 | tf_op jit(solution)/shard_map/all_to_all | solution.py:159

commit v9 on v8

--- a/solution.py
+++ b/solution.py
@@ -34,12 +34,6 @@
     n = rows.shape[-1]
     split = rows.reshape(lead + (n // PHASE, PHASE))
     return jnp.swapaxes(split, -1, -2)
-
-
-def pick_rows(onehot, table):
-    flat = table.reshape(table.shape[0], -1)
-    out = jnp.dot(onehot, flat, preferred_element_type=jnp.float32).astype(table.dtype)
-    return out.reshape((onehot.shape[0],) + table.shape[1:])
 
 
 def window_kernel(phased_ref, win_ref):
@@ -150,8 +144,7 @@
     index_in = lax.all_to_all(send_index, "lane", split_axis=0, concat_axis=0, tiled=True)
     both = deinterleave(jnp.stack([waveforms, levels], axis=1))
     both = jnp.concatenate([both[:, :1], both[:, 1:, ::-1]], axis=1)
-    pick = (index_in.reshape(-1)[:, None] == jnp.arange(lane_dev)[None, :]).astype(jnp.bfloat16)
-    reply = pick_rows(pick, both).reshape((lane_count, capacity) + both.shape[1:])
+    reply = both[index_in.reshape(-1)].reshape((lane_count, capacity) + both.shape[1:])
     got = lax.all_to_all(reply, "lane", split_axis=0, concat_axis=0, tiled=True)
     got = got.reshape((lane_count * capacity,) + both.shape[1:])
     lag_dev = LAGS // rec_count

time: 115 us -> 114 us (level)
    unnamed x11 -> x9, local copies, waits for them, and re-layouts: 4.25 us -> 2.15 us
    gather x0 -> x1, local copies, waits for them, and re-layouts: none -> 2.02 us  [per_device(): both[index_in.reshape(-1)].reshape((lane_count, capacity) + both.shape[1:])]
where the time goes in v9:
time: 114 us; the launch traced here: 113 us
  waiting for transfers between devices  45.5 us (40%)
  starting transfers between devices  30.2 us (26%)
  Pallas kernels  17.4 us (15%)
  local copies, waits for them, and re-layouts  13.7 us (12%)
  other arithmetic  5.63 us (5%)
    all_to_all x1, waiting for transfers between devices, per_device(): got = lax.all_to_all(reply, 'lane', split_axis=0, concat_axis=0, tiled=True)  28.2 us
    all_to_all x1, starting transfers between devices, per_device(): lax.all_to_all(send_index, 'lane', split_axis=0, concat_axis=0, tiled=True)  13 us
    all_to_all x1, waiting for transfers between devices, per_device(): lax.all_to_all(terms, 'rec', split_axis=0, concat_axis=0, tiled=True)  11.9 us
    pallas_call x1, Pallas kernels, windows(): pl.pallas_call(window_kernel, grid=(lanes,), in_specs=[pl.BlockSpec((1, 2...  11 us
    all_to_all x1, starting transfers between devices, per_device(): lax.all_to_all(terms, 'rec', split_axis=0, concat_axis=0, tiled=True)  8.4 us
    pallas_call x1, Pallas kernels, correlate(): pl.pallas_call(functools.partial(lane_kernel, slots, group), grid_spec=gr...  6.37 us
    all_to_all x1, starting transfers between devices, per_device(): got = lax.all_to_all(reply, 'lane', split_axis=0, concat_axis=0, tiled=True)  4.41 us
    ppermute x2, starting transfers between devices, passed_along(): return lax.ppermute(block, axis, route)  4.41 us
  transfers between devices with their start and end apart: 5, of which 4 were waited for; matrix products, arithmetic and copies ran while one was open for 10% of the time, Pallas kernels for 10%

profile of v9, /device:TPU:1, one launch (start us, length us, event | category | flops | bytes accessed | tf_op | source)
XLA Modules:
  0.0 112.7 jit_solution(13017938457542271518)
XLA Ops:
  0.0 0.0 copy-start.1
  0.0 0.8 copy.17
  0.8 0.1 reshape.155
  0.9 0.2 convert_reduce_fusion
  1.1 0.0 copy-start.2
  1.1 0.1 select_reduce_fusion
  1.2 1.2 %gather_fusion = s32[128]{0:T(128)S(1)} fusion(s32[128]{0:T(128)S(1)} %get-tuple-element.9, s32[1024]{0:T(1024)S(1)} %pad_clamp_fusion.1), kind=kCustom, calls=%fused_computation | custom fusion | bytes 1536 | tf_op jit(solution)/shard_map/gather | solution.py:143
  2.5 0.7 all_to_all.12
  3.2 13.0 %all-to-all-start = ((s32[32,1,4]{2,1,0:T(1,128)}), s32[32,1,4]{2,1,0:T(1,128)S(1)}, u32[]{:S(2)}, u32[]{:S(2)}) async-start(s32[32,1,4]{2,1,0:T(1,128)} %bitcast.3), calls=%async_computation | async-start | bytes 32768 | tf_op jit(solution)/shard_map/all_to_all | solution.py:144
  16.2 1.0 add_convert_fusion
  17.2 0.8 stack.19
  18.0 0.3 copy.19
  18.3 0.0 copy-done.1
  18.3 0.8 stack.18
  19.2 0.0 copy-done.2
  19.2 0.3 copy.18
  19.5 0.1 rev.6
  19.7 4.2 %all-to-all-done = s32[32,1,4]{2,1,0:T(1,128)S(1)} async-done(((s32[32,1,4]{2,1,0:T(1,128)}), s32[32,1,4]{2,1,0:T(1,128)S(1)}, u32[]{:S(2)}, u32[]{:S(2)}) %all-to-all-start) | async-done | bytes 544 | tf_op jit(solution)/shard_map/all_to_all | solution.py:144
  23.9 0.5 broadcast.162
  24.5 0.7 reduce.3
  25.1 0.1 reshape.156
  25.3 2.0 %gather_fusion.1 = bf16[128,2,16,256]{3,2,1,0:T(8,128)(2,1)} fusion(bf16[16,2,16,256]{3,2,1,0:T(8,128)(2,1)S(1)} %pad_maximum_fusion, s32[1024]{0:T(1024)S(1)} %pad_clamp_fusion), kind=kCustom, calls=%fused_computation.1 | custom fusion | bytes 4194816 | tf_op jit(solution)/shard_map/gather | solution.py:147
  27.3 4.4 %all-to-all-start.1 = ((bf16[32,4,2,16,256]{4,3,2,1,0:T(8,128)(2,1)}), bf16[32,4,2,16,256]{4,3,2,1,0:T(8,128)(2,1)S(1)}, u32[]{:S(2)}, u32[]{:S(2)}) async-start(bf16[32,4,2,16,256]{4,3,2,1,0:T(8,128)(2,1)} %bitcast.14), calls=%async_computation.1 | async-start | bytes 4194304 | tf_op jit(solution)/shard_map/all_to_all | solution.py:148
  31.7 3.1 %collective-permute-start.1 = (bf16[16,256]{1,0:T(8,128)(2,1)S(1)}, bf16[16,256]{1,0:T(8,128)(2,1)S(1)}, u32[]{:S(2)}, u32[]{:S(2)}) collective-permute-start(bf16[16,256]{1,0:T(8,128)(2,1)S(1)} %slice.34), channel_id=1, source_target_pairs={{0,1},{1,2},{2,3},{3,4},{4,5},{5,6},{6,7},{7,8},{8,9},{9,10},{10,1... | collective-permute-start | bytes 24584 | tf_op jit(solution)/shard_map/ppermute | solution.py:19
  34.9 1.3 %collective-permute-start = (bf16[16,256]{1,0:T(8,128)(2,1)S(1)}, bf16[16,256]{1,0:T(8,128)(2,1)S(1)}, u32[]{:S(2)}, u32[]{:S(2)}) collective-permute-start(bf16[16,256]{1,0:T(8,128)(2,1)S(1)} %slice.23), channel_id=1, source_target_pairs={{1,0},{2,1},{3,2},{4,3},{5,4},{6,5},{7,6},{8,7},{9,8},{10,9},{11,1... | collective-permute-start | bytes 24584 | tf_op jit(solution)/shard_map/ppermute | solution.py:19
  36.2 0.0 collective-permute-done.1
  36.2 0.1 slice.35
  36.3 0.2 concatenate.16
  36.5 0.8 stack.22
  37.3 1.1 copy.22
  38.4 1.2 %collective-permute-done = bf16[16,256]{1,0:T(8,128)(2,1)S(1)} collective-permute-done((bf16[16,256]{1,0:T(8,128)(2,1)S(1)}, bf16[16,256]{1,0:T(8,128)(2,1)S(1)}, u32[]{:S(2)}, u32[]{:S(2)}) %collective-permute-start) | collective-permute-done | bytes 8224 | tf_op jit(solution)/shard_map/ppermute | solution.py:19
  39.6 0.9 maximum_maximum_fusion
  40.5 0.8 stack.21
  41.3 1.1 %copy.21 = bf16[16,1,280,16]{2,3,1,0:T(8,128)(2,1)} copy(bf16[16,1,280,16]{3,2,0,1:T(8,128)(2,1)S(1)} %stack.21) | data formatting | bytes 286720 | tf_op jit(solution)/shard_map/stack | solution.py:136
  42.4 1.1 maximum_bitcast_fusion
  43.6 0.2 rev.7
  43.8 0.9 fusion.2.phased_ref
  44.6 11.0 %shard_map.46.win_ref = bf16[16,2,256,384]{3,2,1,0:T(8,128)(2,1)} custom-call(bf16[16,2,16,384]{3,2,1,0:T(8,128)(2,1)} %fusion.2.phased_ref), custom_call_target="tpu_custom_call" | custom-call | tf_op jit(solution)/shard_map/pallas_call | solution.py:54
  55.7 28.2 %all-to-all-done.1 = bf16[32,4,2,16,256]{4,3,2,1,0:T(8,128)(2,1)S(1)} async-done(((bf16[32,4,2,16,256]{4,3,2,1,0:T(8,128)(2,1)}), bf16[32,4,2,16,256]{4,3,2,1,0:T(8,128)(2,1)S(1)}, u32[]{:S(2)}, u32[]{:S(2)}) %all-to-all-start.1) | async-done | bytes 2097184 | tf_op jit(solution)/shard_map/all_to_all | solution.py:148
  83.9 0.0 copy-start
  83.9 1.3 %copy-done = bf16[32,4,2,16,256]{4,3,2,1,0:T(8,128)(2,1)} copy-done((bf16[32,4,2,16,256]{4,3,2,1,0:T(8,128)(2,1)}, bf16[32,4,2,16,256]{4,3,2,1,0:T(8,128)(2,1)S(1)}, u32[]{:S(2)}) %copy-start) | copy-done | bytes 2097176
  85.2 0.0 copy-start.3
  85.2 6.4 %shard_map.47 = f32[16,2,16,128]{3,2,1,0:T(8,128)} custom-call(s32[128]{0:T(128)} %copy-done.2, bf16[128,2,16,256]{3,2,1,0:T(8,128)(2,1)} %bitcast.13, bf16[16,2,256,384]{3,2,1,0:T(8,128)(2,1)} %shard_map.46.win_ref), custom_call_target="tpu_custom_call" | custom-call | tf_op jit(solution)/shard_map/pallas_call | solution.py:110
  91.6 8.4 %all-to-all-start.2 = ((f32[16,2,16,128]{3,2,1,0:T(8,128)}), f32[16,2,16,128]{3,2,1,0:T(8,128)S(1)}, u32[]{:S(2)}, u32[]{:S(2)}) async-start(f32[16,2,16,128]{3,2,1,0:T(8,128)} %shard_map.47), calls=%async_computation.2 | async-start | bytes 524288 | tf_op jit(solution)/shard_map/all_to_all | solution.py:152
  100.0 0.0 copy-done.3
  100.0 0.1 fusion.4
  100.1 0.1 reshape.159
  100.2 11.9 %all-to-all-done.2 = f32[16,2,16,128]{3,2,1,0:T(8,128)S(1)} async-done(((f32[16,2,16,128]{3,2,1,0:T(8,128)}), f32[16,2,16,128]{3,2,1,0:T(8,128)S(1)}, u32[]{:S(2)}, u32[]{:S(2)}) %all-to-all-start.2) | async-done | bytes 262176 | tf_op jit(solution)/shard_map/all_to_all | solution.py:152
  112.1 0.6 multiply_multiply_fusion
  (16 shorter events, 0.2 us)
Async XLA Ops:
  0.0 18.3 %copy-start.1 = (bf16[16,4096]{1,0:T(8,128)(2,1)S(1)}, bf16[16,4096]{1,0:T(8,128)(2,1)}, u32[]{:S(2)}) copy-start(bf16[16,4096]{1,0:T(8,128)(2,1)} %param.4) | copy-start | bytes 393220
  1.1 18.1 %copy-start.2 = (s32[128]{0:T(128)}, s32[128]{0:T(128)S(1)}, u32[]{:S(2)}) copy-start(s32[128]{0:T(128)S(1)} %multiply_add_fusion.slot_ref) | copy-start | bytes 1540
  3.2 20.8 %all-to-all-start = ((s32[32,1,4]{2,1,0:T(1,128)}), s32[32,1,4]{2,1,0:T(1,128)S(1)}, u32[]{:S(2)}, u32[]{:S(2)}) async-start(s32[32,1,4]{2,1,0:T(1,128)} %bitcast.3), calls=%async_computation | async-start | bytes 32768 | tf_op jit(solution)/shard_map/all_to_all | solution.py:144
  27.3 56.6 %all-to-all-start.1 = ((bf16[32,4,2,16,256]{4,3,2,1,0:T(8,128)(2,1)}), bf16[32,4,2,16,256]{4,3,2,1,0:T(8,128)(2,1)S(1)}, u32[]{:S(2)}, u32[]{:S(2)}) async-start(bf16[32,4,2,16,256]{4,3,2,1,0:T(8,128)(2,1)} %bitcast.14), calls=%async_computation.1 | async-start | bytes 4194304 | tf_op jit(solution)/shard_map/all_to_all | solution.py:148
  31.7 4.5 %collective-permute-start.1 = (bf16[16,256]{1,0:T(8,128)(2,1)S(1)}, bf16[16,256]{1,0:T(8,128)(2,1)S(1)}, u32[]{:S(2)}, u32[]{:S(2)}) collective-permute-start(bf16[16,256]{1,0:T(8,128)(2,1)S(1)} %slice.34), channel_id=1, source_target_pairs={{0,1},{1,2},{2,3},{3,4},{4,5},{5,6},{6,7},{7,8},{8,9},{9,10},{10,1... | collective-permute-start | bytes 24584 | tf_op jit(solution)/shard_map/ppermute | solution.py:19
  34.9 4.7 %collective-permute-start = (bf16[16,256]{1,0:T(8,128)(2,1)S(1)}, bf16[16,256]{1,0:T(8,128)(2,1)S(1)}, u32[]{:S(2)}, u32[]{:S(2)}) collective-permute-start(bf16[16,256]{1,0:T(8,128)(2,1)S(1)} %slice.23), channel_id=1, source_target_pairs={{1,0},{2,1},{3,2},{4,3},{5,4},{6,5},{7,6},{8,7},{9,8},{10,9},{11,1... | collective-permute-start | bytes 24584 | tf_op jit(solution)/shard_map/ppermute | solution.py:19
  83.9 1.3 %copy-start = (bf16[32,4,2,16,256]{4,3,2,1,0:T(8,128)(2,1)}, bf16[32,4,2,16,256]{4,3,2,1,0:T(8,128)(2,1)S(1)}, u32[]{:S(2)}) copy-start(bf16[32,4,2,16,256]{4,3,2,1,0:T(8,128)(2,1)S(1)} %all-to-all-done.1) | copy-start | bytes 6291460
  85.2 14.8 %copy-start.3 = (s32[16]{0:T(128)S(1)}, s32[16]{0:T(128)}, u32[]{:S(2)}) copy-start(s32[16]{0:T(128)} %param.7) | copy-start | bytes 196
  91.6 20.5 %all-to-all-start.2 = ((f32[16,2,16,128]{3,2,1,0:T(8,128)}), f32[16,2,16,128]{3,2,1,0:T(8,128)S(1)}, u32[]{:S(2)}, u32[]{:S(2)}) async-start(f32[16,2,16,128]{3,2,1,0:T(8,128)} %shard_map.47), calls=%async_computation.2 | async-start | bytes 524288 | tf_op jit(solution)/shard_map/all_to_all | solution.py:152

commit v10 on v9

--- a/solution.py
+++ b/solution.py
@@ -138,9 +138,12 @@
     phased = jnp.pad(phased, ((0, 0), (0, 0), (0, 0), (0, WIDE - phased.shape[3])))
 
     targets = partners.reshape(-1)
-    slot_of, order = request_layout(targets, lane_dev, capacity)
+    slot_of, _ = request_layout(targets, lane_dev, capacity)
     local_index = targets % lane_dev
-    send_index = local_index[order].reshape(lane_count, capacity)
+    serial = jnp.arange(targets.shape[0], dtype=jnp.int32)
+    chosen = slot_of[None, :] == serial[:, None]
+    send_index = jnp.sum(jnp.where(chosen, local_index[None, :], 0), axis=1)
+    send_index = send_index.reshape(lane_count, capacity)
     index_in = lax.all_to_all(send_index, "lane", split_axis=0, concat_axis=0, tiled=True)
     both = deinterleave(jnp.stack([waveforms, levels], axis=1))
     both = jnp.concatenate([both[:, :1], both[:, 1:, ::-1]], axis=1)

time: 114 us -> 113 us (level)
  local copies, waits for them, and re-layouts: 13.7 us -> 12.5 us
    gather x1 -> x0, local copies, waits for them, and re-layouts: 1.23 us -> none  [per_device(): send_index = local_index[order].reshape(lane_count, capacity)]
where the time goes in v10:
time: 113 us; the launch traced here: 111 us
  waiting for transfers between devices  45.5 us (40%)
  starting transfers between devices  30.2 us (27%)
  Pallas kernels  17.4 us (15%)
  local copies, waits for them, and re-layouts  12.5 us (11%)
  other arithmetic  5.62 us (5%)
    all_to_all x1, waiting for transfers between devices, per_device(): got = lax.all_to_all(reply, 'lane', split_axis=0, concat_axis=0, tiled=True)  28.2 us
    all_to_all x1, starting transfers between devices, per_device(): lax.all_to_all(send_index, 'lane', split_axis=0, concat_axis=0, tiled=True)  13 us
    all_to_all x1, waiting for transfers between devices, per_device(): lax.all_to_all(terms, 'rec', split_axis=0, concat_axis=0, tiled=True)  11.9 us
    pallas_call x1, Pallas kernels, windows(): pl.pallas_call(window_kernel, grid=(lanes,), in_specs=[pl.BlockSpec((1, 2...  11 us
    all_to_all x1, starting transfers between devices, per_device(): lax.all_to_all(terms, 'rec', split_axis=0, concat_axis=0, tiled=True)  8.4 us
    pallas_call x1, Pallas kernels, correlate(): pl.pallas_call(functools.partial(lane_kernel, slots, group), grid_spec=gr...  6.37 us
    all_to_all x1, starting transfers between devices, per_device(): got = lax.all_to_all(reply, 'lane', split_axis=0, concat_axis=0, tiled=True)  4.41 us
    ppermute x2, starting transfers between devices, passed_along(): return lax.ppermute(block, axis, route)  4.41 us
  transfers between devices with their start and end apart: 5, of which 4 were waited for; matrix products, arithmetic and copies ran while one was open for 10% of the time, Pallas kernels for 10%

profile of v10, /device:TPU:1, one launch (start us, length us, event | category | flops | bytes accessed | tf_op | source)
XLA Modules:
  0.0 111.5 jit_solution(11759852469469090358)
XLA Ops:
  0.0 0.0 copy-start.1
  0.0 0.8 copy.17
  0.8 0.1 reshape.163
  0.9 0.2 convert_reduce_fusion
  1.1 0.0 copy-start.2
  1.1 0.1 select_reduce_fusion
  1.2 0.7 all_to_all.12
  1.9 13.0 %all-to-all-start = ((s32[32,1,4]{2,1,0:T(1,128)}), s32[32,1,4]{2,1,0:T(1,128)S(1)}, u32[]{:S(2)}, u32[]{:S(2)}) async-start(s32[32,1,4]{2,1,0:T(1,128)} %bitcast.1), calls=%async_computation | async-start | bytes 32768 | tf_op jit(solution)/shard_map/all_to_all | solution.py:147
  14.9 1.0 add_convert_fusion
  15.9 0.8 stack.19
  16.7 0.3 copy.19
  17.1 0.0 copy-done.1
  17.1 0.8 stack.18
  17.9 0.3 copy.18
  18.2 0.0 copy-done.2
  18.3 0.1 rev.6
  18.5 4.2 %all-to-all-done = s32[32,1,4]{2,1,0:T(1,128)S(1)} async-done(((s32[32,1,4]{2,1,0:T(1,128)}), s32[32,1,4]{2,1,0:T(1,128)S(1)}, u32[]{:S(2)}, u32[]{:S(2)}) %all-to-all-start) | async-done | bytes 544 | tf_op jit(solution)/shard_map/all_to_all | solution.py:147
  22.7 0.5 broadcast.161
  23.2 0.7 reduce.3
  23.9 0.1 reshape.164
  24.0 2.0 %gather_fusion = bf16[128,2,16,256]{3,2,1,0:T(8,128)(2,1)} fusion(bf16[16,2,16,256]{3,2,1,0:T(8,128)(2,1)S(1)} %pad_maximum_fusion, s32[1024]{0:T(1024)S(1)} %pad_clamp_fusion), kind=kCustom, calls=%fused_computation | custom fusion | bytes 4194816 | tf_op jit(solution)/shard_map/gather | solution.py:150
  26.1 4.4 %all-to-all-start.1 = ((bf16[32,4,2,16,256]{4,3,2,1,0:T(8,128)(2,1)}), bf16[32,4,2,16,256]{4,3,2,1,0:T(8,128)(2,1)S(1)}, u32[]{:S(2)}, u32[]{:S(2)}) async-start(bf16[32,4,2,16,256]{4,3,2,1,0:T(8,128)(2,1)} %bitcast.10), calls=%async_computation.1 | async-start | bytes 4194304 | tf_op jit(solution)/shard_map/all_to_all | solution.py:151
  30.5 3.1 %collective-permute-start.1 = (bf16[16,256]{1,0:T(8,128)(2,1)S(1)}, bf16[16,256]{1,0:T(8,128)(2,1)S(1)}, u32[]{:S(2)}, u32[]{:S(2)}) collective-permute-start(bf16[16,256]{1,0:T(8,128)(2,1)S(1)} %slice.32), channel_id=1, source_target_pairs={{0,1},{1,2},{2,3},{3,4},{4,5},{5,6},{6,7},{7,8},{8,9},{9,10},{10,1... | collective-permute-start | bytes 24584 | tf_op jit(solution)/shard_map/ppermute | solution.py:19
  33.6 1.3 %collective-permute-start = (bf16[16,256]{1,0:T(8,128)(2,1)S(1)}, bf16[16,256]{1,0:T(8,128)(2,1)S(1)}, u32[]{:S(2)}, u32[]{:S(2)}) collective-permute-start(bf16[16,256]{1,0:T(8,128)(2,1)S(1)} %slice.23), channel_id=1, source_target_pairs={{1,0},{2,1},{3,2},{4,3},{5,4},{6,5},{7,6},{8,7},{9,8},{10,9},{11,1... | collective-permute-start | bytes 24584 | tf_op jit(solution)/shard_map/ppermute | solution.py:19
  34.9 0.0 collective-permute-done.1
  35.0 0.1 slice.33
  35.0 0.2 concatenate.16
  35.2 0.8 stack.22
  36.0 1.1 %copy.22 = bf16[16,1,280,16]{2,3,1,0:T(8,128)(2,1)} copy(bf16[16,1,280,16]{3,2,0,1:T(8,128)(2,1)S(1)} %stack.22) | data formatting | bytes 286720 | tf_op jit(solution)/shard_map/stack | solution.py:136
  37.2 1.2 %collective-permute-done = bf16[16,256]{1,0:T(8,128)(2,1)S(1)} collective-permute-done((bf16[16,256]{1,0:T(8,128)(2,1)S(1)}, bf16[16,256]{1,0:T(8,128)(2,1)S(1)}, u32[]{:S(2)}, u32[]{:S(2)}) %collective-permute-start) | collective-permute-done | bytes 8224 | tf_op jit(solution)/shard_map/ppermute | solution.py:19
  38.3 0.9 maximum_maximum_fusion
  39.2 0.8 stack.21
  40.1 1.1 %copy.21 = bf16[16,1,280,16]{2,3,1,0:T(8,128)(2,1)} copy(bf16[16,1,280,16]{3,2,0,1:T(8,128)(2,1)S(1)} %stack.21) | data formatting | bytes 286720 | tf_op jit(solution)/shard_map/stack | solution.py:136
  41.2 1.1 maximum_bitcast_fusion
  42.3 0.2 rev.7
  42.5 0.9 fusion.2.phased_ref
  43.4 11.0 %shard_map.46.win_ref = bf16[16,2,256,384]{3,2,1,0:T(8,128)(2,1)} custom-call(bf16[16,2,16,384]{3,2,1,0:T(8,128)(2,1)} %fusion.2.phased_ref), custom_call_target="tpu_custom_call" | custom-call | tf_op jit(solution)/shard_map/pallas_call | solution.py:54
  54.4 28.2 %all-to-all-done.1 = bf16[32,4,2,16,256]{4,3,2,1,0:T(8,128)(2,1)S(1)} async-done(((bf16[32,4,2,16,256]{4,3,2,1,0:T(8,128)(2,1)}), bf16[32,4,2,16,256]{4,3,2,1,0:T(8,128)(2,1)S(1)}, u32[]{:S(2)}, u32[]{:S(2)}) %all-to-all-start.1) | async-done | bytes 2097184 | tf_op jit(solution)/shard_map/all_to_all | solution.py:151
  82.6 0.0 copy-start
  82.6 1.3 %copy-done = bf16[32,4,2,16,256]{4,3,2,1,0:T(8,128)(2,1)} copy-done((bf16[32,4,2,16,256]{4,3,2,1,0:T(8,128)(2,1)}, bf16[32,4,2,16,256]{4,3,2,1,0:T(8,128)(2,1)S(1)}, u32[]{:S(2)}) %copy-start) | copy-done | bytes 2097176
  84.0 0.0 copy-start.3
  84.0 6.4 %shard_map.47 = f32[16,2,16,128]{3,2,1,0:T(8,128)} custom-call(s32[128]{0:T(128)} %copy-done.2, bf16[128,2,16,256]{3,2,1,0:T(8,128)(2,1)} %bitcast.9, bf16[16,2,256,384]{3,2,1,0:T(8,128)(2,1)} %shard_map.46.win_ref), custom_call_target="tpu_custom_call" | custom-call | tf_op jit(solution)/shard_map/pallas_call | solution.py:110
  90.4 8.4 %all-to-all-start.2 = ((f32[16,2,16,128]{3,2,1,0:T(8,128)}), f32[16,2,16,128]{3,2,1,0:T(8,128)S(1)}, u32[]{:S(2)}, u32[]{:S(2)}) async-start(f32[16,2,16,128]{3,2,1,0:T(8,128)} %shard_map.47), calls=%async_computation.2 | async-start | bytes 524288 | tf_op jit(solution)/shard_map/all_to_all | solution.py:155
  98.8 0.0 copy-done.3
  98.8 0.1 fusion.4
  98.9 0.1 reshape.167
  99.0 11.9 %all-to-all-done.2 = f32[16,2,16,128]{3,2,1,0:T(8,128)S(1)} async-done(((f32[16,2,16,128]{3,2,1,0:T(8,128)}), f32[16,2,16,128]{3,2,1,0:T(8,128)S(1)}, u32[]{:S(2)}, u32[]{:S(2)}) %all-to-all-start.2) | async-done | bytes 262176 | tf_op jit(solution)/shard_map/all_to_all | solution.py:155
  110.9 0.6 multiply_multiply_fusion
  (14 shorter events, 0.2 us)
Async XLA Ops:
  0.0 17.1 %copy-start.1 = (bf16[16,4096]{1,0:T(8,128)(2,1)S(1)}, bf16[16,4096]{1,0:T(8,128)(2,1)}, u32[]{:S(2)}) copy-start(bf16[16,4096]{1,0:T(8,128)(2,1)} %param.4) | copy-start | bytes 393220
  1.1 17.1 %copy-start.2 = (s32[128]{0:T(128)}, s32[128]{0:T(128)S(1)}, u32[]{:S(2)}) copy-start(s32[128]{0:T(128)S(1)} %multiply_add_fusion.slot_ref) | copy-start | bytes 1540
  1.9 20.8 %all-to-all-start = ((s32[32,1,4]{2,1,0:T(1,128)}), s32[32,1,4]{2,1,0:T(1,128)S(1)}, u32[]{:S(2)}, u32[]{:S(2)}) async-start(s32[32,1,4]{2,1,0:T(1,128)} %bitcast.1), calls=%async_computation | async-start | bytes 32768 | tf_op jit(solution)/shard_map/all_to_all | solution.py:147
  26.1 56.6 %all-to-all-start.1 = ((bf16[32,4,2,16,256]{4,3,2,1,0:T(8,128)(2,1)}), bf16[32,4,2,16,256]{4,3,2,1,0:T(8,128)(2,1)S(1)}, u32[]{:S(2)}, u32[]{:S(2)}) async-start(bf16[32,4,2,16,256]{4,3,2,1,0:T(8,128)(2,1)} %bitcast.10), calls=%async_computation.1 | async-start | bytes 4194304 | tf_op jit(solution)/shard_map/all_to_all | solution.py:151
  30.5 4.5 %collective-permute-start.1 = (bf16[16,256]{1,0:T(8,128)(2,1)S(1)}, bf16[16,256]{1,0:T(8,128)(2,1)S(1)}, u32[]{:S(2)}, u32[]{:S(2)}) collective-permute-start(bf16[16,256]{1,0:T(8,128)(2,1)S(1)} %slice.32), channel_id=1, source_target_pairs={{0,1},{1,2},{2,3},{3,4},{4,5},{5,6},{6,7},{7,8},{8,9},{9,10},{10,1... | collective-permute-start | bytes 24584 | tf_op jit(solution)/shard_map/ppermute | solution.py:19
  33.6 4.7 %collective-permute-start = (bf16[16,256]{1,0:T(8,128)(2,1)S(1)}, bf16[16,256]{1,0:T(8,128)(2,1)S(1)}, u32[]{:S(2)}, u32[]{:S(2)}) collective-permute-start(bf16[16,256]{1,0:T(8,128)(2,1)S(1)} %slice.23), channel_id=1, source_target_pairs={{1,0},{2,1},{3,2},{4,3},{5,4},{6,5},{7,6},{8,7},{9,8},{10,9},{11,1... | collective-permute-start | bytes 24584 | tf_op jit(solution)/shard_map/ppermute | solution.py:19
  82.6 1.3 %copy-start = (bf16[32,4,2,16,256]{4,3,2,1,0:T(8,128)(2,1)}, bf16[32,4,2,16,256]{4,3,2,1,0:T(8,128)(2,1)S(1)}, u32[]{:S(2)}) copy-start(bf16[32,4,2,16,256]{4,3,2,1,0:T(8,128)(2,1)S(1)} %all-to-all-done.1) | copy-start | bytes 6291460
  84.0 14.8 %copy-start.3 = (s32[16]{0:T(128)S(1)}, s32[16]{0:T(128)}, u32[]{:S(2)}) copy-start(s32[16]{0:T(128)} %param.7) | copy-start | bytes 196
  90.4 20.5 %all-to-all-start.2 = ((f32[16,2,16,128]{3,2,1,0:T(8,128)}), f32[16,2,16,128]{3,2,1,0:T(8,128)S(1)}, u32[]{:S(2)}, u32[]{:S(2)}) async-start(f32[16,2,16,128]{3,2,1,0:T(8,128)} %shard_map.47), calls=%async_computation.2 | async-start | bytes 524288 | tf_op jit(solution)/shard_map/all_to_all | solution.py:155

commit v11 on v10

--- a/solution.py
+++ b/solution.py
@@ -147,7 +147,8 @@
     index_in = lax.all_to_all(send_index, "lane", split_axis=0, concat_axis=0, tiled=True)
     both = deinterleave(jnp.stack([waveforms, levels], axis=1))
     both = jnp.concatenate([both[:, :1], both[:, 1:, ::-1]], axis=1)
-    reply = both[index_in.reshape(-1)].reshape((lane_count, capacity) + both.shape[1:])
+    reply = jnp.take(both, index_in.reshape(-1), axis=0, mode="clip")
+    reply = reply.reshape((lane_count, capacity) + both.shape[1:])
     got = lax.all_to_all(reply, "lane", split_axis=0, concat_axis=0, tiled=True)
     got = got.reshape((lane_count * capacity,) + both.shape[1:])
     lag_dev = LAGS // rec_count

time: 113 us -> 113 us (level)
  no operation moved by 1% of the time
where the time goes in v11:
time: 113 us; the launch traced here: 111 us
  waiting for transfers between devices  45.5 us (40%)
  starting transfers between devices  30.2 us (27%)
  Pallas kernels  17.4 us (15%)
  local copies, waits for them, and re-layouts  12.5 us (11%)
  other arithmetic  5.62 us (5%)
    all_to_all x1, waiting for transfers between devices, per_device(): got = lax.all_to_all(reply, 'lane', split_axis=0, concat_axis=0, tiled=True)  28.2 us
    all_to_all x1, starting transfers between devices, per_device(): lax.all_to_all(send_index, 'lane', split_axis=0, concat_axis=0, tiled=True)  13 us
    all_to_all x1, waiting for transfers between devices, per_device(): lax.all_to_all(terms, 'rec', split_axis=0, concat_axis=0, tiled=True)  11.9 us
    pallas_call x1, Pallas kernels, windows(): pl.pallas_call(window_kernel, grid=(lanes,), in_specs=[pl.BlockSpec((1, 2...  11 us
    all_to_all x1, starting transfers between devices, per_device(): lax.all_to_all(terms, 'rec', split_axis=0, concat_axis=0, tiled=True)  8.4 us
    pallas_call x1, Pallas kernels, correlate(): pl.pallas_call(functools.partial(lane_kernel, slots, group), grid_spec=gr...  6.38 us
    all_to_all x1, starting transfers between devices, per_device(): got = lax.all_to_all(reply, 'lane', split_axis=0, concat_axis=0, tiled=True)  4.41 us
    ppermute x2, starting transfers between devices, passed_along(): return lax.ppermute(block, axis, route)  4.41 us
  transfers between devices with their start and end apart: 5, of which 4 were waited for; matrix products, arithmetic and copies ran while one was open for 10% of the time, Pallas kernels for 10%

profile of v11, /device:TPU:1, one launch (start us, length us, event | category | flops | bytes accessed | tf_op | source)
XLA Modules:
  0.0 111.5 jit_solution(2401566387188598636)
XLA Ops:
  0.0 0.0 copy-start.1
  0.0 0.8 copy.17
  0.8 0.1 reshape.134
  0.9 0.2 convert_reduce_fusion
  1.1 0.0 copy-start.2
  1.1 0.1 select_reduce_fusion
  1.2 0.7 all_to_all.12
  1.9 13.0 %all-to-all-start = ((s32[32,1,4]{2,1,0:T(1,128)}), s32[32,1,4]{2,1,0:T(1,128)S(1)}, u32[]{:S(2)}, u32[]{:S(2)}) async-start(s32[32,1,4]{2,1,0:T(1,128)} %bitcast.1), calls=%async_computation | async-start | bytes 32768 | tf_op jit(solution)/shard_map/all_to_all | solution.py:147
  14.9 1.0 add_convert_fusion
  15.9 0.8 stack.19
  16.7 0.3 copy.19
  17.1 0.0 copy-done.1
  17.1 0.8 stack.18
  17.9 0.3 copy.18
  18.2 0.0 copy-done.2
  18.3 0.1 rev.6
  18.5 4.2 %all-to-all-done = s32[32,1,4]{2,1,0:T(1,128)S(1)} async-done(((s32[32,1,4]{2,1,0:T(1,128)}), s32[32,1,4]{2,1,0:T(1,128)S(1)}, u32[]{:S(2)}, u32[]{:S(2)}) %all-to-all-start) | async-done | bytes 544 | tf_op jit(solution)/shard_map/all_to_all | solution.py:147
  22.7 0.5 broadcast.143
  23.2 0.7 reduce.3
  23.9 0.1 reshape.140
  24.0 2.0 %gather_fusion = bf16[128,2,16,256]{3,2,1,0:T(8,128)(2,1)} fusion(bf16[16,2,16,256]{3,2,1,0:T(8,128)(2,1)S(1)} %pad_maximum_fusion, s32[1024]{0:T(1024)S(1)} %pad_clamp_fusion), kind=kCustom, calls=%fused_computation | custom fusion | bytes 4194816 | tf_op jit(solution)/shard_map/jit(_take)/gather | solution.py:150
  26.0 4.4 %all-to-all-start.1 = ((bf16[32,4,2,16,256]{4,3,2,1,0:T(8,128)(2,1)}), bf16[32,4,2,16,256]{4,3,2,1,0:T(8,128)(2,1)S(1)}, u32[]{:S(2)}, u32[]{:S(2)}) async-start(bf16[32,4,2,16,256]{4,3,2,1,0:T(8,128)(2,1)} %bitcast.8), calls=%async_computation.1 | async-start | bytes 4194304 | tf_op jit(solution)/shard_map/all_to_all | solution.py:152
  30.5 3.1 %collective-permute-start.1 = (bf16[16,256]{1,0:T(8,128)(2,1)S(1)}, bf16[16,256]{1,0:T(8,128)(2,1)S(1)}, u32[]{:S(2)}, u32[]{:S(2)}) collective-permute-start(bf16[16,256]{1,0:T(8,128)(2,1)S(1)} %slice.32), channel_id=1, source_target_pairs={{0,1},{1,2},{2,3},{3,4},{4,5},{5,6},{6,7},{7,8},{8,9},{9,10},{10,1... | collective-permute-start | bytes 24584 | tf_op jit(solution)/shard_map/ppermute | solution.py:19
  33.6 1.3 %collective-permute-start = (bf16[16,256]{1,0:T(8,128)(2,1)S(1)}, bf16[16,256]{1,0:T(8,128)(2,1)S(1)}, u32[]{:S(2)}, u32[]{:S(2)}) collective-permute-start(bf16[16,256]{1,0:T(8,128)(2,1)S(1)} %slice.23), channel_id=1, source_target_pairs={{1,0},{2,1},{3,2},{4,3},{5,4},{6,5},{7,6},{8,7},{9,8},{10,9},{11,1... | collective-permute-start | bytes 24584 | tf_op jit(solution)/shard_map/ppermute | solution.py:19
  34.9 0.0 collective-permute-done.1
  34.9 0.1 slice.33
  35.0 0.2 concatenate.16
  35.2 0.8 stack.22
  36.0 1.1 %copy.22 = bf16[16,1,280,16]{2,3,1,0:T(8,128)(2,1)} copy(bf16[16,1,280,16]{3,2,0,1:T(8,128)(2,1)S(1)} %stack.22) | data formatting | bytes 286720 | tf_op jit(solution)/shard_map/stack | solution.py:136
  37.1 1.2 %collective-permute-done = bf16[16,256]{1,0:T(8,128)(2,1)S(1)} collective-permute-done((bf16[16,256]{1,0:T(8,128)(2,1)S(1)}, bf16[16,256]{1,0:T(8,128)(2,1)S(1)}, u32[]{:S(2)}, u32[]{:S(2)}) %collective-permute-start) | collective-permute-done | bytes 8224 | tf_op jit(solution)/shard_map/ppermute | solution.py:19
  38.3 0.9 maximum_maximum_fusion
  39.2 0.8 stack.21
  40.0 1.1 %copy.21 = bf16[16,1,280,16]{2,3,1,0:T(8,128)(2,1)} copy(bf16[16,1,280,16]{3,2,0,1:T(8,128)(2,1)S(1)} %stack.21) | data formatting | bytes 286720 | tf_op jit(solution)/shard_map/stack | solution.py:136
  41.2 1.1 maximum_bitcast_fusion
  42.3 0.2 rev.7
  42.5 0.9 fusion.2.phased_ref
  43.4 11.0 %shard_map.46.win_ref = bf16[16,2,256,384]{3,2,1,0:T(8,128)(2,1)} custom-call(bf16[16,2,16,384]{3,2,1,0:T(8,128)(2,1)} %fusion.2.phased_ref), custom_call_target="tpu_custom_call" | custom-call | tf_op jit(solution)/shard_map/pallas_call | solution.py:54
  54.4 28.2 %all-to-all-done.1 = bf16[32,4,2,16,256]{4,3,2,1,0:T(8,128)(2,1)S(1)} async-done(((bf16[32,4,2,16,256]{4,3,2,1,0:T(8,128)(2,1)}), bf16[32,4,2,16,256]{4,3,2,1,0:T(8,128)(2,1)S(1)}, u32[]{:S(2)}, u32[]{:S(2)}) %all-to-all-start.1) | async-done | bytes 2097184 | tf_op jit(solution)/shard_map/all_to_all | solution.py:152
  82.6 0.0 copy-start
  82.6 1.3 %copy-done = bf16[32,4,2,16,256]{4,3,2,1,0:T(8,128)(2,1)} copy-done((bf16[32,4,2,16,256]{4,3,2,1,0:T(8,128)(2,1)}, bf16[32,4,2,16,256]{4,3,2,1,0:T(8,128)(2,1)S(1)}, u32[]{:S(2)}) %copy-start) | copy-done | bytes 2097176
  84.0 0.0 copy-start.3
  84.0 6.4 %shard_map.47 = f32[16,2,16,128]{3,2,1,0:T(8,128)} custom-call(s32[128]{0:T(128)} %copy-done.2, bf16[128,2,16,256]{3,2,1,0:T(8,128)(2,1)} %bitcast.7, bf16[16,2,256,384]{3,2,1,0:T(8,128)(2,1)} %shard_map.46.win_ref), custom_call_target="tpu_custom_call" | custom-call | tf_op jit(solution)/shard_map/pallas_call | solution.py:110
  90.4 8.4 %all-to-all-start.2 = ((f32[16,2,16,128]{3,2,1,0:T(8,128)}), f32[16,2,16,128]{3,2,1,0:T(8,128)S(1)}, u32[]{:S(2)}, u32[]{:S(2)}) async-start(f32[16,2,16,128]{3,2,1,0:T(8,128)} %shard_map.47), calls=%async_computation.2 | async-start | bytes 524288 | tf_op jit(solution)/shard_map/all_to_all | solution.py:156
  98.8 0.0 copy-done.3
  98.8 0.1 fusion.4
  98.8 0.1 reshape.137
  98.9 11.9 %all-to-all-done.2 = f32[16,2,16,128]{3,2,1,0:T(8,128)S(1)} async-done(((f32[16,2,16,128]{3,2,1,0:T(8,128)}), f32[16,2,16,128]{3,2,1,0:T(8,128)S(1)}, u32[]{:S(2)}, u32[]{:S(2)}) %all-to-all-start.2) | async-done | bytes 262176 | tf_op jit(solution)/shard_map/all_to_all | solution.py:156
  110.9 0.6 multiply_multiply_fusion
  (13 shorter events, 0.2 us)
Async XLA Ops:
  0.0 17.1 %copy-start.1 = (bf16[16,4096]{1,0:T(8,128)(2,1)S(1)}, bf16[16,4096]{1,0:T(8,128)(2,1)}, u32[]{:S(2)}) copy-start(bf16[16,4096]{1,0:T(8,128)(2,1)} %param.4) | copy-start | bytes 393220
  1.1 17.1 %copy-start.2 = (s32[128]{0:T(128)}, s32[128]{0:T(128)S(1)}, u32[]{:S(2)}) copy-start(s32[128]{0:T(128)S(1)} %multiply_add_fusion.slot_ref) | copy-start | bytes 1540
  1.9 20.8 %all-to-all-start = ((s32[32,1,4]{2,1,0:T(1,128)}), s32[32,1,4]{2,1,0:T(1,128)S(1)}, u32[]{:S(2)}, u32[]{:S(2)}) async-start(s32[32,1,4]{2,1,0:T(1,128)} %bitcast.1), calls=%async_computation | async-start | bytes 32768 | tf_op jit(solution)/shard_map/all_to_all | solution.py:147
  26.0 56.6 %all-to-all-start.1 = ((bf16[32,4,2,16,256]{4,3,2,1,0:T(8,128)(2,1)}), bf16[32,4,2,16,256]{4,3,2,1,0:T(8,128)(2,1)S(1)}, u32[]{:S(2)}, u32[]{:S(2)}) async-start(bf16[32,4,2,16,256]{4,3,2,1,0:T(8,128)(2,1)} %bitcast.8), calls=%async_computation.1 | async-start | bytes 4194304 | tf_op jit(solution)/shard_map/all_to_all | solution.py:152
  30.5 4.5 %collective-permute-start.1 = (bf16[16,256]{1,0:T(8,128)(2,1)S(1)}, bf16[16,256]{1,0:T(8,128)(2,1)S(1)}, u32[]{:S(2)}, u32[]{:S(2)}) collective-permute-start(bf16[16,256]{1,0:T(8,128)(2,1)S(1)} %slice.32), channel_id=1, source_target_pairs={{0,1},{1,2},{2,3},{3,4},{4,5},{5,6},{6,7},{7,8},{8,9},{9,10},{10,1... | collective-permute-start | bytes 24584 | tf_op jit(solution)/shard_map/ppermute | solution.py:19
  33.6 4.7 %collective-permute-start = (bf16[16,256]{1,0:T(8,128)(2,1)S(1)}, bf16[16,256]{1,0:T(8,128)(2,1)S(1)}, u32[]{:S(2)}, u32[]{:S(2)}) collective-permute-start(bf16[16,256]{1,0:T(8,128)(2,1)S(1)} %slice.23), channel_id=1, source_target_pairs={{1,0},{2,1},{3,2},{4,3},{5,4},{6,5},{7,6},{8,7},{9,8},{10,9},{11,1... | collective-permute-start | bytes 24584 | tf_op jit(solution)/shard_map/ppermute | solution.py:19
  82.6 1.3 %copy-start = (bf16[32,4,2,16,256]{4,3,2,1,0:T(8,128)(2,1)}, bf16[32,4,2,16,256]{4,3,2,1,0:T(8,128)(2,1)S(1)}, u32[]{:S(2)}) copy-start(bf16[32,4,2,16,256]{4,3,2,1,0:T(8,128)(2,1)S(1)} %all-to-all-done.1) | copy-start | bytes 6291460
  84.0 14.8 %copy-start.3 = (s32[16]{0:T(128)S(1)}, s32[16]{0:T(128)}, u32[]{:S(2)}) copy-start(s32[16]{0:T(128)} %param.7) | copy-start | bytes 196
  90.4 20.5 %all-to-all-start.2 = ((f32[16,2,16,128]{3,2,1,0:T(8,128)}), f32[16,2,16,128]{3,2,1,0:T(8,128)S(1)}, u32[]{:S(2)}, u32[]{:S(2)}) async-start(f32[16,2,16,128]{3,2,1,0:T(8,128)} %shard_map.47), calls=%async_computation.2 | async-start | bytes 524288 | tf_op jit(solution)/shard_map/all_to_all | solution.py:156
